TPU v7x, 32 devices: a whole 2x2x4 slice. The times are simulated.
32 devices in a mesh: dp: 8 (over y, x, core), tensor: 4 (over z).
Axes of the slice: x: 2, y: 2, z: 4, core: 2. Of those that a mesh axis runs over, the one named last changes fastest.
Arguments:
- frames: bfloat16 [8, 1024, 1024], P('dp'), may hold values from -6 to 6
- text_states: bfloat16 [8, 128, 1024], P('dp'), may hold values from -6 to 6
- frame_len: int32 [8], P('dp'), may hold values from 170 to 1024, as said below
- text_token_length: int32 [8], P('dp'), may hold values from 5 to 128, as said below
- self_gain: float32 [1024], replicated, may hold values from 0.5 to 1.5
- self_bias: float32 [1024], replicated, may hold values from -2 to 2
- cross_gain: float32 [1024], replicated, may hold values from 0.5 to 1.5
- cross_bias: float32 [1024], replicated, may hold values from -2 to 2
- feed_gain: float32 [1024], replicated, may hold values from 0.5 to 1.5
- feed_bias: float32 [1024], replicated, may hold values from -2 to 2
- self_qkv: bfloat16 [3, 1024, 1024], P(None, None, 'tensor'), may hold values from -0.1875 to 0.1875
- self_out: bfloat16 [1024, 1024], P('tensor'), may hold values from -0.75 to 0.75
- cross_query: bfloat16 [1024, 1024], P(None, 'tensor'), may hold values from -0.1875 to 0.1875
- cross_keyval: bfloat16 [2, 1024, 1024], P(None, None, 'tensor'), may hold values from -0.1875 to 0.1875
- cross_out: bfloat16 [1024, 1024], P('tensor'), may hold values from -0.75 to 0.75
- feed_up: bfloat16 [1024, 4096], P(None, 'tensor'), may hold values from -0.1875 to 0.1875
- feed_down: bfloat16 [4096, 1024], P('tensor'), may hold values from -0.125 to 0.125
- cotangent: bfloat16 [8, 1024, 1024], P('dp'), may hold values from -6 to 6
Outputs:
- block_out: bfloat16 [8, 1024, 1024], P('dp')
- frames_grad: float32 [8, 1024, 1024], P('dp')
- text_grad: float32 [8, 128, 1024], P('dp')
- self_gain_grad: float32 [1024], replicated
- self_bias_grad: float32 [1024], replicated
- cross_gain_grad: float32 [1024], replicated
- cross_bias_grad: float32 [1024], replicated
- feed_gain_grad: float32 [1024], replicated
- feed_bias_grad: float32 [1024], replicated
- self_qkv_grad: float32 [3, 1024, 1024], P(None, None, 'tensor')
- self_out_grad: float32 [1024, 1024], P('tensor')
- cross_query_grad: float32 [1024, 1024], P(None, 'tensor')
- cross_keyval_grad: float32 [2, 1024, 1024], P(None, None, 'tensor')
- cross_out_grad: float32 [1024, 1024], P('tensor')
- feed_up_grad: float32 [1024, 4096], P(None, 'tensor')
- feed_down_grad: float32 [4096, 1024], P('tensor')
Inputs may be any that keep to these rules, and one draw needn't show every extreme that they name: Frames of a clip at or after its frame_len are padding: no query sees them as keys. Some clip of every draw has all 1024 frames. Text tokens of a clip at or after its text_token_length are padding that no query sees. Some clip of every draw has all 128 tokens.
All inputs are finite; a program needn't handle non-finite values.
Results may differ from a plain program's by a relative error of at most 0.03.
Values may be sent and summed in bfloat16 or wider, within the bound.
No kernel may reach another device: no remote copies, remote signals or barrier semaphores. Data moves between devices by JAX's collectives and lax.ppermute only.
A program may use at most 128 MiB of HBM per device.

v0:
```python
import jax
import jax.numpy as jnp
from jax import lax
from jax.sharding import PartitionSpec as P

HEAD = 64


EPSILON = 1e-05
MASKED = -1e30


def layer_norm(inputs, norm_gain, norm_bias):
    row_mean = jnp.mean(inputs, axis=-1, keepdims=True)
    centred = inputs - row_mean
    spread = jnp.mean(centred * centred, axis=-1, keepdims=True)
    return centred * lax.rsqrt(spread + EPSILON) * norm_gain + norm_bias


def norm_back(inputs, norm_gain, norm_bias, upstream):
    _, pullback = jax.vjp(layer_norm, inputs, norm_gain, norm_bias)
    return pullback(upstream)


def gelu_exact(inputs):
    return jax.nn.gelu(inputs, approximate=False)


def masked_scores(portion, offset, key_rows, key_limit, causal, score_scale):
    scores = (
        jnp.einsum("bhe,khe->hbk", portion, key_rows, preferred_element_type=jnp.float32)
        * score_scale
    )
    key_pos = jnp.arange(key_rows.shape[0])
    allowed = key_pos[None, :] < key_limit
    if causal:
        allowed = allowed & (key_pos[None, :] <= offset + jnp.arange(portion.shape[0])[:, None])
    return jnp.where(allowed[None], scores, MASKED)


def attend(queries, key_rows, values, key_limit, causal, score_scale):
    row_count, head_count, head_size = queries.shape
    block_len = min(512, row_count)
    portions = queries.reshape(row_count // block_len, block_len, head_count, head_size)
    offsets = jnp.arange(row_count // block_len) * block_len

    def one_block(entries):
        portion, offset = entries
        scores = masked_scores(portion, offset, key_rows, key_limit, causal, score_scale)
        row_max = jnp.max(scores, axis=-1, keepdims=True)
        unnormed = jnp.exp(scores - row_max)
        row_sum = jnp.sum(unnormed, axis=-1, keepdims=True)
        probs_low = (unnormed / row_sum).astype(jnp.bfloat16)
        result = jnp.einsum("hbk,khe->bhe", probs_low, values, preferred_element_type=jnp.float32)
        return (result.astype(jnp.bfloat16), row_max[..., 0] + jnp.log(row_sum[..., 0]))

    result, log_total = lax.map(one_block, (portions, offsets))
    return (result.reshape(row_count, head_count, head_size), log_total)


def attend_back(queries, key_rows, values, log_total, out_grad, key_limit, causal, score_scale):
    row_count, head_count, head_size = queries.shape
    block_len = min(512, row_count)
    portions = queries.reshape(row_count // block_len, block_len, head_count, head_size)
    grad_parts = out_grad.reshape(row_count // block_len, block_len, head_count, head_size)
    offsets = jnp.arange(row_count // block_len) * block_len

    def one_block(carry, entries):
        key_grad, value_grad = carry
        portion, grad_part, log_part, offset = entries
        scores = masked_scores(portion, offset, key_rows, key_limit, causal, score_scale)
        probs = jnp.exp(scores - log_part[..., None])
        probs_grad = jnp.einsum(
            "bhe,khe->hbk", grad_part, values, preferred_element_type=jnp.float32
        )
        row_dot = jnp.sum(probs * probs_grad, axis=-1, keepdims=True)
        scores_grad = (probs * (probs_grad - row_dot)).astype(jnp.bfloat16)
        value_grad = value_grad + jnp.einsum(
            "hbk,bhe->khe",
            probs.astype(jnp.bfloat16),
            grad_part,
            preferred_element_type=jnp.float32,
        )
        key_grad = (
            key_grad
            + jnp.einsum("hbk,bhe->khe", scores_grad, portion, preferred_element_type=jnp.float32)
            * score_scale
        )
        query_grad = (
            jnp.einsum("hbk,khe->bhe", scores_grad, key_rows, preferred_element_type=jnp.float32)
            * score_scale
        )
        return ((key_grad, value_grad), query_grad)

    empty = jnp.zeros(key_rows.shape, jnp.float32)
    (key_grad, value_grad), query_grad = lax.scan(
        one_block, (empty, empty), (portions, grad_parts, log_total, offsets)
    )
    return (query_grad.reshape(row_count, head_count, head_size), key_grad, value_grad)


def head_total(partial_value):
    return lax.psum(partial_value.astype(jnp.bfloat16), "tensor").astype(jnp.float32)


def local(
    frames,
    text_states,
    frame_len,
    text_token_length,
    self_gain,
    self_bias,
    cross_gain,
    cross_bias,
    feed_gain,
    feed_bias,
    self_qkv,
    self_out,
    cross_query,
    cross_keyval,
    cross_out,
    feed_up,
    feed_down,
    cotangent,
):
    clip_count, slot_len, model_width = frames.shape
    text_count = text_states.shape[1]
    local_width = self_out.shape[0]
    head_count = local_width // HEAD
    score_scale = HEAD ** (-0.5)
    row_total = clip_count * slot_len
    inputs = frames.reshape(row_total, model_width).astype(jnp.float32)
    out_grad = cotangent.reshape(row_total, model_width)
    normed_self = layer_norm(inputs, self_gain, self_bias).astype(jnp.bfloat16)
    projected = jnp.einsum(
        "sd,cde->cse", normed_self, self_qkv, preferred_element_type=jnp.float32
    ).astype(jnp.bfloat16)
    projected = projected.reshape(3, clip_count, slot_len, head_count, HEAD)

    def self_clip(entries):
        return attend(entries[0], entries[1], entries[2], entries[3], True, score_scale)

    self_heads, self_log = lax.map(self_clip, (projected[0], projected[1], projected[2], frame_len))
    self_flat = self_heads.reshape(row_total, local_width)
    self_part = jnp.dot(self_flat, self_out, preferred_element_type=jnp.float32)
    after_self = inputs + head_total(self_part)
    normed_cross = layer_norm(after_self, cross_gain, cross_bias).astype(jnp.bfloat16)
    cross_queries = jnp.dot(normed_cross, cross_query, preferred_element_type=jnp.float32).astype(
        jnp.bfloat16
    )
    cross_queries = cross_queries.reshape(clip_count, slot_len, head_count, HEAD)
    text_proj = jnp.einsum(
        "ctd,gde->gcte", text_states, cross_keyval, preferred_element_type=jnp.float32
    ).astype(jnp.bfloat16)
    text_proj = text_proj.reshape(2, clip_count, text_count, head_count, HEAD)

    def cross_clip(entries):
        return attend(entries[0], entries[1], entries[2], entries[3], False, score_scale)

    cross_heads, cross_log = lax.map(
        cross_clip, (cross_queries, text_proj[0], text_proj[1], text_token_length)
    )
    cross_flat = cross_heads.reshape(row_total, local_width)
    cross_part = jnp.dot(cross_flat, cross_out, preferred_element_type=jnp.float32)
    after_cross = after_self + head_total(cross_part)
    normed_feed = layer_norm(after_cross, feed_gain, feed_bias).astype(jnp.bfloat16)
    upward = jnp.dot(normed_feed, feed_up, preferred_element_type=jnp.float32)
    active = gelu_exact(upward).astype(jnp.bfloat16)
    feed_part = jnp.dot(active, feed_down, preferred_element_type=jnp.float32)
    block_out = (after_cross + head_total(feed_part)).astype(jnp.bfloat16)
    active_grad = jnp.einsum("sd,kd->sk", out_grad, feed_down, preferred_element_type=jnp.float32)
    _, gelu_pull = jax.vjp(gelu_exact, upward)
    upward_grad = gelu_pull(active_grad)[0].astype(jnp.bfloat16)
    downward_gradient = jnp.einsum(
        "sk,sd->kd", active, out_grad, preferred_element_type=jnp.float32
    )
    up_grad = jnp.einsum("sd,sk->dk", normed_feed, upward_grad, preferred_element_type=jnp.float32)
    feed_input_part = jnp.einsum(
        "sk,dk->sd", upward_grad, feed_up, preferred_element_type=jnp.float32
    )
    feed_back = norm_back(after_cross, feed_gain, feed_bias, head_total(feed_input_part))
    cross_grad_rows = out_grad.astype(jnp.float32) + feed_back[0]
    cross_grad_low = cross_grad_rows.astype(jnp.bfloat16)
    cout_grad = jnp.einsum(
        "sk,sd->kd", cross_flat, cross_grad_low, preferred_element_type=jnp.float32
    )
    cross_heads_grad = jnp.einsum(
        "sd,kd->sk", cross_grad_low, cross_out, preferred_element_type=jnp.float32
    ).astype(jnp.bfloat16)
    cross_heads_grad = cross_heads_grad.reshape(clip_count, slot_len, head_count, HEAD)

    def cross_clip_back(entries):
        return attend_back(
            entries[0],
            entries[1],
            entries[2],
            entries[3],
            entries[4],
            entries[5],
            False,
            score_scale,
        )

    cquery_heads, ckey_heads, cvalue_heads = lax.map(
        cross_clip_back,
        (cross_queries, text_proj[0], text_proj[1], cross_log, cross_heads_grad, text_token_length),
    )
    query_grad_low = cquery_heads.reshape(row_total, local_width).astype(jnp.bfloat16)
    keyval_grad_low = jnp.stack((ckey_heads, cvalue_heads)).astype(jnp.bfloat16)
    keyval_grad_low = keyval_grad_low.reshape(2, clip_count, text_count, local_width)
    cquery_grad = jnp.einsum(
        "sd,se->de", normed_cross, query_grad_low, preferred_element_type=jnp.float32
    )
    ckeyval_grad = jnp.einsum(
        "ctd,gcte->gde", text_states, keyval_grad_low, preferred_element_type=jnp.float32
    )
    cross_input_part = jnp.einsum(
        "se,de->sd", query_grad_low, cross_query, preferred_element_type=jnp.float32
    )
    text_part = jnp.einsum(
        "gcte,gde->ctd", keyval_grad_low, cross_keyval, preferred_element_type=jnp.float32
    )
    cross_sum, text_grad = (
        lax.psum(cross_input_part.astype(jnp.bfloat16), "tensor").astype(jnp.float32),
        lax.psum(text_part.astype(jnp.bfloat16), "tensor").astype(jnp.float32),
    )
    cross_back = norm_back(after_self, cross_gain, cross_bias, cross_sum)
    self_grad_rows = cross_grad_rows + cross_back[0]
    self_grad_low = self_grad_rows.astype(jnp.bfloat16)
    sout_grad = jnp.einsum(
        "sk,sd->kd", self_flat, self_grad_low, preferred_element_type=jnp.float32
    )
    self_heads_grad = jnp.einsum(
        "sd,kd->sk", self_grad_low, self_out, preferred_element_type=jnp.float32
    ).astype(jnp.bfloat16)
    self_heads_grad = self_heads_grad.reshape(clip_count, slot_len, head_count, HEAD)

    def self_clip_back(entries):
        return attend_back(
            entries[0],
            entries[1],
            entries[2],
            entries[3],
            entries[4],
            entries[5],
            True,
            score_scale,
        )

    self_query_heads, self_key_heads, self_value_heads = lax.map(
        self_clip_back,
        (projected[0], projected[1], projected[2], self_log, self_heads_grad, frame_len),
    )
    projection_gradient = jnp.stack((self_query_heads, self_key_heads, self_value_heads)).astype(
        jnp.bfloat16
    )
    projection_gradient = projection_gradient.reshape(3, row_total, local_width)
    qkv_grad = jnp.einsum(
        "sd,cse->cde", normed_self, projection_gradient, preferred_element_type=jnp.float32
    )
    self_input_part = jnp.einsum(
        "cse,cde->sd", projection_gradient, self_qkv, preferred_element_type=jnp.float32
    )
    self_back = norm_back(inputs, self_gain, self_bias, head_total(self_input_part))
    frames_grad = self_grad_rows + self_back[0]
    gain_terms = (
        self_back[1],
        self_back[2],
        cross_back[1],
        cross_back[2],
        feed_back[1],
        feed_back[2],
    )
    summed = (
        lax.psum(gain_terms[0].astype(jnp.bfloat16), "dp").astype(jnp.float32),
        lax.psum(gain_terms[1].astype(jnp.bfloat16), "dp").astype(jnp.float32),
        lax.psum(gain_terms[2].astype(jnp.bfloat16), "dp").astype(jnp.float32),
        lax.psum(gain_terms[3].astype(jnp.bfloat16), "dp").astype(jnp.float32),
        lax.psum(gain_terms[4].astype(jnp.bfloat16), "dp").astype(jnp.float32),
        lax.psum(gain_terms[5].astype(jnp.bfloat16), "dp").astype(jnp.float32),
        lax.psum(qkv_grad.astype(jnp.bfloat16), "dp").astype(jnp.float32),
        lax.psum(sout_grad.astype(jnp.bfloat16), "dp").astype(jnp.float32),
        lax.psum(cquery_grad.astype(jnp.bfloat16), "dp").astype(jnp.float32),
        lax.psum(ckeyval_grad.astype(jnp.bfloat16), "dp").astype(jnp.float32),
        lax.psum(cout_grad.astype(jnp.bfloat16), "dp").astype(jnp.float32),
        lax.psum(up_grad.astype(jnp.bfloat16), "dp").astype(jnp.float32),
        lax.psum(downward_gradient.astype(jnp.bfloat16), "dp").astype(jnp.float32),
    )
    return (
        block_out.reshape(clip_count, slot_len, model_width),
        frames_grad.reshape(clip_count, slot_len, model_width),
        text_grad,
        summed[0],
        summed[1],
        summed[2],
        summed[3],
        summed[4],
        summed[5],
        summed[6],
        summed[7],
        summed[8],
        summed[9],
        summed[10],
        summed[11],
        summed[12],
    )


def solution(mesh):
    return jax.shard_map(
        local,
        mesh=mesh,
        in_specs=(
            P("dp", None, None),
            P("dp", None, None),
            P("dp"),
            P("dp"),
            P(),
            P(),
            P(),
            P(),
            P(),
            P(),
            P(None, None, "tensor"),
            P("tensor", None),
            P(None, "tensor"),
            P(None, None, "tensor"),
            P("tensor", None),
            P(None, "tensor"),
            P("tensor", None),
            P("dp", None, None),
        ),
        out_specs=(
            P("dp", None, None),
            P("dp", None, None),
            P("dp", None, None),
            P(),
            P(),
            P(),
            P(),
            P(),
            P(),
            P(None, None, "tensor"),
            P("tensor", None),
            P(None, "tensor"),
            P(None, None, "tensor"),
            P("tensor", None),
            P(None, "tensor"),
            P("tensor", None),
        ),
        check_vma=False,
    )
```

profile of v0, /device:TPU:0, one launch (start us, length us, event | category | flops | bytes accessed | tf_op | source)
XLA Modules:
  0.0 890.4 jit_solution(7422087750435936070)
XLA Ops:
  19.1 21.6 %while.94 = (s32[]{:T(128)}, bf16[2,512,4,64]{1,3,2,0:T(8,128)(2,1)}, f32[2,4,512]{2,1,0:T(4,128)S(1)}, s32[]{:T(128)}, s32[2]{0:T(128)}, /*index=5*/bf16[2,512,...) while((s32[]{:T(128)}, ...), condition=%wide.region_5.6_spmd, body=%wide.region_2.5_spmd.sunk | while | flops 563215872 | bytes 35199192 | solution.py:57
  48.7 86.7 %all-reduce.10.cloned.1.call-done = bf16[1024,1024]{1,0:T(8,128)(2,1)} async-done(((bf16[1024,1024]{1,0:T(8,128)(2,1)}), bf16[1024,1024]{1,0:T(8,128)(2,1)}) %all-reduce.10.cloned.1.call-update) | async-done | bytes 2097168 | tf_op jit(solution)/shard_map/psum | solution.py:103
  149.6 6.4 while.95
  161.8 85.1 %all-reduce.12.cloned.1.call-done = bf16[1024,1024]{1,0:T(8,128)(2,1)} async-done(((bf16[1024,1024]{1,0:T(8,128)(2,1)}), bf16[1024,1024]{1,0:T(8,128)(2,1)}) %all-reduce.12.cloned.1.call-update) | async-done | bytes 2097168 | tf_op jit(solution)/shard_map/psum | solution.py:103
  246.9 3.7 fusion.138
  251.5 12.8 %multiply_convert_fusion.2 = (bf16[1024,1024]{1,0:T(8,128)(2,1)}, f32[1024,1024]{1,0:T(8,128)S(1)}, f32[1024,1024]{1,0:T(8,128)S(1)}) fusion(bf16[1024,1024]{1,0:T(8,128)(2,1)S(1)} %copy-done, f32[1024,1024]{1,0:T(8,128)S(1)} %get-tuple-element.594, f32[1024]{0:T(1024)S(1)} %copy-done.84, f32[1024]{0:T(1024)S(1)} %copy-done.77, f32[1024]{0:T(1024)S(1)} %fusion.127, ...), kind=kOutput, calls=%fused_computation.138 | convolution fusion | flops 2220883968 | bytes 16793600 | tf_op jit(solution)/shard_map/dot_general | solution.py:167
  269.1 3.7 convolution_convert_fusion.3
  273.1 85.0 %all-reduce.14.cloned.1.call-done = bf16[1024,1024]{1,0:T(8,128)(2,1)} async-done(((bf16[1024,1024]{1,0:T(8,128)(2,1)}), bf16[1024,1024]{1,0:T(8,128)(2,1)}) %all-reduce.14.cloned.1.call-update) | async-done | bytes 2097168 | tf_op jit(solution)/shard_map/psum | solution.py:103
  358.1 4.7 fusion.91
  375.7 14.2 %while.96 = (s32[]{:T(128)}, f32[128,4,64]{0,2,1:T(8,128)S(1)}, f32[128,4,64]{0,2,1:T(8,128)S(1)}, bf16[2,512,4,64]{1,3,2,0:T(8,128)(2,1)}, bf16[2,512,4,64]{1,3...) while((s32[]{:T(128)}, f32[128,4,64]{0,2,1:T(8,128)S(1)}, ...), condition=%wide.region_22.23_spmd.clone, body=%wide.region_20.22_spmd.clone.sunk | while | flops 170424448 | bytes 16491000 | solution.py:96
  396.2 5.5 fusion.112
  401.8 4.1 convolution_convert_fusion.1
  414.3 66.7 %all-reduce.16.cloned.1.call-done = bf16[1024,1024]{1,0:T(8,128)(2,1)} async-done(((bf16[1024,1024]{1,0:T(8,128)(2,1)}), bf16[1024,1024]{1,0:T(8,128)(2,1)}) %all-reduce.16.cloned.1.call-update) | async-done | bytes 2097168 | tf_op jit(solution)/shard_map/psum | solution.py:224
  481.0 3.6 fusion.87
  499.7 32.0 %while.97 = (s32[]{:T(128)}, f32[1024,4,64]{0,2,1:T(8,128)}, f32[1024,4,64]{0,2,1:T(8,128)}, bf16[2,512,4,64]{1,3,2,0:T(8,128)(2,1)}, bf16[2,512,4,64]{1,3,2,0:T...) while((s32[]{:T(128)}, f32[1024,4,64]{0,2,1:T(8,128)}, ...), condition=%wide.region_28.29_spmd.clone, body=%wide.region_26.28_spmd.clone.sunk | while | flops 1376124416 | bytes 97581464 | solution.py:96
  539.7 4.5 fusion.116
  544.4 6.0 convolution_convert_fusion.4
  558.9 111.5 %all-reduce.18.cloned.1.call-done = (bf16[3,1024,256]{1,2,0:T(8,128)(2,1)}, bf16[2,1024,256]{1,2,0:T(8,128)(2,1)}, bf16[256,1024]{1,0:T(8,128)(2,1)}, bf16[1024,...) async-done(((bf16[3,1024,256]{1,2,0:T(8,128)(2,1)}, bf16[2,1024,256]{1,2,0:T(8,128)(2,1)}, ...) | async-done | bytes 8388624 | tf_op jit(solution)/shard_map/psum | solution.py:281
  681.8 4.2 convert_element_type.284
  688.5 148.8 %all-reduce.20.cloned.1.call-done = (bf16[1024,1024]{1,0:T(8,128)(2,1)}, bf16[1024,1024]{1,0:T(8,128)(2,1)}, bf16[1,128,1024]{2,1,0:T(8,128)(2,1)}) async-done(((bf16[1024,1024]{1,0:T(8,128)(2,1)}, bf16[1024,1024]{1,0:T(8,128)(2,1)}, bf16[1,128,1024]{2,1,0:T(8,128)(2,1)}), (bf16[1024,1024]{1,0:T(8,128)(2,1)}, bf16[1024,1024]{1,0:T(8,128)(2,1)}, ...) | async-done | bytes 4456464 | tf_op jit(solution)/shard_map/psum | solution.py:103
  837.2 5.1 fusion.104
  845.3 3.9 fusion.93
  849.2 23.8 %all-reduce = (bf16[1024]{0:T(1024)(128)(2,1)S(1)}, bf16[1024]{0:T(1024)(128)(2,1)S(1)}, bf16[1024]{0:T(1024)(128)(2,1)S(1)}, bf16[1024]{0:T(1024)(128)(2,1)S(1)...) all-reduce(bf16[1024]{0:T(1024)(128)(2,1)S(1)} %get-tuple-element.4, ...), channel_id=1, replica_groups=mesh['dp'=8,'tensor'=4] {'dp'}, use_global_device_ids=true, to_apply=%region_34.35 | all-reduce | flops 6144 | bytes 24576 | tf_op jit(solution)/shard_map/psum | solution.py:275
  876.7 5.8 add_bitcast_fusion
  (375 shorter events, 199.0 us)
Async XLA Ops:
  7.2 244.1 %copy-start = (bf16[1024,1024]{1,0:T(8,128)(2,1)S(1)}, bf16[1024,1024]{1,0:T(8,128)(2,1)}, u32[]{:S(2)}) copy-start(bf16[1024,1024]{1,0:T(8,128)(2,1)} %param.41) | copy-start | bytes 6291460
  7.2 128.2 %all-reduce.10.cloned.1.call-start = ((), (), s32[]{:S(2)}) async-start(), calls=%async_computation | async-start | bytes 4194304 | tf_op jit(solution)/shard_map/psum | solution.py:103
  46.4 200.6 %all-reduce.12.cloned.1.call-start = ((), (), s32[]{:S(2)}) async-start(), calls=%async_computation.1 | async-start | bytes 4194304 | tf_op jit(solution)/shard_map/psum | solution.py:103
  48.7 91.1 %copy-start.60 = (f32[1024]{0:T(1024)S(1)}, f32[1024]{0:T(1024)}, u32[]{:S(2)}) copy-start(f32[1024]{0:T(1024)} %param.32) | copy-start | bytes 12292
  48.7 91.1 %copy-start.80 = (f32[1024]{0:T(1024)S(1)}, f32[1024]{0:T(1024)}, u32[]{:S(2)}) copy-start(f32[1024]{0:T(1024)} %param.33) | copy-start | bytes 12292
  156.0 94.6 %copy-start.53 = (f32[2,4,512]{2,1,0:T(4,128)}, f32[2,4,512]{2,1,0:T(4,128)S(1)}, u32[]{:S(2)}) copy-start(f32[2,4,512]{2,1,0:T(4,128)S(1)} %get-tuple-element.903) | copy-start | bytes 49156
  161.6 196.5 %all-reduce.14.cloned.1.call-start = ((), (), s32[]{:S(2)}) async-start(), calls=%async_computation.2 | async-start | bytes 4194304 | tf_op jit(solution)/shard_map/psum | solution.py:103
  250.7 13.6 %copy-start.5 = (f32[1024,1024]{1,0:T(8,128)}, f32[1024,1024]{1,0:T(8,128)S(1)}, u32[]{:S(2)}) copy-start(f32[1024,1024]{1,0:T(8,128)S(1)} %get-tuple-element.594) | copy-start | bytes 12582916
  250.7 13.5 %copy-start.62 = (f32[1024]{0:T(1024)}, f32[1024]{0:T(1024)S(1)}, u32[]{:S(2)}) copy-start(f32[1024]{0:T(1024)S(1)} %broadcast_multiply_fusion) | copy-start | bytes 12292
  251.3 13.0 %copy-start.76 = (f32[1024]{0:T(1024)}, f32[1024]{0:T(1024)S(1)}, u32[]{:S(2)}) copy-start(f32[1024]{0:T(1024)S(1)} %multiply_reduce_fusion.2) | copy-start | bytes 12292
  251.5 12.8 %copy-start.72 = (f32[1024]{0:T(1024)}, f32[1024]{0:T(1024)S(1)}, u32[]{:S(2)}) copy-start(f32[1024]{0:T(1024)S(1)} %fusion.127) | copy-start | bytes 12292
  251.5 12.8 %copy-start.21 = (bf16[1,1024,1024]{2,1,0:T(8,128)(2,1)S(1)}, bf16[1,1024,1024]{2,1,0:T(8,128)(2,1)}, u32[]{:S(2)}) copy-start(bf16[1,1024,1024]{2,1,0:T(8,128)(2,1)} %param.43) | copy-start | bytes 6291460
  251.5 12.8 %copy-start.81 = (bf16[1024,1024]{1,0:T(8,128)(2,1)S(1)}, bf16[1024,1024]{1,0:T(8,128)(2,1)}, u32[]{:S(2)}) copy-start(bf16[1024,1024]{1,0:T(8,128)(2,1)} %param.42) | copy-start | bytes 6291460
  272.8 208.1 %all-reduce.16.cloned.1.call-start = ((), (), s32[]{:S(2)}) async-start(), calls=%async_computation.3 | async-start | bytes 4194304 | tf_op jit(solution)/shard_map/psum | solution.py:224
  395.7 274.7 %all-reduce.18.cloned.1.call-start = ((), (), s32[]{:S(2)}) async-start(), calls=%async_computation.4 | async-start | bytes 16777216 | tf_op jit(solution)/shard_map/psum | solution.py:281
  407.6 73.4 %copy-start.4 = (bf16[1,1024,1024]{2,1,0:T(8,128)(2,1)S(1)}, bf16[1,1024,1024]{2,1,0:T(8,128)(2,1)}, u32[]{:S(2)}) copy-start(bf16[1,1024,1024]{2,1,0:T(8,128)(2,1)} %param.26) | copy-start | bytes 6291460
  407.6 73.4 %copy-start.55 = (f32[1024]{0:T(1024)S(1)}, f32[1024]{0:T(1024)}, u32[]{:S(2)}) copy-start(f32[1024]{0:T(1024)} %copy-done.54) | copy-start | bytes 12292
  407.6 73.4 %copy-start.61 = (f32[1024]{0:T(1024)S(1)}, f32[1024]{0:T(1024)}, u32[]{:S(2)}) copy-start(f32[1024]{0:T(1024)} %param.32) | copy-start | bytes 12292
  414.2 70.4 %copy-start.75 = (f32[1024]{0:T(1024)S(1)}, f32[1024]{0:T(1024)}, u32[]{:S(2)}) copy-start(f32[1024]{0:T(1024)} %copy-done.74) | copy-start | bytes 12292
  414.3 70.4 %copy-start.59 = (f32[1024]{0:T(1024)S(1)}, f32[1024]{0:T(1024)}, u32[]{:S(2)}) copy-start(f32[1024]{0:T(1024)} %copy-done.58) | copy-start | bytes 12292
  531.7 8.0 copy-start.65
  531.7 8.0 copy-start.67
  531.7 8.0 copy-start.87
  544.3 292.9 %all-reduce.20.cloned.1.call-start = ((), (), s32[]{:S(2)}) async-start(), calls=%async_computation.5 | async-start | bytes 8912896 | tf_op jit(solution)/shard_map/psum | solution.py:103
  (86 other events, 298.8 us)
Sparse Core Ops, SparseCore 0:
  46.5 88.8 all-reduce.9
  161.7 85.1 all-reduce.11
  273.0 85.1 all-reduce.13
  395.8 85.1 all-reduce.15
  544.4 125.9 all-reduce.17
  673.3 163.8 all-reduce.19
where the time goes:
time: 899 us; the launch traced here: 890 us
  waiting for transfers between devices  584 us (65%)
  matrix products  115 us (13%)
  other arithmetic  94 us (10%)
  local copies, waits for them, and re-layouts  56.5 us (6%)
  blocking collectives  23.8 us (3%)
  between operations  15.3 us (2%)
    psum x4, waiting for transfers between devices, head_total(): lax.psum(partial_value.astype(jnp.bfloat16), 'tensor').astype(jnp.float32)  406 us
    psum x1, waiting for transfers between devices, local(): lax.psum(qkv_grad.astype(jnp.bfloat16), 'dp').astype(jnp.float32)  111 us
    psum x1, waiting for transfers between devices, local(): lax.psum(cross_input_part.astype(jnp.bfloat16), 'tensor')  66.7 us
    psum x1, blocking collectives, local(): lax.psum(gain_terms[0].astype(jnp.bfloat16), 'dp').astype(jnp.float32)  23.8 us
    reduce_sum x8, other arithmetic, layer_norm(): return centred * lax.rsqrt(spread + EPSILON) * norm_gain + norm_bias  22.3 us
    unnamed x159, local copies, waits for them, and re-layouts  18.2 us
  transfers between devices with their start and end apart: 6, of which 6 were waited for; matrix products, arithmetic and copies ran while one was open for 6% of the time, Pallas kernels for 0%

commit v1 on v0

--- a/solution.py
+++ b/solution.py
@@ -101,6 +101,63 @@
 
 def head_total(partial_value):
     return lax.psum(partial_value.astype(jnp.bfloat16), "tensor").astype(jnp.float32)
+
+
+def _shift(value, axis, count, step):
+    pairs = [(i, i + step) for i in range(count) if 0 <= i + step < count]
+    return lax.ppermute(value, axis, pairs)
+
+
+def relay_gather(block, axis):
+    count = lax.axis_size(axis)
+    me = lax.axis_index(axis)
+    out = jnp.zeros((count + 1,) + block.shape, block.dtype)
+    out = lax.dynamic_update_index_in_dim(out, block, me, 0)
+    from_left, from_right = block, block
+    for k in range(1, count):
+        from_left = _shift(from_left, axis, count, 1)
+        from_right = _shift(from_right, axis, count, -1)
+        out = lax.dynamic_update_index_in_dim(
+            out, from_left, jnp.where(me - k >= 0, me - k, count), 0
+        )
+        out = lax.dynamic_update_index_in_dim(
+            out, from_right, jnp.where(me + k < count, me + k, count), 0
+        )
+    return out[:count]
+
+
+def relay_scatter(value, axis):
+    count = lax.axis_size(axis)
+    me = lax.axis_index(axis)
+    shards = value.reshape((count, value.shape[0] // count) + value.shape[1:])
+
+    def pick(index):
+        return lax.dynamic_index_in_dim(shards, jnp.clip(index, 0, count - 1), 0, keepdims=False)
+
+    to_right = to_left = None
+    for k in range(1, count):
+        send_right = pick(me + count - k).astype(jnp.float32)
+        send_left = pick(me - (count - k)).astype(jnp.float32)
+        if to_right is not None:
+            send_right = send_right + to_right.astype(jnp.float32)
+            send_left = send_left + to_left.astype(jnp.float32)
+        to_right = _shift(send_right.astype(value.dtype), axis, count, 1)
+        to_left = _shift(send_left.astype(value.dtype), axis, count, -1)
+    total = pick(me).astype(jnp.float32)
+    if to_right is not None:
+        total = total + to_right.astype(jnp.float32) + to_left.astype(jnp.float32)
+    return total.astype(value.dtype)
+
+
+def relay_total(partial_value):
+    low_value = partial_value.astype(jnp.bfloat16)
+    reduced = relay_scatter(low_value, "tensor")
+    return relay_gather(reduced, "tensor").reshape(low_value.shape).astype(jnp.float32)
+
+
+def gathered_sum(pieces, weights, spec):
+    partial_value = jnp.einsum(spec, pieces, weights, preferred_element_type=jnp.float32)
+    return jnp.sum(partial_value.astype(jnp.bfloat16).astype(jnp.float32), axis=0)
 
 
 def local(
@@ -142,8 +199,11 @@
 
     self_heads, self_log = lax.map(self_clip, (projected[0], projected[1], projected[2], frame_len))
     self_flat = self_heads.reshape(row_total, local_width)
-    self_part = jnp.dot(self_flat, self_out, preferred_element_type=jnp.float32)
-    after_self = inputs + head_total(self_part)
+    self_out_all = lax.all_gather(self_out, "tensor")
+    cross_out_all = lax.all_gather(cross_out, "tensor")
+    cross_query_all = lax.all_gather(cross_query, "tensor")
+    self_pieces = relay_gather(self_flat, "tensor")
+    after_self = inputs + gathered_sum(self_pieces, self_out_all, "gsk,gkd->gsd")
     normed_cross = layer_norm(after_self, cross_gain, cross_bias).astype(jnp.bfloat16)
     cross_queries = jnp.dot(normed_cross, cross_query, preferred_element_type=jnp.float32).astype(
         jnp.bfloat16
@@ -161,8 +221,8 @@
         cross_clip, (cross_queries, text_proj[0], text_proj[1], text_token_length)
     )
     cross_flat = cross_heads.reshape(row_total, local_width)
-    cross_part = jnp.dot(cross_flat, cross_out, preferred_element_type=jnp.float32)
-    after_cross = after_self + head_total(cross_part)
+    cross_pieces = relay_gather(cross_flat, "tensor")
+    after_cross = after_self + gathered_sum(cross_pieces, cross_out_all, "gsk,gkd->gsd")
     normed_feed = layer_norm(after_cross, feed_gain, feed_bias).astype(jnp.bfloat16)
     upward = jnp.dot(normed_feed, feed_up, preferred_element_type=jnp.float32)
     active = gelu_exact(upward).astype(jnp.bfloat16)
@@ -178,7 +238,7 @@
     feed_input_part = jnp.einsum(
         "sk,dk->sd", upward_grad, feed_up, preferred_element_type=jnp.float32
     )
-    feed_back = norm_back(after_cross, feed_gain, feed_bias, head_total(feed_input_part))
+    feed_back = norm_back(after_cross, feed_gain, feed_bias, relay_total(feed_input_part))
     cross_grad_rows = out_grad.astype(jnp.float32) + feed_back[0]
     cross_grad_low = cross_grad_rows.astype(jnp.bfloat16)
     cout_grad = jnp.einsum(
@@ -214,16 +274,12 @@
     ckeyval_grad = jnp.einsum(
         "ctd,gcte->gde", text_states, keyval_grad_low, preferred_element_type=jnp.float32
     )
-    cross_input_part = jnp.einsum(
-        "se,de->sd", query_grad_low, cross_query, preferred_element_type=jnp.float32
-    )
     text_part = jnp.einsum(
         "gcte,gde->ctd", keyval_grad_low, cross_keyval, preferred_element_type=jnp.float32
     )
-    cross_sum, text_grad = (
-        lax.psum(cross_input_part.astype(jnp.bfloat16), "tensor").astype(jnp.float32),
-        lax.psum(text_part.astype(jnp.bfloat16), "tensor").astype(jnp.float32),
-    )
+    query_pieces = relay_gather(query_grad_low, "tensor")
+    cross_sum = gathered_sum(query_pieces, cross_query_all, "gse,gde->gsd")
+    text_grad = lax.psum(text_part.astype(jnp.bfloat16), "tensor").astype(jnp.float32)
     cross_back = norm_back(after_self, cross_gain, cross_bias, cross_sum)
     self_grad_rows = cross_grad_rows + cross_back[0]
     self_grad_low = self_grad_rows.astype(jnp.bfloat16)
@@ -261,7 +317,7 @@
     self_input_part = jnp.einsum(
         "cse,cde->sd", projection_gradient, self_qkv, preferred_element_type=jnp.float32
     )
-    self_back = norm_back(inputs, self_gain, self_bias, head_total(self_input_part))
+    self_back = norm_back(inputs, self_gain, self_bias, relay_total(self_input_part))
     frames_grad = self_grad_rows + self_back[0]
     gain_terms = (
         self_back[1],

time: 899 us -> 831 us (0.924)
  waiting for transfers between devices: 584 us -> 305 us
  starting transfers between devices: 1.56 us -> 138 us
  local copies, waits for them, and re-layouts: 56.5 us -> 114 us
  other arithmetic: 94 us -> 114 us
    psum x4 -> x1, waiting for transfers between devices: 406 us -> 14.3 us  [head_total(): lax.psum(partial_value.astype(jnp.bfloat16), 'tensor').astype(jnp.float32)]
    ppermute x0 -> x42, waiting for transfers between devices: none -> 194 us  [_shift(): return lax.ppermute(value, axis, pairs)]
    ppermute x0 -> x42, starting transfers between devices: none -> 138 us  [_shift(): return lax.ppermute(value, axis, pairs)]
    psum x1 -> x0, waiting for transfers between devices: 66.7 us -> none  [local(): lax.psum(cross_input_part.astype(jnp.bfloat16), 'tensor')]
    dynamic_update_slice x0 -> x33, local copies, waits for them, and re-layouts: none -> 39.9 us  [the longest x15 19.8 us: relay_gather(): lax.dynamic_update_index_in_dim(out, from_left, jnp.where(me - k >= 0, me...]
    psum x1, waiting for transfers between devices: 111 us -> 95.7 us  [local(): lax.psum(qkv_grad.astype(jnp.bfloat16), 'dp').astype(jnp.float32)]
    dot_general x3, matrix products: 9.35 us -> 20.5 us  [gathered_sum(): jnp.einsum(spec, pieces, weights, preferred_element_type=jnp.float32)]
    add x1 -> x2, other arithmetic: 2.38 us -> 13.3 us  [the longest x1 10.3 us: local(): frames_grad = self_grad_rows + self_back[0]]
  transfers between devices with their start and end apart: 6 -> 47, of which waited for: 6 -> 34; matrix products, arithmetic and copies ran while one was open for 6% -> 25% of each run, Pallas kernels for 0% -> 0%
where the time goes in v1:
time: 831 us; the launch traced here: 820 us
  waiting for transfers between devices  305 us (37%)
  starting transfers between devices  138 us (17%)
  local copies, waits for them, and re-layouts  114 us (14%)
  other arithmetic  114 us (14%)
  matrix products  107 us (13%)
  blocking collectives  25.5 us (3%)
  between operations  15.9 us (2%)
    ppermute x42, waiting for transfers between devices, _shift(): return lax.ppermute(value, axis, pairs)  194 us
    ppermute x42, starting transfers between devices, _shift(): return lax.ppermute(value, axis, pairs)  138 us
    psum x1, waiting for transfers between devices, local(): lax.psum(qkv_grad.astype(jnp.bfloat16), 'dp').astype(jnp.float32)  95.7 us
    psum x1, blocking collectives, local(): lax.psum(gain_terms[0].astype(jnp.bfloat16), 'dp').astype(jnp.float32)  25.5 us
    reduce_sum x6, other arithmetic, layer_norm(): return centred * lax.rsqrt(spread + EPSILON) * norm_gain + norm_bias  24.5 us
    dot_general x3, matrix products, gathered_sum(): jnp.einsum(spec, pieces, weights, preferred_element_type=jnp.float32)  20.5 us
    dynamic_update_slice x15, local copies, waits for them, and re-layouts, relay_gather(): lax.dynamic_update_index_in_dim(out, from_left, jnp.where(me - k >= 0, me...  19.8 us
    unnamed x223, local copies, waits for them, and re-layouts  19.5 us
  transfers between devices with their start and end apart: 47, of which 34 were waited for; matrix products, arithmetic and copies ran while one was open for 25% of the time, Pallas kernels for 0%

profile of v1, /device:TPU:0, one launch (start us, length us, event | category | flops | bytes accessed | tf_op | source)
XLA Modules:
  0.0 820.1 jit_solution(10868901288873138506)
XLA Ops:
  20.5 21.6 %while.94 = (s32[]{:T(128)}, bf16[2,512,4,64]{1,3,2,0:T(8,128)(2,1)}, f32[2,4,512]{2,1,0:T(4,128)}, s32[]{:T(128)}, s32[2]{0:T(128)}, /*index=5*/bf16[2,512,4,64...) while((s32[]{:T(128)}, ...), condition=%wide.region_5.6_spmd, body=%wide.region_2.5_spmd.sunk | while | flops 563215872 | bytes 35199192 | solution.py:57
  77.0 17.0 %collective-permute-done.2 = bf16[1024,256]{1,0:T(8,128)(2,1)} collective-permute-done((bf16[1024,256]{1,0:T(8,128)(2,1)}, bf16[1024,256]{1,0:T(8,128)(2,1)}, u32[]{:S(2)}, u32[]{:S(2)}) %collective-permute-start.2) | collective-permute-done | bytes 524320 | tf_op jit(solution)/shard_map/ppermute | solution.py:108
  93.9 13.9 %collective-permute-start.4 = (bf16[1024,256]{1,0:T(8,128)(2,1)}, bf16[1024,256]{1,0:T(8,128)(2,1)S(1)}, u32[]{:S(2)}, u32[]{:S(2)}) collective-permute-start(bf16[1024,256]{1,0:T(8,128)(2,1)} %collective-permute-done.2), channel_id=1, source_target_pairs={{0,1},{1,2},{2,3},{4,5},{5,6},{6,7},{8,9},{9,10},{10,11},{12,13},{... | collective-permute-start | bytes 1572872 | tf_op jit(solution)/shard_map/ppermute | solution.py:108
  114.9 9.2 %collective-permute-done.4 = bf16[1024,256]{1,0:T(8,128)(2,1)S(1)} collective-permute-done((bf16[1024,256]{1,0:T(8,128)(2,1)}, bf16[1024,256]{1,0:T(8,128)(2,1)S(1)}, u32[]{:S(2)}, u32[]{:S(2)}) %collective-permute-start.4) | collective-permute-done | bytes 524320 | tf_op jit(solution)/shard_map/ppermute | solution.py:108
  152.3 8.9 %collective-permute-done.6 = bf16[1024,256]{1,0:T(8,128)(2,1)} collective-permute-done((bf16[1024,256]{1,0:T(8,128)(2,1)}, bf16[1024,256]{1,0:T(8,128)(2,1)}, u32[]{:S(2)}, u32[]{:S(2)}) %collective-permute-start.6) | collective-permute-done | bytes 524320 | tf_op jit(solution)/shard_map/ppermute | solution.py:108
  190.6 7.0 collective-permute-done.11
  206.2 12.8 %multiply_convert_fusion.2 = (bf16[1024,1024]{1,0:T(8,128)(2,1)}, f32[1024,1024]{1,0:T(8,128)S(1)}, f32[1024,1024]{1,0:T(8,128)S(1)}) fusion(bf16[1024,1024]{1,0:T(8,128)(2,1)S(1)} %copy-done, f32[1024,1024]{1,0:T(8,128)S(1)} %get-tuple-element.602, f32[1024]{0:T(1024)S(1)} %copy-done.107, f32[1024]{0:T(1024)S(1)} %copy-done.77, f32[1024]{0:T(1024)S(1)} %fusion.178, ...), kind=kOutput, calls=%fused_computation.158 | convolution fusion | flops 2220883968 | bytes 16793600 | tf_op jit(solution)/shard_map/dot_general | solution.py:227
  246.4 7.1 collective-permute-done.13
  272.3 10.1 %collective-permute-done.17 = bf16[256,1024]{1,0:T(8,128)(2,1)} collective-permute-done((bf16[256,1024]{1,0:T(8,128)(2,1)}, bf16[256,1024]{1,0:T(8,128)(2,1)}, u32[]{:S(2)}, u32[]{:S(2)}) %collective-permute-start.17) | collective-permute-done | bytes 524320 | tf_op jit(solution)/shard_map/ppermute | solution.py:108
  291.4 8.3 %collective-permute-done.18 = bf16[256,1024]{1,0:T(8,128)(2,1)S(1)} collective-permute-done((bf16[256,1024]{1,0:T(8,128)(2,1)S(1)}, bf16[256,1024]{1,0:T(8,128)(2,1)S(1)}, u32[]{:S(2)}, u32[]{:S(2)}) %collective-permute-start.18) | collective-permute-done | bytes 524320 | tf_op jit(solution)/shard_map/ppermute | solution.py:108
  307.8 7.1 collective-permute-done.20
  327.5 9.9 %collective-permute-done.22 = bf16[256,1024]{1,0:T(8,128)(2,1)S(1)} collective-permute-done((bf16[256,1024]{1,0:T(8,128)(2,1)S(1)}, bf16[256,1024]{1,0:T(8,128)(2,1)S(1)}, u32[]{:S(2)}, u32[]{:S(2)}) %collective-permute-start.22) | collective-permute-done | bytes 524320 | tf_op jit(solution)/shard_map/ppermute | solution.py:108
  338.2 19.6 %collective-permute-done.23 = bf16[256,1024]{1,0:T(8,128)(2,1)S(1)} collective-permute-done((bf16[256,1024]{1,0:T(8,128)(2,1)}, bf16[256,1024]{1,0:T(8,128)(2,1)S(1)}, u32[]{:S(2)}, u32[]{:S(2)}) %collective-permute-start.23) | collective-permute-done | bytes 524320 | tf_op jit(solution)/shard_map/ppermute | solution.py:108
  390.1 9.1 %collective-permute-done.24 = bf16[1024,256]{1,0:T(8,128)(2,1)} collective-permute-done((bf16[1024,256]{1,0:T(8,128)(2,1)S(1)}, bf16[1024,256]{1,0:T(8,128)(2,1)}, u32[]{:S(2)}, u32[]{:S(2)}) %collective-permute-start.24) | collective-permute-done | bytes 524320 | tf_op jit(solution)/shard_map/ppermute | solution.py:108
  432.2 10.5 %convert_reduce_fusion = (f32[1024,1024]{1,0:T(8,128)}, bf16[4,1024,1024]{2,1,0:T(8,128)(2,1)}) fusion(bf16[5,1024,256]{2,1,0:T(8,128)(2,1)} %bitcast_dynamic-update-slice_fusion.9, bf16[4,1024,256]{2,1,0:T(8,128)(2,1)} %bitcast.523), kind=kOutput, calls=%fused_computation.98 | convolution fusion | flops 2159017984 | bytes 17301504 | tf_op jit(solution)/shard_map/gse,gde->gsd/dot_general | solution.py:159
  453.7 31.2 %while.97 = (s32[]{:T(128)}, f32[1024,4,64]{0,2,1:T(8,128)S(1)}, f32[1024,4,64]{0,2,1:T(8,128)}, bf16[2,512,4,64]{1,3,2,0:T(8,128)(2,1)}, bf16[2,512,4,64]{1,3,2...) while((s32[]{:T(128)}, f32[1024,4,64]{0,2,1:T(8,128)S(1)}, ...), condition=%wide.region_27.28_spmd.clone, body=%wide.region_25.27_spmd.clone.sunk | while | flops 1376124416 | bytes 84998440 | solution.py:96
  544.3 7.6 collective-permute-done.35
  579.2 9.4 %collective-permute-done.38 = bf16[256,1024]{1,0:T(8,128)(2,1)S(1)} collective-permute-done((bf16[256,1024]{1,0:T(8,128)(2,1)}, bf16[256,1024]{1,0:T(8,128)(2,1)S(1)}, u32[]{:S(2)}, u32[]{:S(2)}) %collective-permute-start.38) | collective-permute-done | bytes 524320 | tf_op jit(solution)/shard_map/ppermute | solution.py:108
  588.6 12.7 %collective-permute-start.40 = (bf16[256,1024]{1,0:T(8,128)(2,1)S(1)}, bf16[256,1024]{1,0:T(8,128)(2,1)S(1)}, u32[]{:S(2)}, u32[]{:S(2)}) collective-permute-start(bf16[256,1024]{1,0:T(8,128)(2,1)S(1)} %collective-permute-done.38), channel_id=1, source_target_pairs={{0,1},{1,2},{2,3},{4,5},{5,6},{6,7},{8,9},{9,10},{10,11},{12,13},{... | collective-permute-start | bytes 1572872 | tf_op jit(solution)/shard_map/ppermute | solution.py:108
  609.0 7.2 collective-permute-done.40
  632.3 10.3 %fusion.82 = (f32[1,1024,1024]{2,1,0:T(8,128)}, bf16[1,1024,1024]{2,1,0:T(8,128)(2,1)S(1)}, bf16[1,1024,1024]{2,1,0:T(8,128)(2,1)S(1)}) fusion(bf16[1,1024,1024]{2,1,0:T(8,128)(2,1)S(1)} %copy-done.14, f32[1024]{0:T(1024)S(1)} %bitcast.520, f32[1024]{0:T(1024)S(1)} %get-tuple-element.630, f32[1024]{0:T(1024)S(1)} %copy-done.71, f32[1024]{0:T(1024)S(1)} %copy-done.97, ...), kind=kLoop, calls=%fused_computation.119 | loop fusion | flops 31457280 | bytes 33615872 | tf_op jit(solution)/shard_map/add | solution.py:321
  650.3 14.3 %all-reduce.8.cloned.1.call-done = (bf16[1024,1024]{1,0:T(8,128)(2,1)}, bf16[1,128,1024]{2,1,0:T(8,128)(2,1)}) async-done(((bf16[1024,1024]{1,0:T(8,128)(2,1)}, bf16[1,128,1024]{2,1,0:T(8,128)(2,1)}), (bf16[1024,1024]{1,0:T(8,128)(2,1)}, bf16[1,128,1024]{2,1,0:T(8,128)(2,1)})) %all-reduce.8.cloned.1.call-update) | async-done | bytes 2359312 | tf_op jit(solution)/shard_map/psum | solution.py:103
  671.4 25.5 %all-reduce = (bf16[1024]{0:T(1024)(128)(2,1)S(1)}, bf16[1024]{0:T(1024)(128)(2,1)S(1)}, bf16[1024]{0:T(1024)(128)(2,1)S(1)}, bf16[1024]{0:T(1024)(128)(2,1)S(1)...) all-reduce(bf16[1024]{0:T(1024)(128)(2,1)S(1)} %get-tuple-element.4, ...), channel_id=1, replica_groups=mesh['dp'=8,'tensor'=4] {'dp'}, use_global_device_ids=true, to_apply=%region_32.33 | all-reduce | flops 6144 | bytes 24576 | tf_op jit(solution)/shard_map/psum | solution.py:331
  700.5 95.7 %all-reduce.6.cloned.1.call-done = (bf16[3,1024,256]{1,2,0:T(8,128)(2,1)}, bf16[2,1024,256]{1,2,0:T(8,128)(2,1)}, bf16[256,1024]{1,0:T(8,128)(2,1)}, bf16[1024,2...) async-done(((bf16[3,1024,256]{1,2,0:T(8,128)(2,1)}, bf16[2,1024,256]{1,2,0:T(8,128)(2,1)}, ...) | async-done | bytes 8388624 | tf_op jit(solution)/shard_map/psum | solution.py:337
  (563 shorter events, 480.2 us)
Async XLA Ops:
  7.2 120.4 %all-gather.7.cloned.1.call-start = ((), (), s32[]{:S(2)}) async-start(), calls=%async_computation | async-start | bytes 2621440 | tf_op jit(solution)/shard_map/all_gather | solution.py:202
  8.0 190.5 %all-gather.9.cloned.1.call-start = ((), (), s32[]{:S(2)}) async-start(), calls=%async_computation.1 | async-start | bytes 2621440 | tf_op jit(solution)/shard_map/all_gather | solution.py:203
  47.0 19.1 %collective-permute-start = (bf16[1024,256]{1,0:T(8,128)(2,1)}, bf16[1024,256]{1,0:T(8,128)(2,1)}, u32[]{:S(2)}, u32[]{:S(2)}) collective-permute-start(bf16[1024,256]{1,0:T(8,128)(2,1)} %copy.70), channel_id=1, source_target_pairs={{0,1},{1,2},{2,3},{4,5},{5,6},{6,7},{8,9},{9,10},{10,11},{12,13},{... | collective-permute-start | bytes 1572872 | tf_op jit(solution)/shard_map/ppermute | solution.py:108
  52.8 18.5 %collective-permute-start.1 = (bf16[1024,256]{1,0:T(8,128)(2,1)}, bf16[1024,256]{1,0:T(8,128)(2,1)}, u32[]{:S(2)}, u32[]{:S(2)}) collective-permute-start(bf16[1024,256]{1,0:T(8,128)(2,1)} %copy.70), channel_id=1, source_target_pairs={{1,0},{2,1},{3,2},{5,4},{6,5},{7,6},{9,8},{10,9},{11,10},{13,12},{... | collective-permute-start | bytes 1572872 | tf_op jit(solution)/shard_map/ppermute | solution.py:108
  54.1 378.1 %all-gather.11.cloned.1.call-start = ((), (), s32[]{:S(2)}) async-start(), calls=%async_computation.2 | async-start | bytes 2621440 | tf_op jit(solution)/shard_map/all_gather | solution.py:204
  66.1 27.9 %collective-permute-start.2 = (bf16[1024,256]{1,0:T(8,128)(2,1)}, bf16[1024,256]{1,0:T(8,128)(2,1)}, u32[]{:S(2)}, u32[]{:S(2)}) collective-permute-start(bf16[1024,256]{1,0:T(8,128)(2,1)} %collective-permute-done), channel_id=1, source_target_pairs={{0,1},{1,2},{2,3},{4,5},{5,6},{6,7},{8,9},{9,10},{10,11},{12,13},{... | collective-permute-start | bytes 1572872 | tf_op jit(solution)/shard_map/ppermute | solution.py:108
  71.3 39.4 %collective-permute-start.3 = (bf16[1024,256]{1,0:T(8,128)(2,1)}, bf16[1024,256]{1,0:T(8,128)(2,1)S(1)}, u32[]{:S(2)}, u32[]{:S(2)}) collective-permute-start(bf16[1024,256]{1,0:T(8,128)(2,1)} %collective-permute-done.1), channel_id=1, source_target_pairs={{1,0},{2,1},{3,2},{5,4},{6,5},{7,6},{9,8},{10,9},{11,10},{13,12},{... | collective-permute-start | bytes 1572872 | tf_op jit(solution)/shard_map/ppermute | solution.py:108
  93.9 30.2 %collective-permute-start.4 = (bf16[1024,256]{1,0:T(8,128)(2,1)}, bf16[1024,256]{1,0:T(8,128)(2,1)S(1)}, u32[]{:S(2)}, u32[]{:S(2)}) collective-permute-start(bf16[1024,256]{1,0:T(8,128)(2,1)} %collective-permute-done.2), channel_id=1, source_target_pairs={{0,1},{1,2},{2,3},{4,5},{5,6},{6,7},{8,9},{9,10},{10,11},{12,13},{... | collective-permute-start | bytes 1572872 | tf_op jit(solution)/shard_map/ppermute | solution.py:108
  110.7 16.0 %collective-permute-start.5 = (bf16[1024,256]{1,0:T(8,128)(2,1)S(1)}, bf16[1024,256]{1,0:T(8,128)(2,1)S(1)}, u32[]{:S(2)}, u32[]{:S(2)}) collective-permute-start(bf16[1024,256]{1,0:T(8,128)(2,1)S(1)} %collective-permute-done.3), channel_id=1, source_target_pairs={{1,0},{2,1},{3,2},{5,4},{6,5},{7,6},{9,8},{10,9},{11,10},{13,12},{... | collective-permute-start | bytes 1572872 | tf_op jit(solution)/shard_map/ppermute | solution.py:108
  151.0 18.9 %collective-permute-start.7 = (bf16[1024,256]{1,0:T(8,128)(2,1)}, bf16[1024,256]{1,0:T(8,128)(2,1)}, u32[]{:S(2)}, u32[]{:S(2)}) collective-permute-start(bf16[1024,256]{1,0:T(8,128)(2,1)} %copy.78), channel_id=1, source_target_pairs={{1,0},{2,1},{3,2},{5,4},{6,5},{7,6},{9,8},{10,9},{11,10},{13,12},{... | collective-permute-start | bytes 1572872 | tf_op jit(solution)/shard_map/ppermute | solution.py:108
  299.7 15.3 %collective-permute-start.20 = (bf16[256,1024]{1,0:T(8,128)(2,1)S(1)}, bf16[256,1024]{1,0:T(8,128)(2,1)S(1)}, u32[]{:S(2)}, u32[]{:S(2)}) collective-permute-start(bf16[256,1024]{1,0:T(8,128)(2,1)S(1)} %collective-permute-done.18), channel_id=1, source_target_pairs={{0,1},{1,2},{2,3},{4,5},{5,6},{6,7},{8,9},{9,10},{10,11},{12,13},{... | collective-permute-start | bytes 1572872 | tf_op jit(solution)/shard_map/ppermute | solution.py:108
  304.3 19.1 %collective-permute-start.21 = (bf16[256,1024]{1,0:T(8,128)(2,1)S(1)}, bf16[256,1024]{1,0:T(8,128)(2,1)}, u32[]{:S(2)}, u32[]{:S(2)}) collective-permute-start(bf16[256,1024]{1,0:T(8,128)(2,1)S(1)} %collective-permute-done.19), channel_id=1, source_target_pairs={{1,0},{2,1},{3,2},{5,4},{6,5},{7,6},{9,8},{10,9},{11,10},{13,12},{... | collective-permute-start | bytes 1572872 | tf_op jit(solution)/shard_map/ppermute | solution.py:108
  305.7 358.9 %all-reduce.8.cloned.1.call-start = ((), (), s32[]{:S(2)}) async-start(), calls=%async_computation.4 | async-start | bytes 4718592 | tf_op jit(solution)/shard_map/psum | solution.py:103
  315.0 22.4 %collective-permute-start.22 = (bf16[256,1024]{1,0:T(8,128)(2,1)S(1)}, bf16[256,1024]{1,0:T(8,128)(2,1)S(1)}, u32[]{:S(2)}, u32[]{:S(2)}) collective-permute-start(bf16[256,1024]{1,0:T(8,128)(2,1)S(1)} %collective-permute-done.20), channel_id=1, source_target_pairs={{0,1},{1,2},{2,3},{4,5},{5,6},{6,7},{8,9},{9,10},{10,11},{12,13},{... | collective-permute-start | bytes 1572872 | tf_op jit(solution)/shard_map/ppermute | solution.py:108
  323.5 34.4 %collective-permute-start.23 = (bf16[256,1024]{1,0:T(8,128)(2,1)}, bf16[256,1024]{1,0:T(8,128)(2,1)S(1)}, u32[]{:S(2)}, u32[]{:S(2)}) collective-permute-start(bf16[256,1024]{1,0:T(8,128)(2,1)} %collective-permute-done.21), channel_id=1, source_target_pairs={{1,0},{2,1},{3,2},{5,4},{6,5},{7,6},{9,8},{10,9},{11,10},{13,12},{... | collective-permute-start | bytes 1572872 | tf_op jit(solution)/shard_map/ppermute | solution.py:108
  388.8 19.2 %collective-permute-start.25 = (bf16[1024,256]{1,0:T(8,128)(2,1)S(1)}, bf16[1024,256]{1,0:T(8,128)(2,1)}, u32[]{:S(2)}, u32[]{:S(2)}) collective-permute-start(bf16[1024,256]{1,0:T(8,128)(2,1)S(1)} %copy.86), channel_id=1, source_target_pairs={{1,0},{2,1},{3,2},{5,4},{6,5},{7,6},{9,8},{10,9},{11,10},{13,12},{... | collective-permute-start | bytes 1572872 | tf_op jit(solution)/shard_map/ppermute | solution.py:108
  499.4 16.0 %collective-permute-start.33 = (bf16[256,1024]{1,0:T(8,128)(2,1)S(1)}, bf16[256,1024]{1,0:T(8,128)(2,1)S(1)}, u32[]{:S(2)}, u32[]{:S(2)}) collective-permute-start(bf16[256,1024]{1,0:T(8,128)(2,1)S(1)} %get-tuple-element.620), channel_id=1, source_target_pairs={{1,0},{2,1},{3,2},{5,4},{6,5},{7,6},{9,8},{10,9},{11,10},{13,12},{... | collective-permute-start | bytes 1572872 | tf_op jit(solution)/shard_map/ppermute | solution.py:108
  518.7 17.3 %collective-permute-start.34 = (bf16[256,1024]{1,0:T(8,128)(2,1)S(1)}, bf16[256,1024]{1,0:T(8,128)(2,1)S(1)}, u32[]{:S(2)}, u32[]{:S(2)}) collective-permute-start(bf16[256,1024]{1,0:T(8,128)(2,1)S(1)} %get-tuple-element.618), channel_id=1, source_target_pairs={{1,0},{2,1},{3,2},{5,4},{6,5},{7,6},{9,8},{10,9},{11,10},{13,12},{... | collective-permute-start | bytes 1572872 | tf_op jit(solution)/shard_map/ppermute | solution.py:108
  524.1 20.2 %collective-permute-start.32 = (bf16[256,1024]{1,0:T(8,128)(2,1)S(1)}, bf16[256,1024]{1,0:T(8,128)(2,1)S(1)}, u32[]{:S(2)}, u32[]{:S(2)}) collective-permute-start(bf16[256,1024]{1,0:T(8,128)(2,1)S(1)} %get-tuple-element.617), channel_id=1, source_target_pairs={{0,1},{1,2},{2,3},{4,5},{5,6},{6,7},{8,9},{9,10},{10,11},{12,13},{... | collective-permute-start | bytes 1572872 | tf_op jit(solution)/shard_map/ppermute | solution.py:108
  537.2 14.8 %collective-permute-start.35 = (bf16[256,1024]{1,0:T(8,128)(2,1)S(1)}, bf16[256,1024]{1,0:T(8,128)(2,1)S(1)}, u32[]{:S(2)}, u32[]{:S(2)}) collective-permute-start(bf16[256,1024]{1,0:T(8,128)(2,1)S(1)} %fusion.159), channel_id=1, source_target_pairs={{1,0},{2,1},{3,2},{5,4},{6,5},{7,6},{9,8},{10,9},{11,10},{13,12},{... | collective-permute-start | bytes 1572872 | tf_op jit(solution)/shard_map/ppermute | solution.py:108
  561.0 235.2 %all-reduce.6.cloned.1.call-start = ((), (), s32[]{:S(2)}) async-start(), calls=%async_computation.3 | async-start | bytes 16777216 | tf_op jit(solution)/shard_map/psum | solution.py:337
  565.7 22.9 %collective-permute-start.38 = (bf16[256,1024]{1,0:T(8,128)(2,1)}, bf16[256,1024]{1,0:T(8,128)(2,1)S(1)}, u32[]{:S(2)}, u32[]{:S(2)}) collective-permute-start(bf16[256,1024]{1,0:T(8,128)(2,1)} %collective-permute-done.36), channel_id=1, source_target_pairs={{0,1},{1,2},{2,3},{4,5},{5,6},{6,7},{8,9},{9,10},{10,11},{12,13},{... | collective-permute-start | bytes 1572872 | tf_op jit(solution)/shard_map/ppermute | solution.py:108
  572.6 33.1 %collective-permute-start.39 = (bf16[256,1024]{1,0:T(8,128)(2,1)}, bf16[256,1024]{1,0:T(8,128)(2,1)S(1)}, u32[]{:S(2)}, u32[]{:S(2)}) collective-permute-start(bf16[256,1024]{1,0:T(8,128)(2,1)} %collective-permute-done.37), channel_id=1, source_target_pairs={{1,0},{2,1},{3,2},{5,4},{6,5},{7,6},{9,8},{10,9},{11,10},{13,12},{... | collective-permute-start | bytes 1572872 | tf_op jit(solution)/shard_map/ppermute | solution.py:108
  588.6 27.5 %collective-permute-start.40 = (bf16[256,1024]{1,0:T(8,128)(2,1)S(1)}, bf16[256,1024]{1,0:T(8,128)(2,1)S(1)}, u32[]{:S(2)}, u32[]{:S(2)}) collective-permute-start(bf16[256,1024]{1,0:T(8,128)(2,1)S(1)} %collective-permute-done.38), channel_id=1, source_target_pairs={{0,1},{1,2},{2,3},{4,5},{5,6},{6,7},{8,9},{9,10},{10,11},{12,13},{... | collective-permute-start | bytes 1572872 | tf_op jit(solution)/shard_map/ppermute | solution.py:108
  (148 other events, 1571.9 us)
Sparse Core Ops, SparseCore 0:
  9.6 48.6 all-gather.6
  59.9 57.2 all-gather.8
  305.8 54.8 all-gather.10
  561.1 103.4 all-reduce.7
  669.8 126.3 all-reduce.5

commit v2 on v0

--- a/solution.py
+++ b/solution.py
@@ -101,6 +101,41 @@
 
 def head_total(partial_value):
     return lax.psum(partial_value.astype(jnp.bfloat16), "tensor").astype(jnp.float32)
+
+
+def _rotate(value, axis, count, step):
+    return lax.ppermute(value, axis, [(i, (i + step) % count) for i in range(count)])
+
+
+def direct_gather(block, axis):
+    count = lax.axis_size(axis)
+    me = lax.axis_index(axis)
+    pieces = [block] + [_rotate(block, axis, count, step) for step in range(1, count)]
+    stacked = jnp.stack(pieces)
+    owner = (me - jnp.arange(count)) % count
+    return jnp.zeros_like(stacked).at[owner].set(stacked)
+
+
+def direct_scatter(value, axis):
+    count = lax.axis_size(axis)
+    me = lax.axis_index(axis)
+    shards = value.reshape((count, value.shape[0] // count) + value.shape[1:])
+    total = lax.dynamic_index_in_dim(shards, me, 0, keepdims=False).astype(jnp.float32)
+    for step in range(1, count):
+        sent = lax.dynamic_index_in_dim(shards, (me + step) % count, 0, keepdims=False)
+        total = total + _rotate(sent, axis, count, step).astype(jnp.float32)
+    return total.astype(value.dtype)
+
+
+def direct_total(partial_value):
+    low_value = partial_value.astype(jnp.bfloat16)
+    reduced = direct_scatter(low_value, "tensor")
+    return direct_gather(reduced, "tensor").reshape(low_value.shape).astype(jnp.float32)
+
+
+def gathered_sum(pieces, weights, spec):
+    partial_value = jnp.einsum(spec, pieces, weights, preferred_element_type=jnp.float32)
+    return jnp.sum(partial_value.astype(jnp.bfloat16).astype(jnp.float32), axis=0)
 
 
 def local(
@@ -142,8 +177,11 @@
 
     self_heads, self_log = lax.map(self_clip, (projected[0], projected[1], projected[2], frame_len))
     self_flat = self_heads.reshape(row_total, local_width)
-    self_part = jnp.dot(self_flat, self_out, preferred_element_type=jnp.float32)
-    after_self = inputs + head_total(self_part)
+    self_out_all = lax.all_gather(self_out, "tensor")
+    cross_out_all = lax.all_gather(cross_out, "tensor")
+    cross_query_all = lax.all_gather(cross_query, "tensor")
+    self_pieces = direct_gather(self_flat, "tensor")
+    after_self = inputs + gathered_sum(self_pieces, self_out_all, "gsk,gkd->gsd")
     normed_cross = layer_norm(after_self, cross_gain, cross_bias).astype(jnp.bfloat16)
     cross_queries = jnp.dot(normed_cross, cross_query, preferred_element_type=jnp.float32).astype(
         jnp.bfloat16
@@ -161,13 +199,13 @@
         cross_clip, (cross_queries, text_proj[0], text_proj[1], text_token_length)
     )
     cross_flat = cross_heads.reshape(row_total, local_width)
-    cross_part = jnp.dot(cross_flat, cross_out, preferred_element_type=jnp.float32)
-    after_cross = after_self + head_total(cross_part)
+    cross_pieces = direct_gather(cross_flat, "tensor")
+    after_cross = after_self + gathered_sum(cross_pieces, cross_out_all, "gsk,gkd->gsd")
     normed_feed = layer_norm(after_cross, feed_gain, feed_bias).astype(jnp.bfloat16)
     upward = jnp.dot(normed_feed, feed_up, preferred_element_type=jnp.float32)
     active = gelu_exact(upward).astype(jnp.bfloat16)
     feed_part = jnp.dot(active, feed_down, preferred_element_type=jnp.float32)
-    block_out = (after_cross + head_total(feed_part)).astype(jnp.bfloat16)
+    block_out = (after_cross + direct_total(feed_part)).astype(jnp.bfloat16)
     active_grad = jnp.einsum("sd,kd->sk", out_grad, feed_down, preferred_element_type=jnp.float32)
     _, gelu_pull = jax.vjp(gelu_exact, upward)
     upward_grad = gelu_pull(active_grad)[0].astype(jnp.bfloat16)
@@ -175,10 +213,14 @@
         "sk,sd->kd", active, out_grad, preferred_element_type=jnp.float32
     )
     up_grad = jnp.einsum("sd,sk->dk", normed_feed, upward_grad, preferred_element_type=jnp.float32)
+    feed_sums = (
+        lax.psum(up_grad.astype(jnp.bfloat16), "dp").astype(jnp.float32),
+        lax.psum(downward_gradient.astype(jnp.bfloat16), "dp").astype(jnp.float32),
+    )
     feed_input_part = jnp.einsum(
         "sk,dk->sd", upward_grad, feed_up, preferred_element_type=jnp.float32
     )
-    feed_back = norm_back(after_cross, feed_gain, feed_bias, head_total(feed_input_part))
+    feed_back = norm_back(after_cross, feed_gain, feed_bias, direct_total(feed_input_part))
     cross_grad_rows = out_grad.astype(jnp.float32) + feed_back[0]
     cross_grad_low = cross_grad_rows.astype(jnp.bfloat16)
     cout_grad = jnp.einsum(
@@ -214,18 +256,15 @@
     ckeyval_grad = jnp.einsum(
         "ctd,gcte->gde", text_states, keyval_grad_low, preferred_element_type=jnp.float32
     )
-    cross_input_part = jnp.einsum(
-        "se,de->sd", query_grad_low, cross_query, preferred_element_type=jnp.float32
-    )
     text_part = jnp.einsum(
         "gcte,gde->ctd", keyval_grad_low, cross_keyval, preferred_element_type=jnp.float32
     )
-    cross_sum, text_grad = (
-        lax.psum(cross_input_part.astype(jnp.bfloat16), "tensor").astype(jnp.float32),
-        lax.psum(text_part.astype(jnp.bfloat16), "tensor").astype(jnp.float32),
-    )
+    query_pieces = direct_gather(query_grad_low, "tensor")
+    cross_sum = gathered_sum(query_pieces, cross_query_all, "gse,gde->gsd")
+    text_grad = lax.psum(text_part.astype(jnp.bfloat16), "tensor").astype(jnp.float32)
     cross_back = norm_back(after_self, cross_gain, cross_bias, cross_sum)
     self_grad_rows = cross_grad_rows + cross_back[0]
+    feed_sums, self_grad_rows = lax.optimization_barrier((feed_sums, self_grad_rows))
     self_grad_low = self_grad_rows.astype(jnp.bfloat16)
     sout_grad = jnp.einsum(
         "sk,sd->kd", self_flat, self_grad_low, preferred_element_type=jnp.float32
@@ -261,7 +300,7 @@
     self_input_part = jnp.einsum(
         "cse,cde->sd", projection_gradient, self_qkv, preferred_element_type=jnp.float32
     )
-    self_back = norm_back(inputs, self_gain, self_bias, head_total(self_input_part))
+    self_back = norm_back(inputs, self_gain, self_bias, direct_total(self_input_part))
     frames_grad = self_grad_rows + self_back[0]
     gain_terms = (
         self_back[1],
@@ -283,8 +322,8 @@
         lax.psum(cquery_grad.astype(jnp.bfloat16), "dp").astype(jnp.float32),
         lax.psum(ckeyval_grad.astype(jnp.bfloat16), "dp").astype(jnp.float32),
         lax.psum(cout_grad.astype(jnp.bfloat16), "dp").astype(jnp.float32),
-        lax.psum(up_grad.astype(jnp.bfloat16), "dp").astype(jnp.float32),
-        lax.psum(downward_gradient.astype(jnp.bfloat16), "dp").astype(jnp.float32),
+        feed_sums[0],
+        feed_sums[1],
     )
     return (
         block_out.reshape(clip_count, slot_len, model_width),

time: 899 us -> 782 us (0.87)
  waiting for transfers between devices: 584 us -> 250 us
  starting transfers between devices: 1.56 us -> 139 us
  local copies, waits for them, and re-layouts: 56.5 us -> 113 us
  other arithmetic: 94 us -> 116 us
    psum x5 -> x2, waiting for transfers between devices: 472 us -> 0.01 us  [the longest x1 0.01 us: local(): lax.psum(up_grad.astype(jnp.bfloat16), 'dp').astype(jnp.float32)]
    ppermute x0 -> x27, waiting for transfers between devices: none -> 249 us  [_rotate(): lax.ppermute(value, axis, [(i, (i + step) % count) for i in range(count)])]
    ppermute x0 -> x27, starting transfers between devices: none -> 138 us  [_rotate(): lax.ppermute(value, axis, [(i, (i + step) % count) for i in range(count)])]
    psum x1, waiting for transfers between devices: 111 us -> 0.01 us  [local(): lax.psum(qkv_grad.astype(jnp.bfloat16), 'dp').astype(jnp.float32)]
    scatter x0 -> x6, local copies, waits for them, and re-layouts: none -> 31.2 us  [direct_gather(): return jnp.zeros_like(stacked).at[owner].set(stacked)]
    another operation x6 -> x17, local copies, waits for them, and re-layouts: 3.35 us -> 25.2 us  [the longest x5 14.8 us: direct_gather(): stacked = jnp.stack(pieces)]
    another operation x4 -> x10, other arithmetic: 2.67 us -> 14.4 us  [the longest x6 14.2 us: direct_gather(): stacked = jnp.stack(pieces)]
    dot_general x3, matrix products: 9.35 us -> 20 us  [gathered_sum(): jnp.einsum(spec, pieces, weights, preferred_element_type=jnp.float32)]
  transfers between devices with their start and end apart: 6 -> 33, of which waited for: 6 -> 12; matrix products, arithmetic and copies ran while one was open for 6% -> 40% of each run, Pallas kernels for 0% -> 0%
where the time goes in v2:
time: 782 us; the launch traced here: 772 us
  waiting for transfers between devices  250 us (32%)
  starting transfers between devices  139 us (18%)
  other arithmetic  116 us (15%)
  local copies, waits for them, and re-layouts  113 us (14%)
  matrix products  113 us (14%)
  blocking collectives  23.6 us (3%)
  between operations  15.9 us (2%)
    ppermute x27, waiting for transfers between devices, _rotate(): lax.ppermute(value, axis, [(i, (i + step) % count) for i in range(count)])  249 us
    ppermute x27, starting transfers between devices, _rotate(): lax.ppermute(value, axis, [(i, (i + step) % count) for i in range(count)])  138 us
    scatter x6, local copies, waits for them, and re-layouts, direct_gather(): return jnp.zeros_like(stacked).at[owner].set(stacked)  31.2 us
    unnamed x201, local copies, waits for them, and re-layouts  24.5 us
    psum x1, blocking collectives, local(): lax.psum(gain_terms[0].astype(jnp.bfloat16), 'dp').astype(jnp.float32)  23.6 us
    dot_general x3, matrix products, gathered_sum(): jnp.einsum(spec, pieces, weights, preferred_element_type=jnp.float32)  20 us
    reduce_sum x5, other arithmetic, layer_norm(): return centred * lax.rsqrt(spread + EPSILON) * norm_gain + norm_bias  18.4 us
  transfers between devices with their start and end apart: 33, of which 12 were waited for; matrix products, arithmetic and copies ran while one was open for 40% of the time, Pallas kernels for 0%

profile of v2, /device:TPU:0, one launch (start us, length us, event | category | flops | bytes accessed | tf_op | source)
XLA Modules:
  0.0 771.7 jit_solution(18396485057692820861)
XLA Ops:
  19.3 20.4 %while.94 = (s32[]{:T(128)}, bf16[2,512,4,64]{1,3,2,0:T(8,128)(2,1)}, f32[2,4,512]{2,1,0:T(4,128)S(1)}, s32[]{:T(128)}, s32[2]{0:T(128)S(1)}, /*index=5*/bf16[2,...) while((s32[]{:T(128)}, ...), condition=%wide.region_5.6_spmd, body=%wide.region_2.5_spmd.sunk | while | flops 563215872 | bytes 35199192 | solution.py:57
  53.8 14.0 %collective-permute-done.2 = bf16[1024,256]{0,1:T(8,128)(2,1)} collective-permute-done((bf16[1024,256]{0,1:T(8,128)(2,1)}, bf16[1024,256]{0,1:T(8,128)(2,1)}, u32[]{:S(2)}, u32[]{:S(2)}) %collective-permute-start.2) | collective-permute-done | bytes 524320 | tf_op jit(solution)/shard_map/ppermute | solution.py:107
  67.8 54.9 %collective-permute-done.1 = bf16[1024,256]{0,1:T(8,128)(2,1)} collective-permute-done((bf16[1024,256]{0,1:T(8,128)(2,1)}, bf16[1024,256]{0,1:T(8,128)(2,1)}, u32[]{:S(2)}, u32[]{:S(2)}) %collective-permute-start.1) | collective-permute-done | bytes 524320 | tf_op jit(solution)/shard_map/ppermute | solution.py:107
  161.7 9.3 %collective-permute-done.5 = bf16[1024,256]{0,1:T(8,128)(2,1)} collective-permute-done((bf16[1024,256]{0,1:T(8,128)(2,1)}, bf16[1024,256]{0,1:T(8,128)(2,1)}, u32[]{:S(2)}, u32[]{:S(2)}) %collective-permute-start.5) | collective-permute-done | bytes 524320 | tf_op jit(solution)/shard_map/ppermute | solution.py:107
  171.0 58.6 %collective-permute-done.4 = bf16[1024,256]{0,1:T(8,128)(2,1)} collective-permute-done((bf16[1024,256]{0,1:T(8,128)(2,1)}, bf16[1024,256]{0,1:T(8,128)(2,1)}, u32[]{:S(2)}, u32[]{:S(2)}) %collective-permute-start.4) | collective-permute-done | bytes 524320 | tf_op jit(solution)/shard_map/ppermute | solution.py:107
  252.3 11.0 %multiply_convert_fusion.2 = (bf16[1024,1024]{1,0:T(8,128)(2,1)S(1)}, f32[1024,1024]{1,0:T(8,128)S(1)}, f32[1024,1024]{1,0:T(8,128)S(1)}) fusion(bf16[1024,1024]{1,0:T(8,128)(2,1)S(1)} %copy-done, f32[1024,1024]{1,0:T(8,128)S(1)} %get-tuple-element.651, f32[1024]{0:T(1024)S(1)} %copy-done.100, f32[1024]{0:T(1024)S(1)} %copy-done.73, ...), kind=kOutput, calls=%fused_computation.152 | convolution fusion | flops 2220883968 | bytes 16793600 | tf_op jit(solution)/shard_map/dot_general | solution.py:205
  291.1 23.8 %collective-permute-start.7 = (bf16[256,1024]{1,0:T(8,128)(2,1)}, bf16[256,1024]{1,0:T(8,128)(2,1)}, u32[]{:S(2)}, u32[]{:S(2)}) collective-permute-start(bf16[256,1024]{1,0:T(8,128)(2,1)} %get-tuple-element.674), channel_id=1, source_target_pairs={{0,2},{1,3},{2,0},{3,1},{4,6},{5,7},{6,4},{7,5},{8,10},{9,11},{10,... | collective-permute-start | bytes 1572872 | tf_op jit(solution)/shard_map/ppermute | solution.py:107
  314.9 22.4 %collective-permute-done.13 = bf16[256,1024]{1,0:T(8,128)(2,1)S(1)} collective-permute-done((bf16[256,1024]{1,0:T(8,128)(2,1)S(1)}, bf16[256,1024]{1,0:T(8,128)(2,1)S(1)}, u32[]{:S(2)}, u32[]{:S(2)}) %collective-permute-start.13) | collective-permute-done | bytes 524320 | tf_op jit(solution)/shard_map/ppermute | solution.py:107
  338.4 23.4 %collective-permute-start.17 = (bf16[256,1024]{1,0:T(8,128)(2,1)}, bf16[256,1024]{1,0:T(8,128)(2,1)}, u32[]{:S(2)}, u32[]{:S(2)}) collective-permute-start(bf16[256,1024]{1,0:T(8,128)(2,1)} %fusion.137), channel_id=1, source_target_pairs={{0,3},{1,0},{2,1},{3,2},{4,7},{5,4},{6,5},{7,6},{8,11},{9,8},{10,9... | collective-permute-start | bytes 1572872 | tf_op jit(solution)/shard_map/ppermute | solution.py:107
  362.6 18.5 %collective-permute-start.15 = (bf16[256,1024]{1,0:T(8,128)(2,1)}, bf16[256,1024]{1,0:T(8,128)(2,1)}, u32[]{:S(2)}, u32[]{:S(2)}) collective-permute-start(bf16[256,1024]{1,0:T(8,128)(2,1)} %fusion.137), channel_id=1, source_target_pairs={{0,1},{1,2},{2,3},{3,0},{4,5},{5,6},{6,7},{7,4},{8,9},{9,10},{10,1... | collective-permute-start | bytes 1572872 | tf_op jit(solution)/shard_map/ppermute | solution.py:107
  388.8 8.8 %collective-permute-start.11 = (bf16[256,1024]{1,0:T(8,128)(2,1)}, bf16[256,1024]{1,0:T(8,128)(2,1)}, u32[]{:S(2)}, u32[]{:S(2)}) collective-permute-start(bf16[256,1024]{1,0:T(8,128)(2,1)} %fusion.140), channel_id=1, source_target_pairs={{0,3},{1,0},{2,1},{3,2},{4,7},{5,4},{6,5},{7,6},{8,11},{9,8},{10,9... | collective-permute-start | bytes 1572872 | tf_op jit(solution)/shard_map/ppermute | solution.py:107
  398.5 7.4 collective-permute-done.16
  423.9 6.5 fusion.76
  439.8 12.9 %while.96 = (s32[]{:T(128)}, f32[128,4,64]{0,2,1:T(8,128)S(1)}, f32[128,4,64]{0,2,1:T(8,128)S(1)}, bf16[2,512,4,64]{1,3,2,0:T(8,128)(2,1)}, bf16[2,512,4,64]{1,3...) while((s32[]{:T(128)}, f32[128,4,64]{0,2,1:T(8,128)S(1)}, ...), condition=%wide.region_26.27_spmd.clone, body=%wide.region_24.26_spmd.clone.sunk | while | flops 170424448 | bytes 16491000 | solution.py:96
  455.3 22.6 %collective-permute-start.20 = (bf16[1024,256]{0,1:T(8,128)(2,1)}, bf16[1024,256]{0,1:T(8,128)(2,1)}, u32[]{:S(2)}, u32[]{:S(2)}) collective-permute-start(bf16[1024,256]{0,1:T(8,128)(2,1)} %bitcast.128), channel_id=1, source_target_pairs={{0,3},{1,0},{2,1},{3,2},{4,7},{5,4},{6,5},{7,6},{8,11},{9,8},{10,9... | collective-permute-start | bytes 1572872 | tf_op jit(solution)/shard_map/ppermute | solution.py:107
  477.9 10.1 %collective-permute-start.19 = (bf16[1024,256]{0,1:T(8,128)(2,1)}, bf16[1024,256]{0,1:T(8,128)(2,1)}, u32[]{:S(2)}, u32[]{:S(2)}) collective-permute-start(bf16[1024,256]{0,1:T(8,128)(2,1)} %bitcast.128), channel_id=1, source_target_pairs={{0,2},{1,3},{2,0},{3,1},{4,6},{5,7},{6,4},{7,5},{8,10},{9,11},{10,... | collective-permute-start | bytes 1572872 | tf_op jit(solution)/shard_map/ppermute | solution.py:107
  519.7 16.7 %collective-permute-done.19 = bf16[1024,256]{0,1:T(8,128)(2,1)} collective-permute-done((bf16[1024,256]{0,1:T(8,128)(2,1)}, bf16[1024,256]{0,1:T(8,128)(2,1)}, u32[]{:S(2)}, u32[]{:S(2)}) %collective-permute-start.19) | collective-permute-done | bytes 524320 | tf_op jit(solution)/shard_map/ppermute | solution.py:107
  544.1 9.7 %convert_reduce_fusion = (f32[1024,1024]{1,0:T(8,128)}, bf16[4,1024,1024]{2,1,0:T(8,128)(2,1)}) fusion(bf16[4,1024,256]{2,1,0:T(8,128)(2,1)S(1)} %scatter_fusion.4, bf16[4,1024,256]{2,1,0:T(8,128)(2,1)} %bitcast.448), kind=kOutput, calls=%fused_computation.104 | convolution fusion | flops 2159017984 | bytes 16777216 | tf_op jit(solution)/shard_map/gse,gde->gsd/dot_general | solution.py:137
  575.4 29.0 %while.97 = (s32[]{:T(128)}, f32[1024,4,64]{0,2,1:T(8,128)S(1)}, f32[1024,4,64]{0,2,1:T(8,128)}, bf16[2,512,4,64]{1,3,2,0:T(8,128)(2,1)}, bf16[2,512,4,64]{1,3,2...) while((s32[]{:T(128)}, f32[1024,4,64]{0,2,1:T(8,128)S(1)}, ...), condition=%wide.region_33.34_spmd.clone, body=%wide.region_31.33_spmd.clone.sunk | while | flops 1376124416 | bytes 87095624 | solution.py:96
  630.0 7.6 collective-permute-done.23
  637.5 20.2 %collective-permute-done.22 = bf16[256,1024]{1,0:T(8,128)(2,1)} collective-permute-done((bf16[256,1024]{1,0:T(8,128)(2,1)S(1)}, bf16[256,1024]{1,0:T(8,128)(2,1)}, u32[]{:S(2)}, u32[]{:S(2)}) %collective-permute-start.22) | collective-permute-done | bytes 524320 | tf_op jit(solution)/shard_map/ppermute | solution.py:107
  665.2 7.8 %collective-permute-done.26 = bf16[256,1024]{1,0:T(8,128)(2,1)S(1)} collective-permute-done((bf16[256,1024]{1,0:T(8,128)(2,1)S(1)}, bf16[256,1024]{1,0:T(8,128)(2,1)S(1)}, u32[]{:S(2)}, u32[]{:S(2)}) %collective-permute-start.26) | collective-permute-done | bytes 524320 | tf_op jit(solution)/shard_map/ppermute | solution.py:107
  673.0 29.3 %collective-permute-done.25 = bf16[256,1024]{1,0:T(8,128)(2,1)} collective-permute-done((bf16[256,1024]{1,0:T(8,128)(2,1)S(1)}, bf16[256,1024]{1,0:T(8,128)(2,1)}, u32[]{:S(2)}, u32[]{:S(2)}) %collective-permute-start.25) | collective-permute-done | bytes 524320 | tf_op jit(solution)/shard_map/ppermute | solution.py:107
  718.0 23.6 %all-reduce = (bf16[1024]{0:T(1024)(128)(2,1)S(1)}, bf16[1024]{0:T(1024)(128)(2,1)S(1)}, bf16[1024]{0:T(1024)(128)(2,1)S(1)}, bf16[1024]{0:T(1024)(128)(2,1)S(1)...) all-reduce(bf16[1024]{0:T(1024)(128)(2,1)S(1)} %get-tuple-element.5, ...), channel_id=1, replica_groups=mesh['dp'=8,'tensor'=4] {'dp'}, use_global_device_ids=true, to_apply=%region_39.40 | all-reduce | flops 6144 | bytes 24576 | tf_op jit(solution)/shard_map/psum | solution.py:314
  (497 shorter events, 351.6 us)
Async XLA Ops:
  7.2 129.7 %all-gather.7.cloned.1.call-start = ((), (), s32[]{:S(2)}) async-start(), calls=%async_computation.1 | async-start | bytes 2621440 | tf_op jit(solution)/shard_map/all_gather | solution.py:180
  8.0 236.4 %all-gather.9.cloned.1.call-start = ((), (), s32[]{:S(2)}) async-start(), calls=%async_computation.2 | async-start | bytes 2621440 | tf_op jit(solution)/shard_map/all_gather | solution.py:181
  48.5 74.2 %collective-permute-start.1 = (bf16[1024,256]{0,1:T(8,128)(2,1)}, bf16[1024,256]{0,1:T(8,128)(2,1)}, u32[]{:S(2)}, u32[]{:S(2)}) collective-permute-start(bf16[1024,256]{0,1:T(8,128)(2,1)} %bitcast.114), channel_id=1, source_target_pairs={{0,2},{1,3},{2,0},{3,1},{4,6},{5,7},{6,4},{7,5},{8,10},{9,11},{10,... | collective-permute-start | bytes 1572872 | tf_op jit(solution)/shard_map/ppermute | solution.py:107
  48.5 74.2 %collective-permute-start = (bf16[1024,256]{0,1:T(8,128)(2,1)}, bf16[1024,256]{0,1:T(8,128)(2,1)}, u32[]{:S(2)}, u32[]{:S(2)}) collective-permute-start(bf16[1024,256]{0,1:T(8,128)(2,1)} %bitcast.114), channel_id=1, source_target_pairs={{0,1},{1,2},{2,3},{3,0},{4,5},{5,6},{6,7},{7,4},{8,9},{9,10},{10,1... | collective-permute-start | bytes 1572872 | tf_op jit(solution)/shard_map/ppermute | solution.py:107
  49.5 494.5 %all-gather.11.cloned.1.call-start = ((), (), s32[]{:S(2)}) async-start(), calls=%async_computation.3 | async-start | bytes 2621440 | tf_op jit(solution)/shard_map/all_gather | solution.py:182
  156.7 72.9 %collective-permute-start.4 = (bf16[1024,256]{0,1:T(8,128)(2,1)}, bf16[1024,256]{0,1:T(8,128)(2,1)}, u32[]{:S(2)}, u32[]{:S(2)}) collective-permute-start(bf16[1024,256]{0,1:T(8,128)(2,1)} %bitcast.120), channel_id=1, source_target_pairs={{0,2},{1,3},{2,0},{3,1},{4,6},{5,7},{6,4},{7,5},{8,10},{9,11},{10,... | collective-permute-start | bytes 1572872 | tf_op jit(solution)/shard_map/ppermute | solution.py:107
  156.7 72.9 %collective-permute-start.3 = (bf16[1024,256]{0,1:T(8,128)(2,1)}, bf16[1024,256]{0,1:T(8,128)(2,1)}, u32[]{:S(2)}, u32[]{:S(2)}) collective-permute-start(bf16[1024,256]{0,1:T(8,128)(2,1)} %bitcast.120), channel_id=1, source_target_pairs={{0,1},{1,2},{2,3},{3,0},{4,5},{5,6},{6,7},{7,4},{8,9},{9,10},{10,1... | collective-permute-start | bytes 1572872 | tf_op jit(solution)/shard_map/ppermute | solution.py:107
  158.8 403.2 %all-reduce.11.cloned.1.call-start = ((), (), s32[]{:S(2)}) async-start(), calls=%async_computation.5 | async-start | bytes 8388608 | tf_op jit(solution)/shard_map/psum | solution.py:217
  275.7 61.6 %collective-permute-start.13 = (bf16[256,1024]{1,0:T(8,128)(2,1)S(1)}, bf16[256,1024]{1,0:T(8,128)(2,1)S(1)}, u32[]{:S(2)}, u32[]{:S(2)}) collective-permute-start(bf16[256,1024]{1,0:T(8,128)(2,1)S(1)} %get-tuple-element.671), channel_id=1, source_target_pairs={{0,2},{1,3},{2,0},{3,1},{4,6},{5,7},{6,4},{7,5},{8,10},{9,11},{10,... | collective-permute-start | bytes 1572872 | tf_op jit(solution)/shard_map/ppermute | solution.py:107
  283.0 78.8 %collective-permute-start.6 = (bf16[256,1024]{1,0:T(8,128)(2,1)S(1)}, bf16[256,1024]{1,0:T(8,128)(2,1)S(1)}, u32[]{:S(2)}, u32[]{:S(2)}) collective-permute-start(bf16[256,1024]{1,0:T(8,128)(2,1)S(1)} %get-tuple-element.672), channel_id=1, source_target_pairs={{0,1},{1,2},{2,3},{3,0},{4,5},{5,6},{6,7},{7,4},{8,9},{9,10},{10,1... | collective-permute-start | bytes 1572872 | tf_op jit(solution)/shard_map/ppermute | solution.py:107
  287.3 99.0 %collective-permute-start.8 = (bf16[256,1024]{1,0:T(8,128)(2,1)}, bf16[256,1024]{1,0:T(8,128)(2,1)}, u32[]{:S(2)}, u32[]{:S(2)}) collective-permute-start(bf16[256,1024]{1,0:T(8,128)(2,1)} %get-tuple-element.673), channel_id=1, source_target_pairs={{0,3},{1,0},{2,1},{3,2},{4,7},{5,4},{6,5},{7,6},{8,11},{9,8},{10,9... | collective-permute-start | bytes 1572872 | tf_op jit(solution)/shard_map/ppermute | solution.py:107
  291.1 95.2 %collective-permute-start.7 = (bf16[256,1024]{1,0:T(8,128)(2,1)}, bf16[256,1024]{1,0:T(8,128)(2,1)}, u32[]{:S(2)}, u32[]{:S(2)}) collective-permute-start(bf16[256,1024]{1,0:T(8,128)(2,1)} %get-tuple-element.674), channel_id=1, source_target_pairs={{0,2},{1,3},{2,0},{3,1},{4,6},{5,7},{6,4},{7,5},{8,10},{9,11},{10,... | collective-permute-start | bytes 1572872 | tf_op jit(solution)/shard_map/ppermute | solution.py:107
  338.4 59.2 %collective-permute-start.17 = (bf16[256,1024]{1,0:T(8,128)(2,1)}, bf16[256,1024]{1,0:T(8,128)(2,1)}, u32[]{:S(2)}, u32[]{:S(2)}) collective-permute-start(bf16[256,1024]{1,0:T(8,128)(2,1)} %fusion.137), channel_id=1, source_target_pairs={{0,3},{1,0},{2,1},{3,2},{4,7},{5,4},{6,5},{7,6},{8,11},{9,8},{10,9... | collective-permute-start | bytes 1572872 | tf_op jit(solution)/shard_map/ppermute | solution.py:107
  361.8 44.1 %collective-permute-start.16 = (bf16[256,1024]{1,0:T(8,128)(2,1)}, bf16[256,1024]{1,0:T(8,128)(2,1)}, u32[]{:S(2)}, u32[]{:S(2)}) collective-permute-start(bf16[256,1024]{1,0:T(8,128)(2,1)} %fusion.137), channel_id=1, source_target_pairs={{0,2},{1,3},{2,0},{3,1},{4,6},{5,7},{6,4},{7,5},{8,10},{9,11},{10,... | collective-permute-start | bytes 1572872 | tf_op jit(solution)/shard_map/ppermute | solution.py:107
  362.6 43.3 %collective-permute-start.15 = (bf16[256,1024]{1,0:T(8,128)(2,1)}, bf16[256,1024]{1,0:T(8,128)(2,1)}, u32[]{:S(2)}, u32[]{:S(2)}) collective-permute-start(bf16[256,1024]{1,0:T(8,128)(2,1)} %fusion.137), channel_id=1, source_target_pairs={{0,1},{1,2},{2,3},{3,0},{4,5},{5,6},{6,7},{7,4},{8,9},{9,10},{10,1... | collective-permute-start | bytes 1572872 | tf_op jit(solution)/shard_map/ppermute | solution.py:107
  386.2 232.1 %all-reduce.7.cloned.1.call-start = ((), (), s32[]{:S(2)}) async-start(), calls=%async_computation | async-start | bytes 524288 | tf_op jit(solution)/shard_map/psum | solution.py:264
  388.8 99.5 %collective-permute-start.11 = (bf16[256,1024]{1,0:T(8,128)(2,1)}, bf16[256,1024]{1,0:T(8,128)(2,1)}, u32[]{:S(2)}, u32[]{:S(2)}) collective-permute-start(bf16[256,1024]{1,0:T(8,128)(2,1)} %fusion.140), channel_id=1, source_target_pairs={{0,3},{1,0},{2,1},{3,2},{4,7},{5,4},{6,5},{7,6},{8,11},{9,8},{10,9... | collective-permute-start | bytes 1572872 | tf_op jit(solution)/shard_map/ppermute | solution.py:107
  397.6 92.8 %collective-permute-start.10 = (bf16[256,1024]{1,0:T(8,128)(2,1)}, bf16[256,1024]{1,0:T(8,128)(2,1)}, u32[]{:S(2)}, u32[]{:S(2)}) collective-permute-start(bf16[256,1024]{1,0:T(8,128)(2,1)} %fusion.140), channel_id=1, source_target_pairs={{0,2},{1,3},{2,0},{3,1},{4,6},{5,7},{6,4},{7,5},{8,10},{9,11},{10,... | collective-permute-start | bytes 1572872 | tf_op jit(solution)/shard_map/ppermute | solution.py:107
  397.6 92.8 %collective-permute-start.9 = (bf16[256,1024]{1,0:T(8,128)(2,1)}, bf16[256,1024]{1,0:T(8,128)(2,1)}, u32[]{:S(2)}, u32[]{:S(2)}) collective-permute-start(bf16[256,1024]{1,0:T(8,128)(2,1)} %fusion.140), channel_id=1, source_target_pairs={{0,1},{1,2},{2,3},{3,0},{4,5},{5,6},{6,7},{7,4},{8,9},{9,10},{10,1... | collective-permute-start | bytes 1572872 | tf_op jit(solution)/shard_map/ppermute | solution.py:107
  455.3 64.4 %collective-permute-start.20 = (bf16[1024,256]{0,1:T(8,128)(2,1)}, bf16[1024,256]{0,1:T(8,128)(2,1)}, u32[]{:S(2)}, u32[]{:S(2)}) collective-permute-start(bf16[1024,256]{0,1:T(8,128)(2,1)} %bitcast.128), channel_id=1, source_target_pairs={{0,3},{1,0},{2,1},{3,2},{4,7},{5,4},{6,5},{7,6},{8,11},{9,8},{10,9... | collective-permute-start | bytes 1572872 | tf_op jit(solution)/shard_map/ppermute | solution.py:107
  477.9 58.5 %collective-permute-start.19 = (bf16[1024,256]{0,1:T(8,128)(2,1)}, bf16[1024,256]{0,1:T(8,128)(2,1)}, u32[]{:S(2)}, u32[]{:S(2)}) collective-permute-start(bf16[1024,256]{0,1:T(8,128)(2,1)} %bitcast.128), channel_id=1, source_target_pairs={{0,2},{1,3},{2,0},{3,1},{4,6},{5,7},{6,4},{7,5},{8,10},{9,11},{10,... | collective-permute-start | bytes 1572872 | tf_op jit(solution)/shard_map/ppermute | solution.py:107
  488.3 48.1 %collective-permute-start.18 = (bf16[1024,256]{0,1:T(8,128)(2,1)}, bf16[1024,256]{0,1:T(8,128)(2,1)}, u32[]{:S(2)}, u32[]{:S(2)}) collective-permute-start(bf16[1024,256]{0,1:T(8,128)(2,1)} %bitcast.128), channel_id=1, source_target_pairs={{0,1},{1,2},{2,3},{3,0},{4,5},{5,6},{6,7},{7,4},{8,9},{9,10},{10,1... | collective-permute-start | bytes 1572872 | tf_op jit(solution)/shard_map/ppermute | solution.py:107
  514.7 238.3 %all-reduce.9.cloned.1.call-start = ((), (), s32[]{:S(2)}) async-start(), calls=%async_computation.4 | async-start | bytes 8388608 | tf_op jit(solution)/shard_map/psum | solution.py:320
  660.7 41.6 %collective-permute-start.25 = (bf16[256,1024]{1,0:T(8,128)(2,1)S(1)}, bf16[256,1024]{1,0:T(8,128)(2,1)}, u32[]{:S(2)}, u32[]{:S(2)}) collective-permute-start(bf16[256,1024]{1,0:T(8,128)(2,1)S(1)} %fusion.134), channel_id=1, source_target_pairs={{0,2},{1,3},{2,0},{3,1},{4,6},{5,7},{6,4},{7,5},{8,10},{9,11},{10,... | collective-permute-start | bytes 1572872 | tf_op jit(solution)/shard_map/ppermute | solution.py:107
  (127 other events, 1999.5 us)
Sparse Core Ops, SparseCore 0:
  9.6 51.8 all-gather.6
  63.1 73.6 all-gather.8
  158.9 76.2 all-gather.10
  386.4 80.6 all-reduce.10
  514.9 35.4 all-reduce.6
  665.3 81.7 all-reduce.8

commit v3 on v1

--- a/solution.py
+++ b/solution.py
@@ -103,11 +103,6 @@
     return lax.psum(partial_value.astype(jnp.bfloat16), "tensor").astype(jnp.float32)
 
 
-def _shift(value, axis, count, step):
-    pairs = [(i, i + step) for i in range(count) if 0 <= i + step < count]
-    return lax.ppermute(value, axis, pairs)
-
-
 def relay_gather(block, axis):
     count = lax.axis_size(axis)
     me = lax.axis_index(axis)
@@ -115,8 +110,8 @@
     out = lax.dynamic_update_index_in_dim(out, block, me, 0)
     from_left, from_right = block, block
     for k in range(1, count):
-        from_left = _shift(from_left, axis, count, 1)
-        from_right = _shift(from_right, axis, count, -1)
+        from_left = lax.ppermute(from_left, axis, [(i, i + 1) for i in range(k - 1, count - 1)])
+        from_right = lax.ppermute(from_right, axis, [(i, i - 1) for i in range(1, count - k + 1)])
         out = lax.dynamic_update_index_in_dim(
             out, from_left, jnp.where(me - k >= 0, me - k, count), 0
         )
@@ -141,8 +136,12 @@
         if to_right is not None:
             send_right = send_right + to_right.astype(jnp.float32)
             send_left = send_left + to_left.astype(jnp.float32)
-        to_right = _shift(send_right.astype(value.dtype), axis, count, 1)
-        to_left = _shift(send_left.astype(value.dtype), axis, count, -1)
+        to_right = lax.ppermute(
+            send_right.astype(value.dtype), axis, [(i, i + 1) for i in range(min(k, count - 1))]
+        )
+        to_left = lax.ppermute(
+            send_left.astype(value.dtype), axis, [(i, i - 1) for i in range(max(count - k, 1), count)]
+        )
     total = pick(me).astype(jnp.float32)
     if to_right is not None:
         total = total + to_right.astype(jnp.float32) + to_left.astype(jnp.float32)
@@ -227,7 +226,7 @@
     upward = jnp.dot(normed_feed, feed_up, preferred_element_type=jnp.float32)
     active = gelu_exact(upward).astype(jnp.bfloat16)
     feed_part = jnp.dot(active, feed_down, preferred_element_type=jnp.float32)
-    block_out = (after_cross + head_total(feed_part)).astype(jnp.bfloat16)
+    block_out = (after_cross + relay_total(feed_part)).astype(jnp.bfloat16)
     active_grad = jnp.einsum("sd,kd->sk", out_grad, feed_down, preferred_element_type=jnp.float32)
     _, gelu_pull = jax.vjp(gelu_exact, upward)
     upward_grad = gelu_pull(active_grad)[0].astype(jnp.bfloat16)
@@ -235,6 +234,10 @@
         "sk,sd->kd", active, out_grad, preferred_element_type=jnp.float32
     )
     up_grad = jnp.einsum("sd,sk->dk", normed_feed, upward_grad, preferred_element_type=jnp.float32)
+    feed_sums = (
+        lax.psum(up_grad.astype(jnp.bfloat16), "dp").astype(jnp.float32),
+        lax.psum(downward_gradient.astype(jnp.bfloat16), "dp").astype(jnp.float32),
+    )
     feed_input_part = jnp.einsum(
         "sk,dk->sd", upward_grad, feed_up, preferred_element_type=jnp.float32
     )
@@ -282,6 +285,7 @@
     text_grad = lax.psum(text_part.astype(jnp.bfloat16), "tensor").astype(jnp.float32)
     cross_back = norm_back(after_self, cross_gain, cross_bias, cross_sum)
     self_grad_rows = cross_grad_rows + cross_back[0]
+    feed_sums, self_grad_rows = lax.optimization_barrier((feed_sums, self_grad_rows))
     self_grad_low = self_grad_rows.astype(jnp.bfloat16)
     sout_grad = jnp.einsum(
         "sk,sd->kd", self_flat, self_grad_low, preferred_element_type=jnp.float32
@@ -339,8 +343,8 @@
         lax.psum(cquery_grad.astype(jnp.bfloat16), "dp").astype(jnp.float32),
         lax.psum(ckeyval_grad.astype(jnp.bfloat16), "dp").astype(jnp.float32),
         lax.psum(cout_grad.astype(jnp.bfloat16), "dp").astype(jnp.float32),
-        lax.psum(up_grad.astype(jnp.bfloat16), "dp").astype(jnp.float32),
-        lax.psum(downward_gradient.astype(jnp.bfloat16), "dp").astype(jnp.float32),
+        feed_sums[0],
+        feed_sums[1],
     )
     return (
         block_out.reshape(clip_count, slot_len, model_width),

time: 831 us -> 788 us (0.948)
  waiting for transfers between devices: 305 us -> 249 us
  local copies, waits for them, and re-layouts: 114 us -> 137 us
  starting transfers between devices: 138 us -> 120 us
    psum x1, waiting for transfers between devices: 95.7 us -> 25.8 us  [local(): lax.psum(qkv_grad.astype(jnp.bfloat16), 'dp').astype(jnp.float32)]
    convert_element_type x6 -> x11, other arithmetic: 8.14 us -> 26.7 us  [the longest x1 9.14 us: local(): cross_grad_low = cross_grad_rows.astype(jnp.bfloat16)]
    ppermute x42 -> x54, starting transfers between devices: 138 us -> 120 us  [the longest x18 48.7 us: relay_gather(): lax.ppermute(from_left, axis, [(i, i + 1) for i in range(k - 1, count - 1)])]
    ppermute x42 -> x54, waiting for transfers between devices: 194 us -> 209 us  [the longest x18 153 us: relay_gather(): lax.ppermute(from_right, axis, [(i, i - 1) for i in range(1, count - k +...]
    add x1, other arithmetic: 10.3 us -> 0.47 us  [local(): self_grad_rows = cross_grad_rows + cross_back[0]]
    reduce_sum x6 -> x5, other arithmetic: 24.5 us -> 17.3 us  [layer_norm(): return centred * lax.rsqrt(spread + EPSILON) * norm_gain + norm_bias]
    dynamic_update_slice x15 -> x18, local copies, waits for them, and re-layouts: 19.8 us -> 26.8 us  [relay_gather(): lax.dynamic_update_index_in_dim(out, from_left, jnp.where(me - k >= 0, me...]
    dynamic_update_slice x15 -> x18, local copies, waits for them, and re-layouts: 17.7 us -> 24.3 us  [relay_gather(): lax.dynamic_update_index_in_dim(out, from_right, jnp.where(me + k < count...]
  transfers between devices with their start and end apart: 47 -> 60, of which waited for: 34 -> 26; matrix products, arithmetic and copies ran while one was open for 25% -> 40% of each run, Pallas kernels for 0% -> 0%
where the time goes in v3:
time: 788 us; the launch traced here: 775 us
  waiting for transfers between devices  249 us (32%)
  local copies, waits for them, and re-layouts  137 us (17%)
  starting transfers between devices  120 us (15%)
  other arithmetic  120 us (15%)
  matrix products  109 us (14%)
  blocking collectives  22.6 us (3%)
  between operations  16.3 us (2%)
    ppermute x18, waiting for transfers between devices, relay_gather(): lax.ppermute(from_right, axis, [(i, i - 1) for i in range(1, count - k +...  153 us
    ppermute x18, starting transfers between devices, relay_gather(): lax.ppermute(from_left, axis, [(i, i + 1) for i in range(k - 1, count - 1)])  48.7 us
    ppermute x9, starting transfers between devices, relay_scatter(): lax.ppermute(send_right.astype(value.dtype), axis, [(i, i + 1) for i in r...  35.6 us
    dynamic_update_slice x18, local copies, waits for them, and re-layouts, relay_gather(): lax.dynamic_update_index_in_dim(out, from_left, jnp.where(me - k >= 0, me...  26.8 us
    psum x1, waiting for transfers between devices, local(): lax.psum(qkv_grad.astype(jnp.bfloat16), 'dp').astype(jnp.float32)  25.8 us
    ppermute x18, starting transfers between devices, relay_gather(): lax.ppermute(from_right, axis, [(i, i - 1) for i in range(1, count - k +...  24.5 us
    dynamic_update_slice x18, local copies, waits for them, and re-layouts, relay_gather(): lax.dynamic_update_index_in_dim(out, from_right, jnp.where(me + k < count...  24.3 us
    psum x1, blocking collectives, local(): lax.psum(gain_terms[0].astype(jnp.bfloat16), 'dp').astype(jnp.float32)  22.6 us
  transfers between devices with their start and end apart: 60, of which 26 were waited for; matrix products, arithmetic and copies ran while one was open for 40% of the time, Pallas kernels for 0%

profile of v3, /device:TPU:0, one launch (start us, length us, event | category | flops | bytes accessed | tf_op | source)
XLA Modules:
  0.0 775.4 jit_solution(12350436799990054765)
XLA Ops:
  20.5 21.6 %while.94 = (s32[]{:T(128)}, bf16[2,512,4,64]{1,3,2,0:T(8,128)(2,1)}, f32[2,4,512]{2,1,0:T(4,128)}, s32[]{:T(128)}, s32[2]{0:T(128)}, /*index=5*/bf16[2,512,4,64...) while((s32[]{:T(128)}, ...), condition=%wide.region_5.6_spmd, body=%wide.region_2.5_spmd.sunk | while | flops 563215872 | bytes 35199192 | solution.py:57
  77.1 31.6 %collective-permute-done.3 = bf16[1024,256]{1,0:T(8,128)(2,1)S(1)} collective-permute-done((bf16[1024,256]{1,0:T(8,128)(2,1)}, bf16[1024,256]{1,0:T(8,128)(2,1)S(1)}, u32[]{:S(2)}, u32[]{:S(2)}) %collective-permute-start.3) | collective-permute-done | bytes 524320 | tf_op jit(solution)/shard_map/ppermute | solution.py:114
  113.7 13.5 %collective-permute-done.5 = bf16[1024,256]{1,0:T(8,128)(2,1)S(1)} collective-permute-done((bf16[1024,256]{1,0:T(8,128)(2,1)S(1)}, bf16[1024,256]{1,0:T(8,128)(2,1)S(1)}, u32[]{:S(2)}, u32[]{:S(2)}) %collective-permute-start.5) | collective-permute-done | bytes 524320 | tf_op jit(solution)/shard_map/ppermute | solution.py:114
  151.3 8.7 %collective-permute-done.6 = bf16[1024,256]{1,0:T(8,128)(2,1)} collective-permute-done((bf16[1024,256]{1,0:T(8,128)(2,1)}, bf16[1024,256]{1,0:T(8,128)(2,1)}, u32[]{:S(2)}, u32[]{:S(2)}) %collective-permute-start.6) | collective-permute-done | bytes 524320 | tf_op jit(solution)/shard_map/ppermute | solution.py:113
  173.2 10.8 %collective-permute-done.9 = bf16[1024,256]{1,0:T(8,128)(2,1)S(1)} collective-permute-done((bf16[1024,256]{1,0:T(8,128)(2,1)}, bf16[1024,256]{1,0:T(8,128)(2,1)S(1)}, u32[]{:S(2)}, u32[]{:S(2)}) %collective-permute-start.9) | collective-permute-done | bytes 524320 | tf_op jit(solution)/shard_map/ppermute | solution.py:114
  189.1 8.9 %collective-permute-done.11 = bf16[1024,256]{1,0:T(8,128)(2,1)S(1)} collective-permute-done((bf16[1024,256]{1,0:T(8,128)(2,1)S(1)}, bf16[1024,256]{1,0:T(8,128)(2,1)S(1)}, u32[]{:S(2)}, u32[]{:S(2)}) %collective-permute-start.11) | collective-permute-done | bytes 524320 | tf_op jit(solution)/shard_map/ppermute | solution.py:114
  205.2 11.0 %multiply_convert_fusion.2 = (bf16[1024,1024]{1,0:T(8,128)(2,1)S(1)}, f32[1024,1024]{1,0:T(8,128)S(1)}, f32[1024,1024]{1,0:T(8,128)S(1)}) fusion(bf16[1024,1024]{1,0:T(8,128)(2,1)S(1)} %copy-done, f32[1024,1024]{1,0:T(8,128)S(1)} %get-tuple-element.605, f32[1024]{0:T(1024)S(1)} %copy-done.95, f32[1024]{0:T(1024)S(1)} %copy-done.71, f32[1024]{0:T(1024)S(1)} %fusion.160, ...), kind=kOutput, calls=%fused_computation.146 | convolution fusion | flops 2220883968 | bytes 16793600 | tf_op jit(solution)/shard_map/dot_general | solution.py:226
  279.2 6.4 collective-permute-start.14
  296.1 13.0 %collective-permute-start.30 = (bf16[256,1024]{1,0:T(8,128)(2,1)}, bf16[256,1024]{1,0:T(8,128)(2,1)}, u32[]{:S(2)}, u32[]{:S(2)}) collective-permute-start(bf16[256,1024]{1,0:T(8,128)(2,1)} %get-tuple-element.599), channel_id=1, source_target_pairs={{0,1},{1,2},{2,3},{4,5},{5,6},{6,7},{8,9},{9,10},{10,11},{12,13},{... | collective-permute-start | bytes 1572872 | tf_op jit(solution)/shard_map/ppermute | solution.py:113
  322.9 13.6 %all-reduce.11.cloned.1.call-done = (bf16[1024,1024]{1,0:T(8,128)(2,1)}, bf16[1024,1024]{1,0:T(8,128)(2,1)}) async-done(((bf16[1024,1024]{1,0:T(8,128)(2,1)}, bf16[1024,1024]{1,0:T(8,128)(2,1)}), (bf16[1024,1024]{1,0:T(8,128)(2,1)}, bf16[1024,1024]{1,0:T(8,128)(2,1)})) %all-reduce.11.cloned.1.call-update) | async-done | bytes 4194320 | tf_op jit(solution)/shard_map/psum | solution.py:238
  357.2 28.5 %collective-permute-done.33 = bf16[256,1024]{1,0:T(8,128)(2,1)S(1)} collective-permute-done((bf16[256,1024]{1,0:T(8,128)(2,1)}, bf16[256,1024]{1,0:T(8,128)(2,1)S(1)}, u32[]{:S(2)}, u32[]{:S(2)}) %collective-permute-start.33) | collective-permute-done | bytes 524320 | tf_op jit(solution)/shard_map/ppermute | solution.py:114
  391.3 13.5 %collective-permute-done.21 = bf16[256,1024]{1,0:T(8,128)(2,1)} collective-permute-done((bf16[256,1024]{1,0:T(8,128)(2,1)}, bf16[256,1024]{1,0:T(8,128)(2,1)}, u32[]{:S(2)}, u32[]{:S(2)}) %collective-permute-start.21) | collective-permute-done | bytes 524320 | tf_op jit(solution)/shard_map/ppermute | solution.py:114
  409.2 6.7 collective-permute-done.35
  441.1 12.9 %while.96 = (s32[]{:T(128)}, f32[128,4,64]{0,2,1:T(8,128)S(1)}, f32[128,4,64]{0,2,1:T(8,128)S(1)}, bf16[2,512,4,64]{1,3,2,0:T(8,128)(2,1)}, bf16[2,512,4,64]{1,3...) while((s32[]{:T(128)}, f32[128,4,64]{0,2,1:T(8,128)S(1)}, ...), condition=%wide.region_22.23_spmd.clone, body=%wide.region_20.22_spmd.clone.sunk | while | flops 170424448 | bytes 16491000 | solution.py:96
  477.8 9.1 %fusion.101 = (bf16[1024,1024]{1,0:T(8,128)(2,1)}, bf16[1,1024,1024]{2,1,0:T(8,128)(2,1)}) fusion(bf16[1,1024,1024]{2,1,0:T(8,128)(2,1)} %param.43, f32[1024]{0:T(1024)S(1)} %bitcast.542, f32[1024]{0:T(1024)} %get-tuple-element.641, f32[1024]{0:T(1024)S(1)} %copy-done.62, f32[1024]{0:T(1024)S(1)} %copy-done.70, f32[1024]{0:T(1024)S(1)} %copy-done.74, ...), kind=kLoop, calls=%fused_computation.171 | loop fusion | flops 16777216 | bytes 23089152 | tf_op jit(solution)/shard_map/convert_element_type | solution.py:246
  499.6 11.9 %collective-permute-done.39 = bf16[1024,256]{1,0:T(8,128)(2,1)S(1)} collective-permute-done((bf16[1024,256]{1,0:T(8,128)(2,1)}, bf16[1024,256]{1,0:T(8,128)(2,1)S(1)}, u32[]{:S(2)}, u32[]{:S(2)}) %collective-permute-start.39) | collective-permute-done | bytes 524320 | tf_op jit(solution)/shard_map/ppermute | solution.py:114
  515.5 7.8 %collective-permute-done.41 = bf16[1024,256]{1,0:T(8,128)(2,1)S(1)} collective-permute-done((bf16[1024,256]{1,0:T(8,128)(2,1)S(1)}, bf16[1024,256]{1,0:T(8,128)(2,1)S(1)}, u32[]{:S(2)}, u32[]{:S(2)}) %collective-permute-start.41) | collective-permute-done | bytes 524320 | tf_op jit(solution)/shard_map/ppermute | solution.py:114
  524.1 10.5 %convert_reduce_fusion = (f32[1024,1024]{1,0:T(8,128)}, bf16[4,1024,1024]{2,1,0:T(8,128)(2,1)}) fusion(bf16[5,1024,256]{2,1,0:T(8,128)(2,1)} %bitcast_dynamic-update-slice_fusion.9, bf16[4,1024,256]{2,1,0:T(8,128)(2,1)} %bitcast.544), kind=kOutput, calls=%fused_computation.98 | convolution fusion | flops 2159017984 | bytes 17301504 | tf_op jit(solution)/shard_map/gse,gde->gsd/dot_general | solution.py:158
  548.1 31.5 %while.97 = (s32[]{:T(128)}, f32[1024,4,64]{0,2,1:T(8,128)S(1)}, f32[1024,4,64]{0,2,1:T(8,128)}, bf16[2,512,4,64]{1,3,2,0:T(8,128)(2,1)}, bf16[2,512,4,64]{1,3,2...) while((s32[]{:T(128)}, f32[1024,4,64]{0,2,1:T(8,128)S(1)}, ...), condition=%wide.region_28.29_spmd.clone, body=%wide.region_26.28_spmd.clone.sunk | while | flops 1376124416 | bytes 87095624 | solution.py:96
  623.9 12.7 %collective-permute-done.47 = bf16[256,1024]{1,0:T(8,128)(2,1)S(1)} collective-permute-done((bf16[256,1024]{1,0:T(8,128)(2,1)S(1)}, bf16[256,1024]{1,0:T(8,128)(2,1)S(1)}, u32[]{:S(2)}, u32[]{:S(2)}) %collective-permute-start.47) | collective-permute-done | bytes 524320 | tf_op jit(solution)/shard_map/ppermute | solution.py:142
  652.7 9.4 %collective-permute-done.49 = bf16[256,1024]{1,0:T(8,128)(2,1)} collective-permute-done((bf16[256,1024]{1,0:T(8,128)(2,1)S(1)}, bf16[256,1024]{1,0:T(8,128)(2,1)}, u32[]{:S(2)}, u32[]{:S(2)}) %collective-permute-start.49) | collective-permute-done | bytes 524320 | tf_op jit(solution)/shard_map/ppermute | solution.py:114
  669.8 25.8 %all-reduce.9.cloned.1.call-done = (bf16[3,1024,256]{1,2,0:T(8,128)(2,1)}, bf16[2,1024,256]{1,2,0:T(8,128)(2,1)}, bf16[256,1024]{1,0:T(8,128)(2,1)}, bf16[1024,256]{1,0:T(8,128)(2,1)}, bf16[256,1024]{1,0:T(8,128)(2,1)}) async-done(((bf16[3,1024,256]{1,2,0:T(8,128)(2,1)}, bf16[2,1024,256]{1,2,0:T(8,128)(2,1)}, bf16[256,1024]{1,0:T(8,128)(2,1)}, bf16[1024,256]{1,0:T(8,128)(2,1)}, ...) | async-done | bytes 4194320 | tf_op jit(solution)/shard_map/psum | solution.py:341
  717.4 9.3 %collective-permute-done.53 = bf16[256,1024]{1,0:T(8,128)(2,1)S(1)} collective-permute-done((bf16[256,1024]{1,0:T(8,128)(2,1)}, bf16[256,1024]{1,0:T(8,128)(2,1)S(1)}, u32[]{:S(2)}, u32[]{:S(2)}) %collective-permute-start.53) | collective-permute-done | bytes 524320 | tf_op jit(solution)/shard_map/ppermute | solution.py:114
  733.0 22.6 %all-reduce = (bf16[1024]{0:T(1024)(128)(2,1)S(1)}, bf16[1024]{0:T(1024)(128)(2,1)S(1)}, bf16[1024]{0:T(1024)(128)(2,1)S(1)}, bf16[1024]{0:T(1024)(128)(2,1)S(1)...) all-reduce(bf16[1024]{0:T(1024)(128)(2,1)S(1)} %get-tuple-element.5, ...), channel_id=1, replica_groups=mesh['dp'=8,'tensor'=4] {'dp'}, use_global_device_ids=true, to_apply=%region_33.34 | all-reduce | flops 6144 | bytes 24576 | tf_op jit(solution)/shard_map/psum | solution.py:335
  (576 shorter events, 476.0 us)
Async XLA Ops:
  7.2 120.8 %all-gather.7.cloned.1.call-start = ((), (), s32[]{:S(2)}) async-start(), calls=%async_computation.1 | async-start | bytes 2621440 | tf_op jit(solution)/shard_map/all_gather | solution.py:201
  8.0 190.9 %all-gather.9.cloned.1.call-start = ((), (), s32[]{:S(2)}) async-start(), calls=%async_computation.2 | async-start | bytes 2621440 | tf_op jit(solution)/shard_map/all_gather | solution.py:202
  54.1 282.4 %all-reduce.11.cloned.1.call-start = ((), (), s32[]{:S(2)}) async-start(), calls=%async_computation.5 | async-start | bytes 8388608 | tf_op jit(solution)/shard_map/psum | solution.py:238
  68.9 39.8 %collective-permute-start.3 = (bf16[1024,256]{1,0:T(8,128)(2,1)}, bf16[1024,256]{1,0:T(8,128)(2,1)S(1)}, u32[]{:S(2)}, u32[]{:S(2)}) collective-permute-start(bf16[1024,256]{1,0:T(8,128)(2,1)} %collective-permute-done.1), channel_id=1, source_target_pairs={{1,0},{2,1},{5,4},{6,5},{9,8},{10,9},{13,12},{14,13},{17,16},{18,1... | collective-permute-start | bytes 1572872 | tf_op jit(solution)/shard_map/ppermute | solution.py:114
  74.6 38.3 %collective-permute-start.4 = (bf16[1024,256]{1,0:T(8,128)(2,1)}, bf16[1024,256]{1,0:T(8,128)(2,1)S(1)}, u32[]{:S(2)}, u32[]{:S(2)}) collective-permute-start(bf16[1024,256]{1,0:T(8,128)(2,1)} %collective-permute-done.2), channel_id=1, source_target_pairs={{2,3},{6,7},{10,11},{14,15},{18,19},{22,23},{26,27},{30,31}} | collective-permute-start | bytes 1572872 | tf_op jit(solution)/shard_map/ppermute | solution.py:113
  257.4 266.7 %all-gather.11.cloned.1.call-start = ((), (), s32[]{:S(2)}) async-start(), calls=%async_computation.3 | async-start | bytes 2621440 | tf_op jit(solution)/shard_map/all_gather | solution.py:203
  279.2 31.2 %collective-permute-start.14 = (bf16[256,1024]{1,0:T(8,128)(2,1)}, bf16[256,1024]{1,0:T(8,128)(2,1)S(1)}, u32[]{:S(2)}, u32[]{:S(2)}) collective-permute-start(bf16[256,1024]{1,0:T(8,128)(2,1)} %get-tuple-element.628), channel_id=1, source_target_pairs={{0,1},{1,2},{2,3},{4,5},{5,6},{6,7},{8,9},{9,10},{10,11},{12,13},{... | collective-permute-start | bytes 1572872 | tf_op jit(solution)/shard_map/ppermute | solution.py:139
  296.1 47.1 %collective-permute-start.30 = (bf16[256,1024]{1,0:T(8,128)(2,1)}, bf16[256,1024]{1,0:T(8,128)(2,1)}, u32[]{:S(2)}, u32[]{:S(2)}) collective-permute-start(bf16[256,1024]{1,0:T(8,128)(2,1)} %get-tuple-element.599), channel_id=1, source_target_pairs={{0,1},{1,2},{2,3},{4,5},{5,6},{6,7},{8,9},{9,10},{10,11},{12,13},{... | collective-permute-start | bytes 1572872 | tf_op jit(solution)/shard_map/ppermute | solution.py:113
  309.1 36.7 %collective-permute-start.31 = (bf16[256,1024]{1,0:T(8,128)(2,1)}, bf16[256,1024]{1,0:T(8,128)(2,1)}, u32[]{:S(2)}, u32[]{:S(2)}) collective-permute-start(bf16[256,1024]{1,0:T(8,128)(2,1)} %get-tuple-element.599), channel_id=1, source_target_pairs={{1,0},{2,1},{3,2},{5,4},{6,5},{7,6},{9,8},{10,9},{11,10},{13,12},{... | collective-permute-start | bytes 1572872 | tf_op jit(solution)/shard_map/ppermute | solution.py:114
  314.6 34.3 %collective-permute-start.18 = (bf16[256,1024]{1,0:T(8,128)(2,1)}, bf16[256,1024]{1,0:T(8,128)(2,1)}, u32[]{:S(2)}, u32[]{:S(2)}) collective-permute-start(bf16[256,1024]{1,0:T(8,128)(2,1)} %get-tuple-element.601), channel_id=1, source_target_pairs={{0,1},{1,2},{2,3},{4,5},{5,6},{6,7},{8,9},{9,10},{10,11},{12,13},{... | collective-permute-start | bytes 1572872 | tf_op jit(solution)/shard_map/ppermute | solution.py:113
  320.2 343.2 %all-reduce.7.cloned.1.call-start = ((), (), s32[]{:S(2)}) async-start(), calls=%async_computation | async-start | bytes 524288 | tf_op jit(solution)/shard_map/psum | solution.py:285
  321.6 30.9 %collective-permute-start.19 = (bf16[256,1024]{1,0:T(8,128)(2,1)}, bf16[256,1024]{1,0:T(8,128)(2,1)}, u32[]{:S(2)}, u32[]{:S(2)}) collective-permute-start(bf16[256,1024]{1,0:T(8,128)(2,1)} %get-tuple-element.601), channel_id=1, source_target_pairs={{1,0},{2,1},{3,2},{5,4},{6,5},{7,6},{9,8},{10,9},{11,10},{13,12},{... | collective-permute-start | bytes 1572872 | tf_op jit(solution)/shard_map/ppermute | solution.py:114
  345.8 40.0 %collective-permute-start.33 = (bf16[256,1024]{1,0:T(8,128)(2,1)}, bf16[256,1024]{1,0:T(8,128)(2,1)S(1)}, u32[]{:S(2)}, u32[]{:S(2)}) collective-permute-start(bf16[256,1024]{1,0:T(8,128)(2,1)} %collective-permute-done.31), channel_id=1, source_target_pairs={{1,0},{2,1},{5,4},{6,5},{9,8},{10,9},{13,12},{14,13},{17,16},{18,1... | collective-permute-start | bytes 1572872 | tf_op jit(solution)/shard_map/ppermute | solution.py:114
  349.0 38.9 %collective-permute-start.20 = (bf16[256,1024]{1,0:T(8,128)(2,1)}, bf16[256,1024]{1,0:T(8,128)(2,1)}, u32[]{:S(2)}, u32[]{:S(2)}) collective-permute-start(bf16[256,1024]{1,0:T(8,128)(2,1)} %collective-permute-done.18), channel_id=1, source_target_pairs={{1,2},{2,3},{5,6},{6,7},{9,10},{10,11},{13,14},{14,15},{17,18},{18... | collective-permute-start | bytes 1572872 | tf_op jit(solution)/shard_map/ppermute | solution.py:113
  352.5 52.2 %collective-permute-start.21 = (bf16[256,1024]{1,0:T(8,128)(2,1)}, bf16[256,1024]{1,0:T(8,128)(2,1)}, u32[]{:S(2)}, u32[]{:S(2)}) collective-permute-start(bf16[256,1024]{1,0:T(8,128)(2,1)} %collective-permute-done.19), channel_id=1, source_target_pairs={{1,0},{2,1},{5,4},{6,5},{9,8},{10,9},{13,12},{14,13},{17,16},{18,1... | collective-permute-start | bytes 1572872 | tf_op jit(solution)/shard_map/ppermute | solution.py:114
  355.7 52.6 %collective-permute-start.34 = (bf16[256,1024]{1,0:T(8,128)(2,1)S(1)}, bf16[256,1024]{1,0:T(8,128)(2,1)S(1)}, u32[]{:S(2)}, u32[]{:S(2)}) collective-permute-start(bf16[256,1024]{1,0:T(8,128)(2,1)S(1)} %collective-permute-done.32), channel_id=1, source_target_pairs={{2,3},{6,7},{10,11},{14,15},{18,19},{22,23},{26,27},{30,31}} | collective-permute-start | bytes 1572872 | tf_op jit(solution)/shard_map/ppermute | solution.py:113
  385.8 30.1 %collective-permute-start.35 = (bf16[256,1024]{1,0:T(8,128)(2,1)S(1)}, bf16[256,1024]{1,0:T(8,128)(2,1)S(1)}, u32[]{:S(2)}, u32[]{:S(2)}) collective-permute-start(bf16[256,1024]{1,0:T(8,128)(2,1)S(1)} %collective-permute-done.33), channel_id=1, source_target_pairs={{1,0},{5,4},{9,8},{13,12},{17,16},{21,20},{25,24},{29,28}} | collective-permute-start | bytes 1572872 | tf_op jit(solution)/shard_map/ppermute | solution.py:114
  387.9 75.4 %collective-permute-start.22 = (bf16[256,1024]{1,0:T(8,128)(2,1)}, bf16[256,1024]{1,0:T(8,128)(2,1)}, u32[]{:S(2)}, u32[]{:S(2)}) collective-permute-start(bf16[256,1024]{1,0:T(8,128)(2,1)} %collective-permute-done.20), channel_id=1, source_target_pairs={{2,3},{6,7},{10,11},{14,15},{18,19},{22,23},{26,27},{30,31}} | collective-permute-start | bytes 1572872 | tf_op jit(solution)/shard_map/ppermute | solution.py:113
  404.8 60.4 %collective-permute-start.23 = (bf16[256,1024]{1,0:T(8,128)(2,1)}, bf16[256,1024]{1,0:T(8,128)(2,1)}, u32[]{:S(2)}, u32[]{:S(2)}) collective-permute-start(bf16[256,1024]{1,0:T(8,128)(2,1)} %collective-permute-done.21), channel_id=1, source_target_pairs={{1,0},{5,4},{9,8},{13,12},{17,16},{21,20},{25,24},{29,28}} | collective-permute-start | bytes 1572872 | tf_op jit(solution)/shard_map/ppermute | solution.py:114
  456.6 34.8 %collective-permute-start.37 = (bf16[1024,256]{1,0:T(8,128)(2,1)}, bf16[1024,256]{1,0:T(8,128)(2,1)}, u32[]{:S(2)}, u32[]{:S(2)}) collective-permute-start(bf16[1024,256]{1,0:T(8,128)(2,1)} %copy.86), channel_id=1, source_target_pairs={{1,0},{2,1},{3,2},{5,4},{6,5},{7,6},{9,8},{10,9},{11,10},{13,12},{... | collective-permute-start | bytes 1572872 | tf_op jit(solution)/shard_map/ppermute | solution.py:114
  457.9 31.4 %collective-permute-start.36 = (bf16[1024,256]{1,0:T(8,128)(2,1)}, bf16[1024,256]{1,0:T(8,128)(2,1)}, u32[]{:S(2)}, u32[]{:S(2)}) collective-permute-start(bf16[1024,256]{1,0:T(8,128)(2,1)} %copy.86), channel_id=1, source_target_pairs={{0,1},{1,2},{2,3},{4,5},{5,6},{6,7},{8,9},{9,10},{10,11},{12,13},{... | collective-permute-start | bytes 1572872 | tf_op jit(solution)/shard_map/ppermute | solution.py:113
  477.7 217.9 %all-reduce.9.cloned.1.call-start = ((), (), s32[]{:S(2)}) async-start(), calls=%async_computation.4 | async-start | bytes 8388608 | tf_op jit(solution)/shard_map/psum | solution.py:341
  651.2 57.4 %collective-permute-start.50 = (bf16[256,1024]{1,0:T(8,128)(2,1)}, bf16[256,1024]{1,0:T(8,128)(2,1)}, u32[]{:S(2)}, u32[]{:S(2)}) collective-permute-start(bf16[256,1024]{1,0:T(8,128)(2,1)} %collective-permute-done.48), channel_id=1, source_target_pairs={{1,2},{2,3},{5,6},{6,7},{9,10},{10,11},{13,14},{14,15},{17,18},{18... | collective-permute-start | bytes 1572872 | tf_op jit(solution)/shard_map/ppermute | solution.py:113
  662.1 49.1 %collective-permute-start.51 = (bf16[256,1024]{1,0:T(8,128)(2,1)}, bf16[256,1024]{1,0:T(8,128)(2,1)}, u32[]{:S(2)}, u32[]{:S(2)}) collective-permute-start(bf16[256,1024]{1,0:T(8,128)(2,1)} %collective-permute-done.49), channel_id=1, source_target_pairs={{1,0},{2,1},{5,4},{6,5},{9,8},{10,9},{13,12},{14,13},{17,16},{18,1... | collective-permute-start | bytes 1572872 | tf_op jit(solution)/shard_map/ppermute | solution.py:114
  (147 other events, 1810.4 us)
Sparse Core Ops, SparseCore 0:
  9.6 48.6 all-gather.6
  59.9 56.3 all-gather.8
  257.5 78.9 all-reduce.10
  337.9 60.5 all-gather.10
  477.8 35.0 all-reduce.6
  612.4 83.1 all-reduce.8

commit v4 on v3

--- a/solution.py
+++ b/solution.py
@@ -15,6 +15,13 @@
     centred = inputs - row_mean
     spread = jnp.mean(centred * centred, axis=-1, keepdims=True)
     return centred * lax.rsqrt(spread + EPSILON) * norm_gain + norm_bias
+
+
+def normalized(inputs):
+    row_mean = jnp.mean(inputs, axis=-1, keepdims=True)
+    centred = inputs - row_mean
+    spread = jnp.mean(centred * centred, axis=-1, keepdims=True)
+    return centred * lax.rsqrt(spread + EPSILON)
 
 
 def norm_back(inputs, norm_gain, norm_bias, upstream):
@@ -152,6 +159,16 @@
     low_value = partial_value.astype(jnp.bfloat16)
     reduced = relay_scatter(low_value, "tensor")
     return relay_gather(reduced, "tensor").reshape(low_value.shape).astype(jnp.float32)
+
+
+def flat_psum(terms, axis):
+    flat = jnp.concatenate([term.astype(jnp.bfloat16).reshape(-1) for term in terms])
+    flat = lax.psum(flat, axis).astype(jnp.float32)
+    out, start = [], 0
+    for term in terms:
+        out.append(flat[start : start + term.size].reshape(term.shape))
+        start += term.size
+    return out
 
 
 def gathered_sum(pieces, weights, spec):
@@ -226,7 +243,7 @@
     upward = jnp.dot(normed_feed, feed_up, preferred_element_type=jnp.float32)
     active = gelu_exact(upward).astype(jnp.bfloat16)
     feed_part = jnp.dot(active, feed_down, preferred_element_type=jnp.float32)
-    block_out = (after_cross + relay_total(feed_part)).astype(jnp.bfloat16)
+    feed_low = feed_part.astype(jnp.bfloat16)
     active_grad = jnp.einsum("sd,kd->sk", out_grad, feed_down, preferred_element_type=jnp.float32)
     _, gelu_pull = jax.vjp(gelu_exact, upward)
     upward_grad = gelu_pull(active_grad)[0].astype(jnp.bfloat16)
@@ -234,14 +251,11 @@
         "sk,sd->kd", active, out_grad, preferred_element_type=jnp.float32
     )
     up_grad = jnp.einsum("sd,sk->dk", normed_feed, upward_grad, preferred_element_type=jnp.float32)
-    feed_sums = (
-        lax.psum(up_grad.astype(jnp.bfloat16), "dp").astype(jnp.float32),
-        lax.psum(downward_gradient.astype(jnp.bfloat16), "dp").astype(jnp.float32),
-    )
     feed_input_part = jnp.einsum(
         "sk,dk->sd", upward_grad, feed_up, preferred_element_type=jnp.float32
     )
     feed_back = norm_back(after_cross, feed_gain, feed_bias, relay_total(feed_input_part))
+    feed_sums = flat_psum((up_grad, downward_gradient, feed_back[1], feed_back[2]), "dp")
     cross_grad_rows = out_grad.astype(jnp.float32) + feed_back[0]
     cross_grad_low = cross_grad_rows.astype(jnp.bfloat16)
     cout_grad = jnp.einsum(
@@ -269,6 +283,10 @@
         (cross_queries, text_proj[0], text_proj[1], cross_log, cross_heads_grad, text_token_length),
     )
     query_grad_low = cquery_heads.reshape(row_total, local_width).astype(jnp.bfloat16)
+    feed_low, query_grad_low = lax.optimization_barrier((feed_low, query_grad_low))
+    block_out = (after_cross + lax.psum(feed_low, "tensor").astype(jnp.float32)).astype(
+        jnp.bfloat16
+    )
     keyval_grad_low = jnp.stack((ckey_heads, cvalue_heads)).astype(jnp.bfloat16)
     keyval_grad_low = keyval_grad_low.reshape(2, clip_count, text_count, local_width)
     cquery_grad = jnp.einsum(
@@ -322,6 +340,11 @@
         "cse,cde->sd", projection_gradient, self_qkv, preferred_element_type=jnp.float32
     )
     self_back = norm_back(inputs, self_gain, self_bias, relay_total(self_input_part))
+    own_part = self_input_part.astype(jnp.bfloat16).astype(jnp.float32)
+    self_norm_terms = lax.psum(
+        jnp.stack((jnp.sum(own_part * normalized(inputs), axis=0), jnp.sum(own_part, axis=0))),
+        ("dp", "tensor"),
+    )
     frames_grad = self_grad_rows + self_back[0]
     gain_terms = (
         self_back[1],
@@ -331,18 +354,22 @@
         feed_back[1],
         feed_back[2],
     )
+    late_sums = flat_psum(
+        (qkv_grad, sout_grad, cquery_grad, ckeyval_grad, cout_grad, cross_back[1], cross_back[2]),
+        "dp",
+    )
     summed = (
-        lax.psum(gain_terms[0].astype(jnp.bfloat16), "dp").astype(jnp.float32),
-        lax.psum(gain_terms[1].astype(jnp.bfloat16), "dp").astype(jnp.float32),
-        lax.psum(gain_terms[2].astype(jnp.bfloat16), "dp").astype(jnp.float32),
-        lax.psum(gain_terms[3].astype(jnp.bfloat16), "dp").astype(jnp.float32),
-        lax.psum(gain_terms[4].astype(jnp.bfloat16), "dp").astype(jnp.float32),
-        lax.psum(gain_terms[5].astype(jnp.bfloat16), "dp").astype(jnp.float32),
-        lax.psum(qkv_grad.astype(jnp.bfloat16), "dp").astype(jnp.float32),
-        lax.psum(sout_grad.astype(jnp.bfloat16), "dp").astype(jnp.float32),
-        lax.psum(cquery_grad.astype(jnp.bfloat16), "dp").astype(jnp.float32),
-        lax.psum(ckeyval_grad.astype(jnp.bfloat16), "dp").astype(jnp.float32),
-        lax.psum(cout_grad.astype(jnp.bfloat16), "dp").astype(jnp.float32),
+        self_norm_terms[0],
+        self_norm_terms[1],
+        late_sums[5],
+        late_sums[6],
+        feed_sums[2],
+        feed_sums[3],
+        late_sums[0],
+        late_sums[1],
+        late_sums[2],
+        late_sums[3],
+        late_sums[4],
         feed_sums[0],
         feed_sums[1],
     )

time: 788 us -> 797 us (1.011)
  local copies, waits for them, and re-layouts: 137 us -> 186 us
  starting transfers between devices: 120 us -> 83.5 us
  waiting for transfers between devices: 249 us -> 214 us
  blocking collectives: 22.6 us -> 37.4 us
  matrix products: 109 us -> 118 us
  other arithmetic: 120 us -> 128 us
    ppermute x18 -> x15, waiting for transfers between devices: 153 us -> 92.1 us  [relay_gather(): lax.ppermute(from_right, axis, [(i, i - 1) for i in range(1, count - k +...]
    ppermute x9 -> x6, waiting for transfers between devices: 15.4 us -> 50.5 us  [relay_scatter(): lax.ppermute(send_left.astype(value.dtype), axis, [(i, i - 1) for i in ra...]
    slice x1 -> x12, local copies, waits for them, and re-layouts: 3.08 us -> 32.3 us  [the longest x11 31.7 us: flat_psum(): out.append(flat[start:start + term.size].reshape(term.shape))]
    concatenate x0 -> x1, other arithmetic: none -> 20.1 us  [flat_psum(): jnp.concatenate([term.astype(jnp.bfloat16).reshape(-1) for term in terms])]
    convert_element_type x11 -> x1, other arithmetic: 16.7 us -> 0.72 us  [local(): layer_norm(after_self, cross_gain, cross_bias).astype(jnp.bfloat16)]
    psum x1, blocking collectives: 22.6 us -> 37.4 us  [local(): lax.psum(jnp.stack((jnp.sum(own_part * normalized(inputs), axis=0), jnp.s...]
    ppermute x18 -> x15, starting transfers between devices: 48.7 us -> 33.9 us  [relay_gather(): lax.ppermute(from_left, axis, [(i, i + 1) for i in range(k - 1, count - 1)])]
    psum x3, waiting for transfers between devices: 39.4 us -> 25.1 us  [the longest x2 25.1 us: flat_psum(): flat = lax.psum(flat, axis).astype(jnp.float32)]
  transfers between devices with their start and end apart: 60 -> 48, of which waited for: 26 -> 22; matrix products, arithmetic and copies ran while one was open for 40% -> 48% of each run, Pallas kernels for 0% -> 0%
where the time goes in v4:
time: 797 us; the launch traced here: 784 us
  waiting for transfers between devices  214 us (27%)
  local copies, waits for them, and re-layouts  186 us (23%)
  other arithmetic  128 us (16%)
  matrix products  118 us (15%)
  starting transfers between devices  83.5 us (10%)
  blocking collectives  37.4 us (5%)
  between operations  15.7 us (2%)
    ppermute x15, waiting for transfers between devices, relay_gather(): lax.ppermute(from_right, axis, [(i, i - 1) for i in range(1, count - k +...  92.1 us
    ppermute x6, waiting for transfers between devices, relay_scatter(): lax.ppermute(send_left.astype(value.dtype), axis, [(i, i - 1) for i in ra...  50.5 us
    psum x1, blocking collectives, local(): lax.psum(jnp.stack((jnp.sum(own_part * normalized(inputs), axis=0), jnp.s...  37.4 us
    unnamed x194, local copies, waits for them, and re-layouts  34.1 us
    ppermute x15, starting transfers between devices, relay_gather(): lax.ppermute(from_left, axis, [(i, i + 1) for i in range(k - 1, count - 1)])  33.9 us
    slice x11, local copies, waits for them, and re-layouts, flat_psum(): out.append(flat[start:start + term.size].reshape(term.shape))  31.7 us
    ppermute x6, waiting for transfers between devices, relay_scatter(): lax.ppermute(send_right.astype(value.dtype), axis, [(i, i + 1) for i in r...  30.9 us
    psum x2, waiting for transfers between devices, flat_psum(): flat = lax.psum(flat, axis).astype(jnp.float32)  25.1 us
  transfers between devices with their start and end apart: 48, of which 22 were waited for; matrix products, arithmetic and copies ran while one was open for 48% of the time, Pallas kernels for 0%

profile of v4, /device:TPU:0, one launch (start us, length us, event | category | flops | bytes accessed | tf_op | source)
XLA Modules:
  0.0 784.3 jit_solution(16280731302570558542)
XLA Ops:
  20.5 21.6 %while.94 = (s32[]{:T(128)}, bf16[2,512,4,64]{1,3,2,0:T(8,128)(2,1)}, f32[2,4,512]{2,1,0:T(4,128)}, s32[]{:T(128)}, s32[2]{0:T(128)}, /*index=5*/bf16[2,512,4,64...) while((s32[]{:T(128)}, ...), condition=%wide.region_5.6_spmd, body=%wide.region_2.5_spmd.sunk | while | flops 563215872 | bytes 35199192 | solution.py:64
  77.1 31.6 %collective-permute-done.3 = bf16[1024,256]{1,0:T(8,128)(2,1)S(1)} collective-permute-done((bf16[1024,256]{1,0:T(8,128)(2,1)}, bf16[1024,256]{1,0:T(8,128)(2,1)S(1)}, u32[]{:S(2)}, u32[]{:S(2)}) %collective-permute-start.3) | collective-permute-done | bytes 524320 | tf_op jit(solution)/shard_map/ppermute | solution.py:121
  113.8 13.4 %collective-permute-done.5 = bf16[1024,256]{1,0:T(8,128)(2,1)S(1)} collective-permute-done((bf16[1024,256]{1,0:T(8,128)(2,1)S(1)}, bf16[1024,256]{1,0:T(8,128)(2,1)S(1)}, u32[]{:S(2)}, u32[]{:S(2)}) %collective-permute-start.5) | collective-permute-done | bytes 524320 | tf_op jit(solution)/shard_map/ppermute | solution.py:121
  152.4 8.7 %collective-permute-done.6 = bf16[1024,256]{1,0:T(8,128)(2,1)} collective-permute-done((bf16[1024,256]{1,0:T(8,128)(2,1)}, bf16[1024,256]{1,0:T(8,128)(2,1)}, u32[]{:S(2)}, u32[]{:S(2)}) %collective-permute-start.6) | collective-permute-done | bytes 524320 | tf_op jit(solution)/shard_map/ppermute | solution.py:120
  174.3 10.8 %collective-permute-done.9 = bf16[1024,256]{1,0:T(8,128)(2,1)S(1)} collective-permute-done((bf16[1024,256]{1,0:T(8,128)(2,1)}, bf16[1024,256]{1,0:T(8,128)(2,1)S(1)}, u32[]{:S(2)}, u32[]{:S(2)}) %collective-permute-start.9) | collective-permute-done | bytes 524320 | tf_op jit(solution)/shard_map/ppermute | solution.py:121
  190.3 8.8 %collective-permute-done.11 = bf16[1024,256]{1,0:T(8,128)(2,1)S(1)} collective-permute-done((bf16[1024,256]{1,0:T(8,128)(2,1)S(1)}, bf16[1024,256]{1,0:T(8,128)(2,1)S(1)}, u32[]{:S(2)}, u32[]{:S(2)}) %collective-permute-start.11) | collective-permute-done | bytes 524320 | tf_op jit(solution)/shard_map/ppermute | solution.py:121
  207.8 12.7 %multiply_convert_fusion.2 = (bf16[1024,1024]{1,0:T(8,128)(2,1)}, f32[1024,1024]{1,0:T(8,128)S(1)}, f32[1024,1024]{1,0:T(8,128)S(1)}) fusion(bf16[1024,1024]{1,0:T(8,128)(2,1)S(1)} %copy-done, f32[1024,1024]{1,0:T(8,128)S(1)} %get-tuple-element.569, f32[1024]{0:T(1024)S(1)} %copy-done.93, f32[1024]{0:T(1024)S(1)} %copy-done.72, f32[1024]{0:T(1024)S(1)} %fusion.148, ...), kind=kOutput, calls=%fused_computation.144 | convolution fusion | flops 2220883968 | bytes 16793600 | tf_op jit(solution)/shard_map/dot_general | solution.py:243
  230.4 8.0 %collective-permute-done.12 = bf16[256,1024]{1,0:T(8,128)(2,1)S(1)} collective-permute-done((bf16[256,1024]{1,0:T(8,128)(2,1)S(1)}, bf16[256,1024]{1,0:T(8,128)(2,1)S(1)}, u32[]{:S(2)}, u32[]{:S(2)}) %collective-permute-start.12) | collective-permute-done | bytes 524320 | tf_op jit(solution)/shard_map/ppermute | solution.py:146
  244.1 8.0 %collective-permute-done.13 = bf16[256,1024]{1,0:T(8,128)(2,1)S(1)} collective-permute-done((bf16[256,1024]{1,0:T(8,128)(2,1)S(1)}, bf16[256,1024]{1,0:T(8,128)(2,1)S(1)}, u32[]{:S(2)}, u32[]{:S(2)}) %collective-permute-start.13) | collective-permute-done | bytes 524320 | tf_op jit(solution)/shard_map/ppermute | solution.py:146
  262.8 7.2 convert_bitcast_fusion.1
  270.3 34.5 %collective-permute-done.17 = bf16[256,1024]{1,0:T(8,128)(2,1)S(1)} collective-permute-done((bf16[256,1024]{1,0:T(8,128)(2,1)S(1)}, bf16[256,1024]{1,0:T(8,128)(2,1)S(1)}, u32[]{:S(2)}, u32[]{:S(2)}) %collective-permute-start.17) | collective-permute-done | bytes 524320 | tf_op jit(solution)/shard_map/ppermute | solution.py:149
  360.8 20.1 %pad_maximum_fusion = bf16[2099200]{0:T(1024)(128)(2,1)} fusion(bf16[1024]{0:T(1024)(128)(2,1)S(1)} %get-tuple-element.590, bf16[1024]{0:T(1024)(128)(2,1)S(1)} %get-tuple-element.479, bf16[1048576]{0:T(1024)(128)(2,1)S(1)} %bitcast.489, bf16[1048576]{0:T(1024)(128)(2,1)S(1)} %bitcast.488), kind=kLoop, calls=%fused_computation.111 | loop fusion | flops 16793600 | bytes 8396800 | tf_op jit(solution)/shard_map/concatenate | solution.py:165
  385.6 6.4 fusion.77
  401.9 12.9 %while.96 = (s32[]{:T(128)}, f32[128,4,64]{0,2,1:T(8,128)S(1)}, f32[128,4,64]{0,2,1:T(8,128)S(1)}, bf16[2,512,4,64]{1,3,2,0:T(8,128)(2,1)}, bf16[2,512,4,64]{1,3...) while((s32[]{:T(128)}, f32[128,4,64]{0,2,1:T(8,128)S(1)}, ...), condition=%wide.region_20.21_spmd.clone, body=%wide.region_18.20_spmd.clone.sunk | while | flops 170424448 | bytes 16491000 | solution.py:103
  426.1 7.8 fusion.84
  471.6 10.6 %convert_reduce_fusion = (f32[1024,1024]{1,0:T(8,128)}, bf16[4,1024,1024]{2,1,0:T(8,128)(2,1)}) fusion(bf16[5,1024,256]{2,1,0:T(8,128)(2,1)} %bitcast_dynamic-update-slice_fusion.9, bf16[4,1024,256]{2,1,0:T(8,128)(2,1)} %bitcast.523), kind=kOutput, calls=%fused_computation.98 | convolution fusion | flops 2159017984 | bytes 17301504 | tf_op jit(solution)/shard_map/gse,gde->gsd/dot_general | solution.py:175
  493.9 5.9 add_add_fusion.6
  499.8 6.1 fusion.162
  526.3 31.6 %while.97 = (s32[]{:T(128)}, f32[1024,4,64]{0,2,1:T(8,128)S(1)}, f32[1024,4,64]{0,2,1:T(8,128)}, bf16[2,512,4,64]{1,3,2,0:T(8,128)(2,1)}, bf16[2,512,4,64]{1,3,2...) while((s32[]{:T(128)}, f32[1024,4,64]{0,2,1:T(8,128)S(1)}, ...), condition=%wide.region_30.31_spmd.clone, body=%wide.region_28.30_spmd.clone.sunk | while | flops 1376124416 | bytes 87095624 | solution.py:103
  602.8 5.9 collective-permute-done.31
  623.0 16.0 %collective-permute-done.35 = bf16[256,1024]{1,0:T(8,128)(2,1)S(1)} collective-permute-done((bf16[256,1024]{1,0:T(8,128)(2,1)S(1)}, bf16[256,1024]{1,0:T(8,128)(2,1)S(1)}, u32[]{:S(2)}, u32[]{:S(2)}) %collective-permute-start.35) | collective-permute-done | bytes 524320 | tf_op jit(solution)/shard_map/ppermute | solution.py:149
  657.4 25.1 %all-reduce.7.cloned.1.call-done = bf16[2099200]{0:T(1024)(128)(2,1)} async-done(((bf16[2099200]{0:T(1024)(128)(2,1)}), bf16[2099200]{0:T(1024)(128)(2,1)}) %all-reduce.7.cloned.1.call-update) | async-done | bytes 4198416 | tf_op jit(solution)/shard_map/psum | solution.py:166
  716.8 9.3 %collective-permute-done.41 = bf16[256,1024]{1,0:T(8,128)(2,1)S(1)} collective-permute-done((bf16[256,1024]{1,0:T(8,128)(2,1)}, bf16[256,1024]{1,0:T(8,128)(2,1)S(1)}, u32[]{:S(2)}, u32[]{:S(2)}) %collective-permute-start.41) | collective-permute-done | bytes 524320 | tf_op jit(solution)/shard_map/ppermute | solution.py:121
  730.5 37.4 %psum.38 = f32[2,1024]{1,0:T(2,128)S(1)} all-reduce(f32[2,1024]{1,0:T(2,128)S(1)} %pad_maximum_fusion.7), channel_id=1, replica_groups=mesh['dp'=8,'tensor'=4] {'dp','tensor'}, use_global_device_ids=true, to_apply=%region_36.37 | all-reduce | flops 2048 | bytes 16384 | tf_op jit(solution)/shard_map/psum | solution.py:344
  (553 shorter events, 476.4 us)
Async XLA Ops:
  7.2 120.8 %all-gather.7.cloned.1.call-start = ((), (), s32[]{:S(2)}) async-start(), calls=%async_computation.2 | async-start | bytes 2621440 | tf_op jit(solution)/shard_map/all_gather | solution.py:218
  8.0 192.0 %all-gather.9.cloned.1.call-start = ((), (), s32[]{:S(2)}) async-start(), calls=%async_computation.3 | async-start | bytes 2621440 | tf_op jit(solution)/shard_map/all_gather | solution.py:219
  47.0 19.1 %collective-permute-start = (bf16[1024,256]{1,0:T(8,128)(2,1)}, bf16[1024,256]{1,0:T(8,128)(2,1)}, u32[]{:S(2)}, u32[]{:S(2)}) collective-permute-start(bf16[1024,256]{1,0:T(8,128)(2,1)} %copy.67), channel_id=1, source_target_pairs={{0,1},{1,2},{2,3},{4,5},{5,6},{6,7},{8,9},{9,10},{10,11},{12,13},{... | collective-permute-start | bytes 1572872 | tf_op jit(solution)/shard_map/ppermute | solution.py:120
  52.8 16.1 %collective-permute-start.1 = (bf16[1024,256]{1,0:T(8,128)(2,1)}, bf16[1024,256]{1,0:T(8,128)(2,1)}, u32[]{:S(2)}, u32[]{:S(2)}) collective-permute-start(bf16[1024,256]{1,0:T(8,128)(2,1)} %copy.67), channel_id=1, source_target_pairs={{1,0},{2,1},{3,2},{5,4},{6,5},{7,6},{9,8},{10,9},{11,10},{13,12},{... | collective-permute-start | bytes 1572872 | tf_op jit(solution)/shard_map/ppermute | solution.py:121
  54.1 417.5 %all-gather.11.cloned.1.call-start = ((), (), s32[]{:S(2)}) async-start(), calls=%async_computation.4 | async-start | bytes 2621440 | tf_op jit(solution)/shard_map/all_gather | solution.py:220
  68.9 39.8 %collective-permute-start.3 = (bf16[1024,256]{1,0:T(8,128)(2,1)}, bf16[1024,256]{1,0:T(8,128)(2,1)S(1)}, u32[]{:S(2)}, u32[]{:S(2)}) collective-permute-start(bf16[1024,256]{1,0:T(8,128)(2,1)} %collective-permute-done.1), channel_id=1, source_target_pairs={{1,0},{2,1},{5,4},{6,5},{9,8},{10,9},{13,12},{14,13},{17,16},{18,1... | collective-permute-start | bytes 1572872 | tf_op jit(solution)/shard_map/ppermute | solution.py:121
  74.5 38.4 %collective-permute-start.4 = (bf16[1024,256]{1,0:T(8,128)(2,1)}, bf16[1024,256]{1,0:T(8,128)(2,1)S(1)}, u32[]{:S(2)}, u32[]{:S(2)}) collective-permute-start(bf16[1024,256]{1,0:T(8,128)(2,1)} %collective-permute-done.2), channel_id=1, source_target_pairs={{2,3},{6,7},{10,11},{14,15},{18,19},{22,23},{26,27},{30,31}} | collective-permute-start | bytes 1572872 | tf_op jit(solution)/shard_map/ppermute | solution.py:120
  108.7 18.5 %collective-permute-start.5 = (bf16[1024,256]{1,0:T(8,128)(2,1)S(1)}, bf16[1024,256]{1,0:T(8,128)(2,1)S(1)}, u32[]{:S(2)}, u32[]{:S(2)}) collective-permute-start(bf16[1024,256]{1,0:T(8,128)(2,1)S(1)} %collective-permute-done.3), channel_id=1, source_target_pairs={{1,0},{5,4},{9,8},{13,12},{17,16},{21,20},{25,24},{29,28}} | collective-permute-start | bytes 1572872 | tf_op jit(solution)/shard_map/ppermute | solution.py:121
  166.1 19.0 %collective-permute-start.9 = (bf16[1024,256]{1,0:T(8,128)(2,1)}, bf16[1024,256]{1,0:T(8,128)(2,1)S(1)}, u32[]{:S(2)}, u32[]{:S(2)}) collective-permute-start(bf16[1024,256]{1,0:T(8,128)(2,1)} %collective-permute-done.7), channel_id=1, source_target_pairs={{1,0},{2,1},{5,4},{6,5},{9,8},{10,9},{13,12},{14,13},{17,16},{18,1... | collective-permute-start | bytes 1572872 | tf_op jit(solution)/shard_map/ppermute | solution.py:121
  171.7 17.8 %collective-permute-start.10 = (bf16[1024,256]{1,0:T(8,128)(2,1)}, bf16[1024,256]{1,0:T(8,128)(2,1)S(1)}, u32[]{:S(2)}, u32[]{:S(2)}) collective-permute-start(bf16[1024,256]{1,0:T(8,128)(2,1)} %collective-permute-done.8), channel_id=1, source_target_pairs={{2,3},{6,7},{10,11},{14,15},{18,19},{22,23},{26,27},{30,31}} | collective-permute-start | bytes 1572872 | tf_op jit(solution)/shard_map/ppermute | solution.py:120
  255.2 244.6 %all-reduce.5.cloned.1.call-start = ((), (), s32[]{:S(2)}) async-start(), calls=%async_computation | async-start | bytes 8396800 | tf_op jit(solution)/shard_map/psum | solution.py:166
  261.5 43.2 %collective-permute-start.17 = (bf16[256,1024]{1,0:T(8,128)(2,1)S(1)}, bf16[256,1024]{1,0:T(8,128)(2,1)S(1)}, u32[]{:S(2)}, u32[]{:S(2)}) collective-permute-start(bf16[256,1024]{1,0:T(8,128)(2,1)S(1)} %fusion.133), channel_id=1, source_target_pairs={{1,0},{2,1},{3,2},{5,4},{6,5},{7,6},{9,8},{10,9},{11,10},{13,12},{... | collective-permute-start | bytes 1572872 | tf_op jit(solution)/shard_map/ppermute | solution.py:149
  319.6 16.3 %collective-permute-start.20 = (bf16[256,1024]{1,0:T(8,128)(2,1)}, bf16[256,1024]{1,0:T(8,128)(2,1)}, u32[]{:S(2)}, u32[]{:S(2)}) collective-permute-start(bf16[256,1024]{1,0:T(8,128)(2,1)} %collective-permute-done.18), channel_id=1, source_target_pairs={{1,2},{2,3},{5,6},{6,7},{9,10},{10,11},{13,14},{14,15},{17,18},{18... | collective-permute-start | bytes 1572872 | tf_op jit(solution)/shard_map/ppermute | solution.py:120
  400.6 247.2 %all-reduce.9.cloned.1.call-start = ((), (), s32[]{:S(2)}) async-start(), calls=%async_computation.5 | async-start | bytes 4718592 | tf_op jit(solution)/shard_map/psum | solution.py:287
  419.5 26.1 %collective-permute-start.25 = (bf16[1024,256]{1,0:T(8,128)(2,1)}, bf16[1024,256]{1,0:T(8,128)(2,1)}, u32[]{:S(2)}, u32[]{:S(2)}) collective-permute-start(bf16[1024,256]{1,0:T(8,128)(2,1)} %copy.81), channel_id=1, source_target_pairs={{1,0},{2,1},{3,2},{5,4},{6,5},{7,6},{9,8},{10,9},{11,10},{13,12},{... | collective-permute-start | bytes 1572872 | tf_op jit(solution)/shard_map/ppermute | solution.py:121
  420.8 19.8 %collective-permute-start.24 = (bf16[1024,256]{1,0:T(8,128)(2,1)}, bf16[1024,256]{1,0:T(8,128)(2,1)}, u32[]{:S(2)}, u32[]{:S(2)}) collective-permute-start(bf16[1024,256]{1,0:T(8,128)(2,1)} %copy.81), channel_id=1, source_target_pairs={{0,1},{1,2},{2,3},{4,5},{5,6},{6,7},{8,9},{9,10},{10,11},{12,13},{... | collective-permute-start | bytes 1572872 | tf_op jit(solution)/shard_map/ppermute | solution.py:120
  440.6 16.3 %collective-permute-start.26 = (bf16[1024,256]{1,0:T(8,128)(2,1)}, bf16[1024,256]{1,0:T(8,128)(2,1)}, u32[]{:S(2)}, u32[]{:S(2)}) collective-permute-start(bf16[1024,256]{1,0:T(8,128)(2,1)} %collective-permute-done.24), channel_id=1, source_target_pairs={{1,2},{2,3},{5,6},{6,7},{9,10},{10,11},{13,14},{14,15},{17,18},{18... | collective-permute-start | bytes 1572872 | tf_op jit(solution)/shard_map/ppermute | solution.py:120
  455.0 227.6 %all-reduce.7.cloned.1.call-start = ((), (), s32[]{:S(2)}) async-start(), calls=%async_computation.1 | async-start | bytes 8396800 | tf_op jit(solution)/shard_map/psum | solution.py:166
  584.9 17.9 %collective-permute-start.33 = (bf16[256,1024]{1,0:T(8,128)(2,1)}, bf16[256,1024]{1,0:T(8,128)(2,1)S(1)}, u32[]{:S(2)}, u32[]{:S(2)}) collective-permute-start(bf16[256,1024]{1,0:T(8,128)(2,1)} %get-tuple-element.594), channel_id=1, source_target_pairs={{3,2},{7,6},{11,10},{15,14},{19,18},{23,22},{27,26},{31,30}} | collective-permute-start | bytes 1572872 | tf_op jit(solution)/shard_map/ppermute | solution.py:149
  617.6 21.4 %collective-permute-start.35 = (bf16[256,1024]{1,0:T(8,128)(2,1)S(1)}, bf16[256,1024]{1,0:T(8,128)(2,1)S(1)}, u32[]{:S(2)}, u32[]{:S(2)}) collective-permute-start(bf16[256,1024]{1,0:T(8,128)(2,1)S(1)} %fusion.127), channel_id=1, source_target_pairs={{1,0},{2,1},{3,2},{5,4},{6,5},{7,6},{9,8},{10,9},{11,10},{13,12},{... | collective-permute-start | bytes 1572872 | tf_op jit(solution)/shard_map/ppermute | solution.py:149
  654.6 30.9 %collective-permute-start.37 = (bf16[256,1024]{1,0:T(8,128)(2,1)}, bf16[256,1024]{1,0:T(8,128)(2,1)}, u32[]{:S(2)}, u32[]{:S(2)}) collective-permute-start(bf16[256,1024]{1,0:T(8,128)(2,1)} %get-tuple-element.559), channel_id=1, source_target_pairs={{1,0},{2,1},{3,2},{5,4},{6,5},{7,6},{9,8},{10,9},{11,10},{13,12},{... | collective-permute-start | bytes 1572872 | tf_op jit(solution)/shard_map/ppermute | solution.py:121
  655.9 51.9 %collective-permute-start.38 = (bf16[256,1024]{1,0:T(8,128)(2,1)}, bf16[256,1024]{1,0:T(8,128)(2,1)}, u32[]{:S(2)}, u32[]{:S(2)}) collective-permute-start(bf16[256,1024]{1,0:T(8,128)(2,1)} %collective-permute-done.36), channel_id=1, source_target_pairs={{1,2},{2,3},{5,6},{6,7},{9,10},{10,11},{13,14},{14,15},{17,18},{18... | collective-permute-start | bytes 1572872 | tf_op jit(solution)/shard_map/ppermute | solution.py:120
  685.6 24.9 %collective-permute-start.39 = (bf16[256,1024]{1,0:T(8,128)(2,1)}, bf16[256,1024]{1,0:T(8,128)(2,1)}, u32[]{:S(2)}, u32[]{:S(2)}) collective-permute-start(bf16[256,1024]{1,0:T(8,128)(2,1)} %collective-permute-done.37), channel_id=1, source_target_pairs={{1,0},{2,1},{5,4},{6,5},{9,8},{10,9},{13,12},{14,13},{17,16},{18,1... | collective-permute-start | bytes 1572872 | tf_op jit(solution)/shard_map/ppermute | solution.py:121
  710.5 15.7 %collective-permute-start.41 = (bf16[256,1024]{1,0:T(8,128)(2,1)}, bf16[256,1024]{1,0:T(8,128)(2,1)S(1)}, u32[]{:S(2)}, u32[]{:S(2)}) collective-permute-start(bf16[256,1024]{1,0:T(8,128)(2,1)} %collective-permute-done.39), channel_id=1, source_target_pairs={{1,0},{5,4},{9,8},{13,12},{17,16},{21,20},{25,24},{29,28}} | collective-permute-start | bytes 1572872 | tf_op jit(solution)/shard_map/ppermute | solution.py:121
  (133 other events, 1348.0 us)
Sparse Core Ops, SparseCore 0:
  9.6 48.6 all-gather.6
  59.9 56.3 all-gather.8
  255.3 59.4 all-gather.10
  400.7 81.0 all-reduce.4
  484.7 94.6 all-reduce.8
  602.9 79.5 all-reduce.6

commit v5 on v4

--- a/solution.py
+++ b/solution.py
@@ -161,14 +161,17 @@
     return relay_gather(reduced, "tensor").reshape(low_value.shape).astype(jnp.float32)
 
 
-def flat_psum(terms, axis):
-    flat = jnp.concatenate([term.astype(jnp.bfloat16).reshape(-1) for term in terms])
-    flat = lax.psum(flat, axis).astype(jnp.float32)
-    out, start = [], 0
-    for term in terms:
-        out.append(flat[start : start + term.size].reshape(term.shape))
-        start += term.size
-    return out
+def stacked_psum(matrix, rows, axis):
+    pad = (-(matrix.shape[0] + len(rows))) % 16
+    extra = jnp.stack(rows + [jnp.zeros_like(rows[0])] * pad)
+    summed = lax.psum(jnp.concatenate([matrix, extra]).astype(jnp.bfloat16), axis)
+    summed = summed.astype(jnp.float32)
+    count = matrix.shape[0]
+    return [summed[:count]] + [summed[count + i] for i in range(len(rows))]
+
+
+def dp_sum(term):
+    return lax.psum(term.astype(jnp.bfloat16), "dp").astype(jnp.float32)
 
 
 def gathered_sum(pieces, weights, spec):
@@ -255,7 +258,10 @@
         "sk,dk->sd", upward_grad, feed_up, preferred_element_type=jnp.float32
     )
     feed_back = norm_back(after_cross, feed_gain, feed_bias, relay_total(feed_input_part))
-    feed_sums = flat_psum((up_grad, downward_gradient, feed_back[1], feed_back[2]), "dp")
+    feed_sums = [dp_sum(up_grad)] + stacked_psum(
+        downward_gradient, [feed_back[1], feed_back[2]], "dp"
+    )
+    feed_sums = [feed_sums[0], feed_sums[1], feed_sums[2], feed_sums[3]]
     cross_grad_rows = out_grad.astype(jnp.float32) + feed_back[0]
     cross_grad_low = cross_grad_rows.astype(jnp.bfloat16)
     cout_grad = jnp.einsum(
@@ -340,11 +346,7 @@
         "cse,cde->sd", projection_gradient, self_qkv, preferred_element_type=jnp.float32
     )
     self_back = norm_back(inputs, self_gain, self_bias, relay_total(self_input_part))
-    own_part = self_input_part.astype(jnp.bfloat16).astype(jnp.float32)
-    self_norm_terms = lax.psum(
-        jnp.stack((jnp.sum(own_part * normalized(inputs), axis=0), jnp.sum(own_part, axis=0))),
-        ("dp", "tensor"),
-    )
+    self_norm_terms = (dp_sum(self_back[1]), dp_sum(self_back[2]))
     frames_grad = self_grad_rows + self_back[0]
     gain_terms = (
         self_back[1],
@@ -354,10 +356,8 @@
         feed_back[1],
         feed_back[2],
     )
-    late_sums = flat_psum(
-        (qkv_grad, sout_grad, cquery_grad, ckeyval_grad, cout_grad, cross_back[1], cross_back[2]),
-        "dp",
-    )
+    late_sums = [dp_sum(term) for term in (qkv_grad, sout_grad, cquery_grad, ckeyval_grad)]
+    late_sums = late_sums + stacked_psum(cout_grad, [cross_back[1], cross_back[2]], "dp")
     summed = (
         self_norm_terms[0],
         self_norm_terms[1],

time: 797 us -> 751 us (0.942)
  waiting for transfers between devices: 214 us -> 277 us
  local copies, waits for them, and re-layouts: 186 us -> 140 us
  blocking collectives: 37.4 us -> 11.9 us
  other arithmetic: 128 us -> 103 us
  matrix products: 118 us -> 108 us
    psum x1, blocking collectives: 37.4 us -> 11.9 us  [dp_sum(): return lax.psum(term.astype(jnp.bfloat16), 'dp').astype(jnp.float32)]
    slice x12 -> x4, local copies, waits for them, and re-layouts: 32.3 us -> 9.13 us  [stacked_psum(): return [summed[:count]] + [summed[count + i] for i in range(len(rows))]]
    ppermute x15, waiting for transfers between devices: 92.1 us -> 115 us  [relay_gather(): lax.ppermute(from_right, axis, [(i, i - 1) for i in range(1, count - k +...]
    ppermute x6, waiting for transfers between devices: 30.9 us -> 51.1 us  [relay_scatter(): lax.ppermute(send_right.astype(value.dtype), axis, [(i, i + 1) for i in r...]
    concatenate x1 -> x0, other arithmetic: 20.1 us -> none  [flat_psum(): jnp.concatenate([term.astype(jnp.bfloat16).reshape(-1) for term in terms])]
    psum x2, waiting for transfers between devices: 25.1 us -> 41 us  [stacked_psum(): lax.psum(jnp.concatenate([matrix, extra]).astype(jnp.bfloat16), axis)]
    concatenate x1 -> x2, local copies, waits for them, and re-layouts: 0.59 us -> 12.6 us  [stacked_psum(): jnp.concatenate([matrix, extra]).astype(jnp.bfloat16)]
    unnamed x194 -> x227, local copies, waits for them, and re-layouts: 34.1 us -> 22.7 us
  transfers between devices with their start and end apart: 48 -> 48, of which waited for: 22 -> 27; matrix products, arithmetic and copies ran while one was open for 48% -> 40% of each run, Pallas kernels for 0% -> 0%
where the time goes in v5:
time: 751 us; the launch traced here: 740 us
  waiting for transfers between devices  277 us (37%)
  local copies, waits for them, and re-layouts  140 us (19%)
  matrix products  108 us (14%)
  other arithmetic  103 us (14%)
  starting transfers between devices  82.6 us (11%)
  between operations  16.1 us (2%)
  blocking collectives  11.9 us (2%)
    ppermute x15, waiting for transfers between devices, relay_gather(): lax.ppermute(from_right, axis, [(i, i - 1) for i in range(1, count - k +...  115 us
    ppermute x6, waiting for transfers between devices, relay_scatter(): lax.ppermute(send_right.astype(value.dtype), axis, [(i, i + 1) for i in r...  51.1 us
    ppermute x6, waiting for transfers between devices, relay_scatter(): lax.ppermute(send_left.astype(value.dtype), axis, [(i, i - 1) for i in ra...  42.8 us
    psum x2, waiting for transfers between devices, stacked_psum(): lax.psum(jnp.concatenate([matrix, extra]).astype(jnp.bfloat16), axis)  41 us
    ppermute x15, starting transfers between devices, relay_gather(): lax.ppermute(from_left, axis, [(i, i + 1) for i in range(k - 1, count - 1)])  30.7 us
    ppermute x15, waiting for transfers between devices, relay_gather(): lax.ppermute(from_left, axis, [(i, i + 1) for i in range(k - 1, count - 1)])  25.6 us
    ppermute x6, starting transfers between devices, relay_scatter(): lax.ppermute(send_right.astype(value.dtype), axis, [(i, i + 1) for i in r...  24.3 us
    unnamed x227, local copies, waits for them, and re-layouts  22.7 us
  transfers between devices with their start and end apart: 48, of which 27 were waited for; matrix products, arithmetic and copies ran while one was open for 40% of the time, Pallas kernels for 0%

profile of v5, /device:TPU:0, one launch (start us, length us, event | category | flops | bytes accessed | tf_op | source)
XLA Modules:
  0.0 740.1 jit_solution(2164478538771001049)
XLA Ops:
  20.4 21.6 %while.94 = (s32[]{:T(128)}, bf16[2,512,4,64]{1,3,2,0:T(8,128)(2,1)}, f32[2,4,512]{2,1,0:T(4,128)}, s32[]{:T(128)}, s32[2]{0:T(128)}, /*index=5*/bf16[2,512,4,64...) while((s32[]{:T(128)}, ...), condition=%wide.region_5.6_spmd, body=%wide.region_2.5_spmd.sunk | while | flops 563215872 | bytes 35199192 | solution.py:64
  77.1 31.6 %collective-permute-done.3 = bf16[1024,256]{1,0:T(8,128)(2,1)S(1)} collective-permute-done((bf16[1024,256]{1,0:T(8,128)(2,1)}, bf16[1024,256]{1,0:T(8,128)(2,1)S(1)}, u32[]{:S(2)}, u32[]{:S(2)}) %collective-permute-start.3) | collective-permute-done | bytes 524320 | tf_op jit(solution)/shard_map/ppermute | solution.py:121
  113.7 13.5 %collective-permute-done.5 = bf16[1024,256]{1,0:T(8,128)(2,1)S(1)} collective-permute-done((bf16[1024,256]{1,0:T(8,128)(2,1)S(1)}, bf16[1024,256]{1,0:T(8,128)(2,1)S(1)}, u32[]{:S(2)}, u32[]{:S(2)}) %collective-permute-start.5) | collective-permute-done | bytes 524320 | tf_op jit(solution)/shard_map/ppermute | solution.py:121
  152.3 8.7 %collective-permute-done.6 = bf16[1024,256]{1,0:T(8,128)(2,1)} collective-permute-done((bf16[1024,256]{1,0:T(8,128)(2,1)}, bf16[1024,256]{1,0:T(8,128)(2,1)}, u32[]{:S(2)}, u32[]{:S(2)}) %collective-permute-start.6) | collective-permute-done | bytes 524320 | tf_op jit(solution)/shard_map/ppermute | solution.py:120
  174.2 10.8 %collective-permute-done.9 = bf16[1024,256]{1,0:T(8,128)(2,1)S(1)} collective-permute-done((bf16[1024,256]{1,0:T(8,128)(2,1)}, bf16[1024,256]{1,0:T(8,128)(2,1)S(1)}, u32[]{:S(2)}, u32[]{:S(2)}) %collective-permute-start.9) | collective-permute-done | bytes 524320 | tf_op jit(solution)/shard_map/ppermute | solution.py:121
  190.0 9.1 %collective-permute-done.11 = bf16[1024,256]{1,0:T(8,128)(2,1)S(1)} collective-permute-done((bf16[1024,256]{1,0:T(8,128)(2,1)S(1)}, bf16[1024,256]{1,0:T(8,128)(2,1)S(1)}, u32[]{:S(2)}, u32[]{:S(2)}) %collective-permute-start.11) | collective-permute-done | bytes 524320 | tf_op jit(solution)/shard_map/ppermute | solution.py:121
  207.7 12.7 %multiply_convert_fusion.2 = (bf16[1024,1024]{1,0:T(8,128)(2,1)}, f32[1024,1024]{1,0:T(8,128)S(1)}, f32[1024,1024]{1,0:T(8,128)S(1)}) fusion(bf16[1024,1024]{1,0:T(8,128)(2,1)S(1)} %copy-done, f32[1024,1024]{1,0:T(8,128)S(1)} %get-tuple-element.609, f32[1024]{0:T(1024)S(1)} %copy-done.113, f32[1024]{0:T(1024)S(1)} %copy-done.87, f32[1024]{0:T(1024)S(1)} %fusion.148, ...), kind=kOutput, calls=%fused_computation.146 | convolution fusion | flops 2220883968 | bytes 16793600 | tf_op jit(solution)/shard_map/dot_general | solution.py:246
  230.5 7.8 %collective-permute-done.12 = bf16[256,1024]{1,0:T(8,128)(2,1)S(1)} collective-permute-done((bf16[256,1024]{1,0:T(8,128)(2,1)S(1)}, bf16[256,1024]{1,0:T(8,128)(2,1)S(1)}, u32[]{:S(2)}, u32[]{:S(2)}) %collective-permute-start.12) | collective-permute-done | bytes 524320 | tf_op jit(solution)/shard_map/ppermute | solution.py:146
  244.0 8.0 %collective-permute-done.13 = bf16[256,1024]{1,0:T(8,128)(2,1)S(1)} collective-permute-done((bf16[256,1024]{1,0:T(8,128)(2,1)S(1)}, bf16[256,1024]{1,0:T(8,128)(2,1)S(1)}, u32[]{:S(2)}, u32[]{:S(2)}) %collective-permute-start.13) | collective-permute-done | bytes 524320 | tf_op jit(solution)/shard_map/ppermute | solution.py:146
  262.8 7.2 convolution_convert_fusion.2
  270.5 34.5 %collective-permute-done.17 = bf16[256,1024]{1,0:T(8,128)(2,1)S(1)} collective-permute-done((bf16[256,1024]{1,0:T(8,128)(2,1)S(1)}, bf16[256,1024]{1,0:T(8,128)(2,1)S(1)}, u32[]{:S(2)}, u32[]{:S(2)}) %collective-permute-start.17) | collective-permute-done | bytes 524320 | tf_op jit(solution)/shard_map/ppermute | solution.py:149
  357.7 6.5 fusion.76
  378.7 8.1 %concatenate.18 = bf16[1040,1024]{1,0:T(8,128)(2,1)} concatenate(bf16[1024,1024]{1,0:T(8,128)(2,1)S(1)} %copy-done.43, bf16[1,1024]{1,0:T(2,128)(2,1)} %reshape.613, bf16[1,1024]{1,0:T(2,128)(2,1)} %reshape.614, bf16[2,1024]{1,0:T(2,128)(2,1)} %broadcast.516, bf16[4,1024]{1,0:T(4,128)(2,1)} %broadcast.517, bf16[8,1024]{1,0:T(8,128)(2,1)} %broadcast.518), dimensions={0} | concatenate | bytes 4259840 | tf_op jit(solution)/shard_map/concatenate | solution.py:167
  387.7 6.9 while.96
  421.7 9.5 %collective-permute-done.27 = bf16[1024,256]{1,0:T(8,128)(2,1)S(1)} collective-permute-done((bf16[1024,256]{1,0:T(8,128)(2,1)}, bf16[1024,256]{1,0:T(8,128)(2,1)S(1)}, u32[]{:S(2)}, u32[]{:S(2)}) %collective-permute-start.27) | collective-permute-done | bytes 524320 | tf_op jit(solution)/shard_map/ppermute | solution.py:121
  443.1 10.5 %convert_reduce_fusion = (f32[1024,1024]{1,0:T(8,128)}, bf16[4,1024,1024]{2,1,0:T(8,128)(2,1)}) fusion(bf16[5,1024,256]{2,1,0:T(8,128)(2,1)} %bitcast_dynamic-update-slice_fusion.9, bf16[4,1024,256]{2,1,0:T(8,128)(2,1)} %bitcast.500), kind=kOutput, calls=%fused_computation.98 | convolution fusion | flops 2159017984 | bytes 17301504 | tf_op jit(solution)/shard_map/gse,gde->gsd/dot_general | solution.py:178
  480.9 31.5 %while.97 = (s32[]{:T(128)}, f32[1024,4,64]{0,2,1:T(8,128)S(1)}, f32[1024,4,64]{0,2,1:T(8,128)}, bf16[2,512,4,64]{1,3,2,0:T(8,128)(2,1)}, bf16[2,512,4,64]{1,3,2...) while((s32[]{:T(128)}, f32[1024,4,64]{0,2,1:T(8,128)S(1)}, ...), condition=%wide.region_31.32_spmd.clone, body=%wide.region_29.31_spmd.clone.sunk | while | flops 1376124416 | bytes 84998440 | solution.py:103
  531.2 17.7 %collective-permute-done.30 = bf16[256,1024]{1,0:T(8,128)(2,1)S(1)} collective-permute-done((bf16[256,1024]{1,0:T(8,128)(2,1)S(1)}, bf16[256,1024]{1,0:T(8,128)(2,1)S(1)}, u32[]{:S(2)}, u32[]{:S(2)}) %collective-permute-start.30) | collective-permute-done | bytes 524320 | tf_op jit(solution)/shard_map/ppermute | solution.py:146
  567.2 10.3 %collective-permute-done.31 = bf16[256,1024]{1,0:T(8,128)(2,1)} collective-permute-done((bf16[256,1024]{1,0:T(8,128)(2,1)}, bf16[256,1024]{1,0:T(8,128)(2,1)}, u32[]{:S(2)}, u32[]{:S(2)}) %collective-permute-start.31) | collective-permute-done | bytes 524320 | tf_op jit(solution)/shard_map/ppermute | solution.py:146
  595.0 6.9 collective-permute-done.32
  601.9 8.3 %collective-permute-done.35 = bf16[256,1024]{1,0:T(8,128)(2,1)S(1)} collective-permute-done((bf16[256,1024]{1,0:T(8,128)(2,1)S(1)}, bf16[256,1024]{1,0:T(8,128)(2,1)S(1)}, u32[]{:S(2)}, u32[]{:S(2)}) %collective-permute-start.35) | collective-permute-done | bytes 524320 | tf_op jit(solution)/shard_map/ppermute | solution.py:149
  636.0 36.1 %all-reduce.8.cloned.1.call-done = (bf16[272,1024]{1,0:T(8,128)(2,1)}, bf16[3,1024,256]{1,2,0:T(8,128)(2,1)}, bf16[2,1024,256]{1,2,0:T(8,128)(2,1)}, bf16[256,1024]{1,0:T(8,128)(2,1)}, bf16[1024,256]{1,0:T(8,128)(2,1)}) async-done(((bf16[272,1024]{1,0:T(8,128)(2,1)}, bf16[3,1024,256]{1,2,0:T(8,128)(2,1)}, bf16[2,1024,256]{1,2,0:T(8,128)(2,1)}, bf16[256,1024]{1,0:T(8,128)(2,1)}, ...) | async-done | bytes 4227088 | tf_op jit(solution)/shard_map/psum | solution.py:167
  694.9 9.8 %collective-permute-done.41 = bf16[256,1024]{1,0:T(8,128)(2,1)S(1)} collective-permute-done((bf16[256,1024]{1,0:T(8,128)(2,1)}, bf16[256,1024]{1,0:T(8,128)(2,1)S(1)}, u32[]{:S(2)}, u32[]{:S(2)}) %collective-permute-start.41) | collective-permute-done | bytes 524320 | tf_op jit(solution)/shard_map/ppermute | solution.py:121
  711.0 11.9 %all-reduce = (bf16[1024]{0:T(1024)(128)(2,1)S(1)}, bf16[1024]{0:T(1024)(128)(2,1)S(1)}) all-reduce(bf16[1024]{0:T(1024)(128)(2,1)S(1)} %get-tuple-element.513, bf16[1024]{0:T(1024)(128)(2,1)S(1)} %slice_reduce_fusion), channel_id=1, replica_groups=mesh['dp'=8,'tensor'=4] {'dp'}, use_global_device_ids=true, to_apply=%region_36.37 | all-reduce | flops 2048 | bytes 8192 | tf_op jit(solution)/shard_map/psum | solution.py:174
  (578 shorter events, 446.7 us)
Async XLA Ops:
  7.2 120.8 %all-gather.7.cloned.1.call-start = ((), (), s32[]{:S(2)}) async-start(), calls=%async_computation | async-start | bytes 2621440 | tf_op jit(solution)/shard_map/all_gather | solution.py:221
  8.0 192.0 %all-gather.9.cloned.1.call-start = ((), (), s32[]{:S(2)}) async-start(), calls=%async_computation.1 | async-start | bytes 2621440 | tf_op jit(solution)/shard_map/all_gather | solution.py:222
  47.0 19.1 %collective-permute-start = (bf16[1024,256]{1,0:T(8,128)(2,1)}, bf16[1024,256]{1,0:T(8,128)(2,1)}, u32[]{:S(2)}, u32[]{:S(2)}) collective-permute-start(bf16[1024,256]{1,0:T(8,128)(2,1)} %copy.69), channel_id=1, source_target_pairs={{0,1},{1,2},{2,3},{4,5},{5,6},{6,7},{8,9},{9,10},{10,11},{12,13},{... | collective-permute-start | bytes 1572872 | tf_op jit(solution)/shard_map/ppermute | solution.py:120
  52.7 16.1 %collective-permute-start.1 = (bf16[1024,256]{1,0:T(8,128)(2,1)}, bf16[1024,256]{1,0:T(8,128)(2,1)}, u32[]{:S(2)}, u32[]{:S(2)}) collective-permute-start(bf16[1024,256]{1,0:T(8,128)(2,1)} %copy.69), channel_id=1, source_target_pairs={{1,0},{2,1},{3,2},{5,4},{6,5},{7,6},{9,8},{10,9},{11,10},{13,12},{... | collective-permute-start | bytes 1572872 | tf_op jit(solution)/shard_map/ppermute | solution.py:121
  54.1 389.0 %all-gather.11.cloned.1.call-start = ((), (), s32[]{:S(2)}) async-start(), calls=%async_computation.2 | async-start | bytes 2621440 | tf_op jit(solution)/shard_map/all_gather | solution.py:223
  68.9 39.8 %collective-permute-start.3 = (bf16[1024,256]{1,0:T(8,128)(2,1)}, bf16[1024,256]{1,0:T(8,128)(2,1)S(1)}, u32[]{:S(2)}, u32[]{:S(2)}) collective-permute-start(bf16[1024,256]{1,0:T(8,128)(2,1)} %collective-permute-done.1), channel_id=1, source_target_pairs={{1,0},{2,1},{5,4},{6,5},{9,8},{10,9},{13,12},{14,13},{17,16},{18,1... | collective-permute-start | bytes 1572872 | tf_op jit(solution)/shard_map/ppermute | solution.py:121
  74.5 38.3 %collective-permute-start.4 = (bf16[1024,256]{1,0:T(8,128)(2,1)}, bf16[1024,256]{1,0:T(8,128)(2,1)S(1)}, u32[]{:S(2)}, u32[]{:S(2)}) collective-permute-start(bf16[1024,256]{1,0:T(8,128)(2,1)} %collective-permute-done.2), channel_id=1, source_target_pairs={{2,3},{6,7},{10,11},{14,15},{18,19},{22,23},{26,27},{30,31}} | collective-permute-start | bytes 1572872 | tf_op jit(solution)/shard_map/ppermute | solution.py:120
  108.7 18.5 %collective-permute-start.5 = (bf16[1024,256]{1,0:T(8,128)(2,1)S(1)}, bf16[1024,256]{1,0:T(8,128)(2,1)S(1)}, u32[]{:S(2)}, u32[]{:S(2)}) collective-permute-start(bf16[1024,256]{1,0:T(8,128)(2,1)S(1)} %collective-permute-done.3), channel_id=1, source_target_pairs={{1,0},{5,4},{9,8},{13,12},{17,16},{21,20},{25,24},{29,28}} | collective-permute-start | bytes 1572872 | tf_op jit(solution)/shard_map/ppermute | solution.py:121
  166.0 19.0 %collective-permute-start.9 = (bf16[1024,256]{1,0:T(8,128)(2,1)}, bf16[1024,256]{1,0:T(8,128)(2,1)S(1)}, u32[]{:S(2)}, u32[]{:S(2)}) collective-permute-start(bf16[1024,256]{1,0:T(8,128)(2,1)} %collective-permute-done.7), channel_id=1, source_target_pairs={{1,0},{2,1},{5,4},{6,5},{9,8},{10,9},{13,12},{14,13},{17,16},{18,1... | collective-permute-start | bytes 1572872 | tf_op jit(solution)/shard_map/ppermute | solution.py:121
  171.6 17.6 %collective-permute-start.10 = (bf16[1024,256]{1,0:T(8,128)(2,1)}, bf16[1024,256]{1,0:T(8,128)(2,1)S(1)}, u32[]{:S(2)}, u32[]{:S(2)}) collective-permute-start(bf16[1024,256]{1,0:T(8,128)(2,1)} %collective-permute-done.8), channel_id=1, source_target_pairs={{2,3},{6,7},{10,11},{14,15},{18,19},{22,23},{26,27},{30,31}} | collective-permute-start | bytes 1572872 | tf_op jit(solution)/shard_map/ppermute | solution.py:120
  255.1 211.6 %all-reduce.10.cloned.1.call-start = ((), (), s32[]{:S(2)}) async-start(), calls=%async_computation.4 | async-start | bytes 8454144 | tf_op jit(solution)/shard_map/psum | solution.py:167
  261.5 43.5 %collective-permute-start.17 = (bf16[256,1024]{1,0:T(8,128)(2,1)S(1)}, bf16[256,1024]{1,0:T(8,128)(2,1)S(1)}, u32[]{:S(2)}, u32[]{:S(2)}) collective-permute-start(bf16[256,1024]{1,0:T(8,128)(2,1)S(1)} %fusion.133), channel_id=1, source_target_pairs={{1,0},{2,1},{3,2},{5,4},{6,5},{7,6},{9,8},{10,9},{11,10},{13,12},{... | collective-permute-start | bytes 1572872 | tf_op jit(solution)/shard_map/ppermute | solution.py:149
  325.6 16.0 %collective-permute-start.21 = (bf16[256,1024]{1,0:T(8,128)(2,1)}, bf16[256,1024]{1,0:T(8,128)(2,1)}, u32[]{:S(2)}, u32[]{:S(2)}) collective-permute-start(bf16[256,1024]{1,0:T(8,128)(2,1)} %collective-permute-done.19), channel_id=1, source_target_pairs={{1,0},{2,1},{5,4},{6,5},{9,8},{10,9},{13,12},{14,13},{17,16},{18,1... | collective-permute-start | bytes 1572872 | tf_op jit(solution)/shard_map/ppermute | solution.py:121
  386.8 241.9 %all-reduce.12.cloned.1.call-start = ((), (), s32[]{:S(2)}) async-start(), calls=%async_computation.5 | async-start | bytes 4718592 | tf_op jit(solution)/shard_map/psum | solution.py:293
  398.9 15.8 %collective-permute-start.25 = (bf16[1024,256]{1,0:T(8,128)(2,1)S(1)}, bf16[1024,256]{1,0:T(8,128)(2,1)}, u32[]{:S(2)}, u32[]{:S(2)}) collective-permute-start(bf16[1024,256]{1,0:T(8,128)(2,1)S(1)} %copy.83), channel_id=1, source_target_pairs={{1,0},{2,1},{3,2},{5,4},{6,5},{7,6},{9,8},{10,9},{11,10},{13,12},{... | collective-permute-start | bytes 1572872 | tf_op jit(solution)/shard_map/ppermute | solution.py:121
  414.7 16.5 %collective-permute-start.27 = (bf16[1024,256]{1,0:T(8,128)(2,1)}, bf16[1024,256]{1,0:T(8,128)(2,1)S(1)}, u32[]{:S(2)}, u32[]{:S(2)}) collective-permute-start(bf16[1024,256]{1,0:T(8,128)(2,1)} %collective-permute-done.25), channel_id=1, source_target_pairs={{1,0},{2,1},{5,4},{6,5},{9,8},{10,9},{13,12},{14,13},{17,16},{18,1... | collective-permute-start | bytes 1572872 | tf_op jit(solution)/shard_map/ppermute | solution.py:121
  417.2 254.9 %all-reduce.8.cloned.1.call-start = ((), (), s32[]{:S(2)}) async-start(), calls=%async_computation.3 | async-start | bytes 8454144 | tf_op jit(solution)/shard_map/psum | solution.py:167
  419.1 16.3 %collective-permute-start.28 = (bf16[1024,256]{1,0:T(8,128)(2,1)}, bf16[1024,256]{1,0:T(8,128)(2,1)S(1)}, u32[]{:S(2)}, u32[]{:S(2)}) collective-permute-start(bf16[1024,256]{1,0:T(8,128)(2,1)} %collective-permute-done.26), channel_id=1, source_target_pairs={{2,3},{6,7},{10,11},{14,15},{18,19},{22,23},{26,27},{30,31}} | collective-permute-start | bytes 1572872 | tf_op jit(solution)/shard_map/ppermute | solution.py:120
  521.9 26.9 %collective-permute-start.30 = (bf16[256,1024]{1,0:T(8,128)(2,1)S(1)}, bf16[256,1024]{1,0:T(8,128)(2,1)S(1)}, u32[]{:S(2)}, u32[]{:S(2)}) collective-permute-start(bf16[256,1024]{1,0:T(8,128)(2,1)S(1)} %get-tuple-element.626), channel_id=1, source_target_pairs={{0,1},{4,5},{8,9},{12,13},{16,17},{20,21},{24,25},{28,29}} | collective-permute-start | bytes 1572872 | tf_op jit(solution)/shard_map/ppermute | solution.py:146
  529.8 37.5 %collective-permute-start.33 = (bf16[256,1024]{1,0:T(8,128)(2,1)}, bf16[256,1024]{1,0:T(8,128)(2,1)}, u32[]{:S(2)}, u32[]{:S(2)}) collective-permute-start(bf16[256,1024]{1,0:T(8,128)(2,1)} %get-tuple-element.627), channel_id=1, source_target_pairs={{3,2},{7,6},{11,10},{15,14},{19,18},{23,22},{27,26},{31,30}} | collective-permute-start | bytes 1572872 | tf_op jit(solution)/shard_map/ppermute | solution.py:149
  549.8 27.6 %collective-permute-start.31 = (bf16[256,1024]{1,0:T(8,128)(2,1)}, bf16[256,1024]{1,0:T(8,128)(2,1)}, u32[]{:S(2)}, u32[]{:S(2)}) collective-permute-start(bf16[256,1024]{1,0:T(8,128)(2,1)} %fusion.128), channel_id=1, source_target_pairs={{0,1},{1,2},{4,5},{5,6},{8,9},{9,10},{12,13},{13,14},{16,17},{17,1... | collective-permute-start | bytes 1572872 | tf_op jit(solution)/shard_map/ppermute | solution.py:146
  593.7 16.5 %collective-permute-start.35 = (bf16[256,1024]{1,0:T(8,128)(2,1)S(1)}, bf16[256,1024]{1,0:T(8,128)(2,1)S(1)}, u32[]{:S(2)}, u32[]{:S(2)}) collective-permute-start(bf16[256,1024]{1,0:T(8,128)(2,1)S(1)} %fusion.127), channel_id=1, source_target_pairs={{1,0},{2,1},{3,2},{5,4},{6,5},{7,6},{9,8},{10,9},{11,10},{13,12},{... | collective-permute-start | bytes 1572872 | tf_op jit(solution)/shard_map/ppermute | solution.py:149
  627.0 59.4 %collective-permute-start.38 = (bf16[256,1024]{1,0:T(8,128)(2,1)}, bf16[256,1024]{1,0:T(8,128)(2,1)}, u32[]{:S(2)}, u32[]{:S(2)}) collective-permute-start(bf16[256,1024]{1,0:T(8,128)(2,1)} %collective-permute-done.36), channel_id=1, source_target_pairs={{1,2},{2,3},{5,6},{6,7},{9,10},{10,11},{13,14},{14,15},{17,18},{18... | collective-permute-start | bytes 1572872 | tf_op jit(solution)/shard_map/ppermute | solution.py:120
  634.7 54.4 %collective-permute-start.39 = (bf16[256,1024]{1,0:T(8,128)(2,1)}, bf16[256,1024]{1,0:T(8,128)(2,1)}, u32[]{:S(2)}, u32[]{:S(2)}) collective-permute-start(bf16[256,1024]{1,0:T(8,128)(2,1)} %collective-permute-done.37), channel_id=1, source_target_pairs={{1,0},{2,1},{5,4},{6,5},{9,8},{10,9},{13,12},{14,13},{17,16},{18,1... | collective-permute-start | bytes 1572872 | tf_op jit(solution)/shard_map/ppermute | solution.py:121
  (151 other events, 1629.9 us)
Sparse Core Ops, SparseCore 0:
  9.6 48.6 all-gather.6
  59.9 56.3 all-gather.8
  255.3 59.4 all-gather.10
  386.9 79.8 all-reduce.9
  469.6 113.7 all-reduce.11
  588.1 83.9 all-reduce.7

commit v6 on v5

--- a/solution.py
+++ b/solution.py
@@ -243,6 +243,7 @@
     cross_pieces = relay_gather(cross_flat, "tensor")
     after_cross = after_self + gathered_sum(cross_pieces, cross_out_all, "gsk,gkd->gsd")
     normed_feed = layer_norm(after_cross, feed_gain, feed_bias).astype(jnp.bfloat16)
+    cross_query_all, normed_feed = lax.optimization_barrier((cross_query_all, normed_feed))
     upward = jnp.dot(normed_feed, feed_up, preferred_element_type=jnp.float32)
     active = gelu_exact(upward).astype(jnp.bfloat16)
     feed_part = jnp.dot(active, feed_down, preferred_element_type=jnp.float32)
@@ -254,14 +255,11 @@
         "sk,sd->kd", active, out_grad, preferred_element_type=jnp.float32
     )
     up_grad = jnp.einsum("sd,sk->dk", normed_feed, upward_grad, preferred_element_type=jnp.float32)
+    feed_sums = [dp_sum(up_grad), dp_sum(downward_gradient)]
     feed_input_part = jnp.einsum(
         "sk,dk->sd", upward_grad, feed_up, preferred_element_type=jnp.float32
     )
     feed_back = norm_back(after_cross, feed_gain, feed_bias, relay_total(feed_input_part))
-    feed_sums = [dp_sum(up_grad)] + stacked_psum(
-        downward_gradient, [feed_back[1], feed_back[2]], "dp"
-    )
-    feed_sums = [feed_sums[0], feed_sums[1], feed_sums[2], feed_sums[3]]
     cross_grad_rows = out_grad.astype(jnp.float32) + feed_back[0]
     cross_grad_low = cross_grad_rows.astype(jnp.bfloat16)
     cout_grad = jnp.einsum(
@@ -357,14 +355,16 @@
         feed_back[2],
     )
     late_sums = [dp_sum(term) for term in (qkv_grad, sout_grad, cquery_grad, ckeyval_grad)]
-    late_sums = late_sums + stacked_psum(cout_grad, [cross_back[1], cross_back[2]], "dp")
+    late_sums = late_sums + stacked_psum(
+        cout_grad, [cross_back[1], cross_back[2], feed_back[1], feed_back[2]], "dp"
+    )
     summed = (
         self_norm_terms[0],
         self_norm_terms[1],
         late_sums[5],
         late_sums[6],
-        feed_sums[2],
-        feed_sums[3],
+        late_sums[7],
+        late_sums[8],
         late_sums[0],
         late_sums[1],
         late_sums[2],

time: 751 us -> 787 us (1.048)
  waiting for transfers between devices: 277 us -> 321 us
  local copies, waits for them, and re-layouts: 140 us -> 128 us
    ppermute x15, waiting for transfers between devices: 115 us -> 176 us  [relay_gather(): lax.ppermute(from_right, axis, [(i, i - 1) for i in range(1, count - k +...]
    psum x0 -> x1, waiting for transfers between devices: none -> 34.3 us  [dp_sum(): return lax.psum(term.astype(jnp.bfloat16), 'dp').astype(jnp.float32)]
    ppermute x6, waiting for transfers between devices: 42.8 us -> 19.7 us  [relay_scatter(): lax.ppermute(send_left.astype(value.dtype), axis, [(i, i - 1) for i in ra...]
    ppermute x6, waiting for transfers between devices: 51.1 us -> 28.2 us  [relay_scatter(): lax.ppermute(send_right.astype(value.dtype), axis, [(i, i + 1) for i in r...]
    concatenate x2 -> x3, local copies, waits for them, and re-layouts: 12.6 us -> 4.42 us  [stacked_psum(): jnp.concatenate([matrix, extra]).astype(jnp.bfloat16)]
    reduce_sum x5 -> x6, other arithmetic: 16.8 us -> 22.2 us  [layer_norm(): return centred * lax.rsqrt(spread + EPSILON) * norm_gain + norm_bias]
    unnamed x227 -> x221, local copies, waits for them, and re-layouts: 22.7 us -> 27.2 us
    psum x2 -> x1, waiting for transfers between devices: 41 us -> 42.5 us  [stacked_psum(): lax.psum(jnp.concatenate([matrix, extra]).astype(jnp.bfloat16), axis)]
  transfers between devices with their start and end apart: 48 -> 48, of which waited for: 27 -> 25; matrix products, arithmetic and copies ran while one was open for 40% -> 36% of each run, Pallas kernels for 0% -> 0%
where the time goes in v6:
time: 787 us; the launch traced here: 776 us
  waiting for transfers between devices  321 us (41%)
  local copies, waits for them, and re-layouts  128 us (16%)
  matrix products  110 us (14%)
  other arithmetic  107 us (14%)
  starting transfers between devices  80.3 us (10%)
  between operations  16.1 us (2%)
  blocking collectives  11.9 us (2%)
    ppermute x15, waiting for transfers between devices, relay_gather(): lax.ppermute(from_right, axis, [(i, i - 1) for i in range(1, count - k +...  176 us
    psum x1, waiting for transfers between devices, stacked_psum(): lax.psum(jnp.concatenate([matrix, extra]).astype(jnp.bfloat16), axis)  42.5 us
    psum x1, waiting for transfers between devices, dp_sum(): return lax.psum(term.astype(jnp.bfloat16), 'dp').astype(jnp.float32)  34.3 us
    ppermute x15, starting transfers between devices, relay_gather(): lax.ppermute(from_left, axis, [(i, i + 1) for i in range(k - 1, count - 1)])  29.6 us
    ppermute x6, waiting for transfers between devices, relay_scatter(): lax.ppermute(send_right.astype(value.dtype), axis, [(i, i + 1) for i in r...  28.2 us
    unnamed x221, local copies, waits for them, and re-layouts  27.2 us
    ppermute x6, starting transfers between devices, relay_scatter(): lax.ppermute(send_right.astype(value.dtype), axis, [(i, i + 1) for i in r...  23.3 us
    reduce_sum x6, other arithmetic, layer_norm(): return centred * lax.rsqrt(spread + EPSILON) * norm_gain + norm_bias  22.2 us
  transfers between devices with their start and end apart: 48, of which 25 were waited for; matrix products, arithmetic and copies ran while one was open for 36% of the time, Pallas kernels for 0%

profile of v6, /device:TPU:0, one launch (start us, length us, event | category | flops | bytes accessed | tf_op | source)
XLA Modules:
  0.0 775.9 jit_solution(18273933623400644172)
XLA Ops:
  20.5 21.7 %while.94 = (s32[]{:T(128)}, bf16[2,512,4,64]{1,3,2,0:T(8,128)(2,1)}, f32[2,4,512]{2,1,0:T(4,128)}, s32[]{:T(128)}, s32[2]{0:T(128)}, /*index=5*/bf16[2,512,4,64...) while((s32[]{:T(128)}, ...), condition=%wide.region_5.6_spmd, body=%wide.region_2.5_spmd.sunk | while | flops 563215872 | bytes 35199192 | solution.py:64
  77.1 31.5 %collective-permute-done.3 = bf16[1024,256]{1,0:T(8,128)(2,1)S(1)} collective-permute-done((bf16[1024,256]{1,0:T(8,128)(2,1)}, bf16[1024,256]{1,0:T(8,128)(2,1)S(1)}, u32[]{:S(2)}, u32[]{:S(2)}) %collective-permute-start.3) | collective-permute-done | bytes 524320 | tf_op jit(solution)/shard_map/ppermute | solution.py:121
  113.7 13.5 %collective-permute-done.5 = bf16[1024,256]{1,0:T(8,128)(2,1)S(1)} collective-permute-done((bf16[1024,256]{1,0:T(8,128)(2,1)S(1)}, bf16[1024,256]{1,0:T(8,128)(2,1)S(1)}, u32[]{:S(2)}, u32[]{:S(2)}) %collective-permute-start.5) | collective-permute-done | bytes 524320 | tf_op jit(solution)/shard_map/ppermute | solution.py:121
  152.3 8.7 %collective-permute-done.6 = bf16[1024,256]{1,0:T(8,128)(2,1)} collective-permute-done((bf16[1024,256]{1,0:T(8,128)(2,1)}, bf16[1024,256]{1,0:T(8,128)(2,1)}, u32[]{:S(2)}, u32[]{:S(2)}) %collective-permute-start.6) | collective-permute-done | bytes 524320 | tf_op jit(solution)/shard_map/ppermute | solution.py:120
  174.3 25.3 %collective-permute-done.9 = bf16[1024,256]{1,0:T(8,128)(2,1)S(1)} collective-permute-done((bf16[1024,256]{1,0:T(8,128)(2,1)}, bf16[1024,256]{1,0:T(8,128)(2,1)S(1)}, u32[]{:S(2)}, u32[]{:S(2)}) %collective-permute-start.9) | collective-permute-done | bytes 524320 | tf_op jit(solution)/shard_map/ppermute | solution.py:121
  204.4 25.6 %collective-permute-done.11 = bf16[1024,256]{1,0:T(8,128)(2,1)S(1)} collective-permute-done((bf16[1024,256]{1,0:T(8,128)(2,1)S(1)}, bf16[1024,256]{1,0:T(8,128)(2,1)S(1)}, u32[]{:S(2)}, u32[]{:S(2)}) %collective-permute-start.11) | collective-permute-done | bytes 524320 | tf_op jit(solution)/shard_map/ppermute | solution.py:121
  241.9 13.5 %multiply_convert_fusion.2 = (bf16[1024,1024]{1,0:T(8,128)(2,1)}, f32[1024,1024]{1,0:T(8,128)S(1)}, f32[1024,1024]{1,0:T(8,128)S(1)}) fusion(bf16[1024,1024]{1,0:T(8,128)(2,1)} %add_convert_fusion.2, bf16[1024,1024]{1,0:T(8,128)(2,1)S(1)} %copy-done), kind=kOutput, calls=%fused_computation.146 | convolution fusion | flops 2215641088 | bytes 14680064 | tf_op jit(solution)/shard_map/dot_general | solution.py:247
  267.2 8.5 %collective-permute-done.12 = bf16[256,1024]{1,0:T(8,128)(2,1)} collective-permute-done((bf16[256,1024]{1,0:T(8,128)(2,1)S(1)}, bf16[256,1024]{1,0:T(8,128)(2,1)}, u32[]{:S(2)}, u32[]{:S(2)}) %collective-permute-start.12) | collective-permute-done | bytes 524320 | tf_op jit(solution)/shard_map/ppermute | solution.py:146
  282.4 9.1 %collective-permute-done.13 = bf16[256,1024]{1,0:T(8,128)(2,1)} collective-permute-done((bf16[256,1024]{1,0:T(8,128)(2,1)S(1)}, bf16[256,1024]{1,0:T(8,128)(2,1)}, u32[]{:S(2)}, u32[]{:S(2)}) %collective-permute-start.13) | collective-permute-done | bytes 524320 | tf_op jit(solution)/shard_map/ppermute | solution.py:146
  309.6 13.4 %collective-permute-done.17 = bf16[256,1024]{1,0:T(8,128)(2,1)S(1)} collective-permute-done((bf16[256,1024]{1,0:T(8,128)(2,1)S(1)}, bf16[256,1024]{1,0:T(8,128)(2,1)S(1)}, u32[]{:S(2)}, u32[]{:S(2)}) %collective-permute-start.17) | collective-permute-done | bytes 524320 | tf_op jit(solution)/shard_map/ppermute | solution.py:149
  345.1 5.9 convolution_convert_fusion.4
  361.3 6.2 collective-permute-done.23
  372.4 6.7 fusion.76
  387.9 6.9 while.96
  399.0 34.3 %all-reduce.10.cloned.1.call-done = (bf16[1024,1024]{1,0:T(8,128)(2,1)}, bf16[1024,1024]{1,0:T(8,128)(2,1)}) async-done(((bf16[1024,1024]{1,0:T(8,128)(2,1)}, bf16[1024,1024]{1,0:T(8,128)(2,1)}), (bf16[1024,1024]{1,0:T(8,128)(2,1)}, bf16[1024,1024]{1,0:T(8,128)(2,1)})) %all-reduce.10.cloned.1.call-update) | async-done | bytes 4194320 | tf_op jit(solution)/shard_map/psum | solution.py:174
  449.5 6.1 collective-permute-done.25
  462.7 18.9 %collective-permute-done.27 = bf16[1024,256]{1,0:T(8,128)(2,1)S(1)} collective-permute-done((bf16[1024,256]{1,0:T(8,128)(2,1)}, bf16[1024,256]{1,0:T(8,128)(2,1)S(1)}, u32[]{:S(2)}, u32[]{:S(2)}) %collective-permute-start.27) | collective-permute-done | bytes 524320 | tf_op jit(solution)/shard_map/ppermute | solution.py:121
  486.7 32.7 %collective-permute-done.29 = bf16[1024,256]{1,0:T(8,128)(2,1)S(1)} collective-permute-done((bf16[1024,256]{1,0:T(8,128)(2,1)S(1)}, bf16[1024,256]{1,0:T(8,128)(2,1)S(1)}, u32[]{:S(2)}, u32[]{:S(2)}) %collective-permute-start.29) | collective-permute-done | bytes 524320 | tf_op jit(solution)/shard_map/ppermute | solution.py:121
  520.2 9.8 %convert_reduce_fusion = (f32[1024,1024]{1,0:T(8,128)}, bf16[4,1024,1024]{2,1,0:T(8,128)(2,1)}) fusion(bf16[5,1024,256]{2,1,0:T(8,128)(2,1)} %bitcast_dynamic-update-slice_fusion.9, bf16[4,1024,256]{2,1,0:T(8,128)(2,1)S(1)} %bitcast.502), kind=kOutput, calls=%fused_computation.98 | convolution fusion | flops 2159017984 | bytes 17301504 | tf_op jit(solution)/shard_map/gse,gde->gsd/dot_general | solution.py:178
  543.0 31.6 %while.97 = (s32[]{:T(128)}, f32[1024,4,64]{0,2,1:T(8,128)S(1)}, f32[1024,4,64]{0,2,1:T(8,128)}, bf16[2,512,4,64]{1,3,2,0:T(8,128)(2,1)}, bf16[2,512,4,64]{1,3,2...) while((s32[]{:T(128)}, f32[1024,4,64]{0,2,1:T(8,128)S(1)}, ...), condition=%wide.region_29.30_spmd.clone, body=%wide.region_27.29_spmd.clone.sunk | while | flops 1376124416 | bytes 84998440 | solution.py:103
  635.7 6.3 collective-permute-done.35
  665.4 42.5 %all-reduce.8.cloned.1.call-done = (bf16[272,1024]{1,0:T(8,128)(2,1)}, bf16[3,1024,256]{1,2,0:T(8,128)(2,1)}, bf16[2,1024,256]{1,2,0:T(8,128)(2,1)}, bf16[256,1024]{1,0:T(8,128)(2,1)}, bf16[1024,256]{1,0:T(8,128)(2,1)}) async-done(((bf16[272,1024]{1,0:T(8,128)(2,1)}, bf16[3,1024,256]{1,2,0:T(8,128)(2,1)}, bf16[2,1024,256]{1,2,0:T(8,128)(2,1)}, bf16[256,1024]{1,0:T(8,128)(2,1)}, ...) | async-done | bytes 4227088 | tf_op jit(solution)/shard_map/psum | solution.py:167
  730.7 9.8 %collective-permute-done.41 = bf16[256,1024]{1,0:T(8,128)(2,1)S(1)} collective-permute-done((bf16[256,1024]{1,0:T(8,128)(2,1)}, bf16[256,1024]{1,0:T(8,128)(2,1)S(1)}, u32[]{:S(2)}, u32[]{:S(2)}) %collective-permute-start.41) | collective-permute-done | bytes 524320 | tf_op jit(solution)/shard_map/ppermute | solution.py:121
  746.8 11.9 %all-reduce = (bf16[1024]{0:T(1024)(128)(2,1)S(1)}, bf16[1024]{0:T(1024)(128)(2,1)S(1)}) all-reduce(bf16[1024]{0:T(1024)(128)(2,1)S(1)} %get-tuple-element.513, bf16[1024]{0:T(1024)(128)(2,1)S(1)} %slice_reduce_fusion), channel_id=1, replica_groups=mesh['dp'=8,'tensor'=4] {'dp'}, use_global_device_ids=true, to_apply=%region_34.35 | all-reduce | flops 2048 | bytes 8192 | tf_op jit(solution)/shard_map/psum | solution.py:174
  (570 shorter events, 421.6 us)
Async XLA Ops:
  7.2 120.8 %all-gather.7.cloned.1.call-start = ((), (), s32[]{:S(2)}) async-start(), calls=%async_computation | async-start | bytes 2621440 | tf_op jit(solution)/shard_map/all_gather | solution.py:221
  8.0 222.9 %all-gather.9.cloned.1.call-start = ((), (), s32[]{:S(2)}) async-start(), calls=%async_computation.1 | async-start | bytes 2621440 | tf_op jit(solution)/shard_map/all_gather | solution.py:222
  47.0 19.0 %collective-permute-start = (bf16[1024,256]{1,0:T(8,128)(2,1)}, bf16[1024,256]{1,0:T(8,128)(2,1)}, u32[]{:S(2)}, u32[]{:S(2)}) collective-permute-start(bf16[1024,256]{1,0:T(8,128)(2,1)} %copy.69), channel_id=1, source_target_pairs={{0,1},{1,2},{2,3},{4,5},{5,6},{6,7},{8,9},{9,10},{10,11},{12,13},{... | collective-permute-start | bytes 1572872 | tf_op jit(solution)/shard_map/ppermute | solution.py:120
  52.8 16.1 %collective-permute-start.1 = (bf16[1024,256]{1,0:T(8,128)(2,1)}, bf16[1024,256]{1,0:T(8,128)(2,1)}, u32[]{:S(2)}, u32[]{:S(2)}) collective-permute-start(bf16[1024,256]{1,0:T(8,128)(2,1)} %copy.69), channel_id=1, source_target_pairs={{1,0},{2,1},{3,2},{5,4},{6,5},{7,6},{9,8},{10,9},{11,10},{13,12},{... | collective-permute-start | bytes 1572872 | tf_op jit(solution)/shard_map/ppermute | solution.py:121
  54.1 187.8 %all-gather.11.cloned.1.call-start = ((), (), s32[]{:S(2)}) async-start(), calls=%async_computation.2 | async-start | bytes 2621440 | tf_op jit(solution)/shard_map/all_gather | solution.py:223
  68.9 39.8 %collective-permute-start.3 = (bf16[1024,256]{1,0:T(8,128)(2,1)}, bf16[1024,256]{1,0:T(8,128)(2,1)S(1)}, u32[]{:S(2)}, u32[]{:S(2)}) collective-permute-start(bf16[1024,256]{1,0:T(8,128)(2,1)} %collective-permute-done.1), channel_id=1, source_target_pairs={{1,0},{2,1},{5,4},{6,5},{9,8},{10,9},{13,12},{14,13},{17,16},{18,1... | collective-permute-start | bytes 1572872 | tf_op jit(solution)/shard_map/ppermute | solution.py:121
  74.6 38.3 %collective-permute-start.4 = (bf16[1024,256]{1,0:T(8,128)(2,1)}, bf16[1024,256]{1,0:T(8,128)(2,1)S(1)}, u32[]{:S(2)}, u32[]{:S(2)}) collective-permute-start(bf16[1024,256]{1,0:T(8,128)(2,1)} %collective-permute-done.2), channel_id=1, source_target_pairs={{2,3},{6,7},{10,11},{14,15},{18,19},{22,23},{26,27},{30,31}} | collective-permute-start | bytes 1572872 | tf_op jit(solution)/shard_map/ppermute | solution.py:120
  108.7 18.5 %collective-permute-start.5 = (bf16[1024,256]{1,0:T(8,128)(2,1)S(1)}, bf16[1024,256]{1,0:T(8,128)(2,1)S(1)}, u32[]{:S(2)}, u32[]{:S(2)}) collective-permute-start(bf16[1024,256]{1,0:T(8,128)(2,1)S(1)} %collective-permute-done.3), channel_id=1, source_target_pairs={{1,0},{5,4},{9,8},{13,12},{17,16},{21,20},{25,24},{29,28}} | collective-permute-start | bytes 1572872 | tf_op jit(solution)/shard_map/ppermute | solution.py:121
  162.5 270.8 %all-reduce.10.cloned.1.call-start = ((), (), s32[]{:S(2)}) async-start(), calls=%async_computation.4 | async-start | bytes 8388608 | tf_op jit(solution)/shard_map/psum | solution.py:174
  166.0 33.6 %collective-permute-start.9 = (bf16[1024,256]{1,0:T(8,128)(2,1)}, bf16[1024,256]{1,0:T(8,128)(2,1)S(1)}, u32[]{:S(2)}, u32[]{:S(2)}) collective-permute-start(bf16[1024,256]{1,0:T(8,128)(2,1)} %collective-permute-done.7), channel_id=1, source_target_pairs={{1,0},{2,1},{5,4},{6,5},{9,8},{10,9},{13,12},{14,13},{17,16},{18,1... | collective-permute-start | bytes 1572872 | tf_op jit(solution)/shard_map/ppermute | solution.py:121
  171.7 31.9 %collective-permute-start.10 = (bf16[1024,256]{1,0:T(8,128)(2,1)}, bf16[1024,256]{1,0:T(8,128)(2,1)S(1)}, u32[]{:S(2)}, u32[]{:S(2)}) collective-permute-start(bf16[1024,256]{1,0:T(8,128)(2,1)} %collective-permute-done.8), channel_id=1, source_target_pairs={{2,3},{6,7},{10,11},{14,15},{18,19},{22,23},{26,27},{30,31}} | collective-permute-start | bytes 1572872 | tf_op jit(solution)/shard_map/ppermute | solution.py:120
  199.6 30.4 %collective-permute-start.11 = (bf16[1024,256]{1,0:T(8,128)(2,1)S(1)}, bf16[1024,256]{1,0:T(8,128)(2,1)S(1)}, u32[]{:S(2)}, u32[]{:S(2)}) collective-permute-start(bf16[1024,256]{1,0:T(8,128)(2,1)S(1)} %collective-permute-done.9), channel_id=1, source_target_pairs={{1,0},{5,4},{9,8},{13,12},{17,16},{21,20},{25,24},{29,28}} | collective-permute-start | bytes 1572872 | tf_op jit(solution)/shard_map/ppermute | solution.py:121
  265.7 16.7 %collective-permute-start.15 = (bf16[256,1024]{1,0:T(8,128)(2,1)}, bf16[256,1024]{1,0:T(8,128)(2,1)}, u32[]{:S(2)}, u32[]{:S(2)}) collective-permute-start(bf16[256,1024]{1,0:T(8,128)(2,1)} %get-tuple-element.629), channel_id=1, source_target_pairs={{3,2},{7,6},{11,10},{15,14},{19,18},{23,22},{27,26},{31,30}} | collective-permute-start | bytes 1572872 | tf_op jit(solution)/shard_map/ppermute | solution.py:149
  301.7 21.4 %collective-permute-start.17 = (bf16[256,1024]{1,0:T(8,128)(2,1)S(1)}, bf16[256,1024]{1,0:T(8,128)(2,1)S(1)}, u32[]{:S(2)}, u32[]{:S(2)}) collective-permute-start(bf16[256,1024]{1,0:T(8,128)(2,1)S(1)} %fusion.133), channel_id=1, source_target_pairs={{1,0},{2,1},{3,2},{5,4},{6,5},{7,6},{9,8},{10,9},{11,10},{13,12},{... | collective-permute-start | bytes 1572872 | tf_op jit(solution)/shard_map/ppermute | solution.py:149
  351.6 306.6 %all-reduce.12.cloned.1.call-start = ((), (), s32[]{:S(2)}) async-start(), calls=%async_computation.5 | async-start | bytes 4718592 | tf_op jit(solution)/shard_map/psum | solution.py:291
  396.7 49.4 %collective-permute-start.24 = (bf16[1024,256]{1,0:T(8,128)(2,1)S(1)}, bf16[1024,256]{1,0:T(8,128)(2,1)}, u32[]{:S(2)}, u32[]{:S(2)}) collective-permute-start(bf16[1024,256]{1,0:T(8,128)(2,1)S(1)} %copy.83), channel_id=1, source_target_pairs={{0,1},{1,2},{2,3},{4,5},{5,6},{6,7},{8,9},{9,10},{10,11},{12,13},{... | collective-permute-start | bytes 1572872 | tf_op jit(solution)/shard_map/ppermute | solution.py:120
  455.6 26.1 %collective-permute-start.27 = (bf16[1024,256]{1,0:T(8,128)(2,1)}, bf16[1024,256]{1,0:T(8,128)(2,1)S(1)}, u32[]{:S(2)}, u32[]{:S(2)}) collective-permute-start(bf16[1024,256]{1,0:T(8,128)(2,1)} %collective-permute-done.25), channel_id=1, source_target_pairs={{1,0},{2,1},{5,4},{6,5},{9,8},{10,9},{13,12},{14,13},{17,16},{18,1... | collective-permute-start | bytes 1572872 | tf_op jit(solution)/shard_map/ppermute | solution.py:121
  458.1 249.8 %all-reduce.8.cloned.1.call-start = ((), (), s32[]{:S(2)}) async-start(), calls=%async_computation.3 | async-start | bytes 8454144 | tf_op jit(solution)/shard_map/psum | solution.py:167
  460.2 25.7 %collective-permute-start.28 = (bf16[1024,256]{1,0:T(8,128)(2,1)}, bf16[1024,256]{1,0:T(8,128)(2,1)S(1)}, u32[]{:S(2)}, u32[]{:S(2)}) collective-permute-start(bf16[1024,256]{1,0:T(8,128)(2,1)} %collective-permute-done.26), channel_id=1, source_target_pairs={{2,3},{6,7},{10,11},{14,15},{18,19},{22,23},{26,27},{30,31}} | collective-permute-start | bytes 1572872 | tf_op jit(solution)/shard_map/ppermute | solution.py:120
  481.7 37.7 %collective-permute-start.29 = (bf16[1024,256]{1,0:T(8,128)(2,1)S(1)}, bf16[1024,256]{1,0:T(8,128)(2,1)S(1)}, u32[]{:S(2)}, u32[]{:S(2)}) collective-permute-start(bf16[1024,256]{1,0:T(8,128)(2,1)S(1)} %collective-permute-done.27), channel_id=1, source_target_pairs={{1,0},{5,4},{9,8},{13,12},{17,16},{21,20},{25,24},{29,28}} | collective-permute-start | bytes 1572872 | tf_op jit(solution)/shard_map/ppermute | solution.py:121
  606.1 22.9 %collective-permute-start.34 = (bf16[256,1024]{1,0:T(8,128)(2,1)}, bf16[256,1024]{1,0:T(8,128)(2,1)S(1)}, u32[]{:S(2)}, u32[]{:S(2)}) collective-permute-start(bf16[256,1024]{1,0:T(8,128)(2,1)} %get-tuple-element.623), channel_id=1, source_target_pairs={{2,1},{3,2},{6,5},{7,6},{10,9},{11,10},{14,13},{15,14},{18,17},{19... | collective-permute-start | bytes 1572872 | tf_op jit(solution)/shard_map/ppermute | solution.py:149
  656.5 65.8 %collective-permute-start.38 = (bf16[256,1024]{1,0:T(8,128)(2,1)}, bf16[256,1024]{1,0:T(8,128)(2,1)}, u32[]{:S(2)}, u32[]{:S(2)}) collective-permute-start(bf16[256,1024]{1,0:T(8,128)(2,1)} %collective-permute-done.36), channel_id=1, source_target_pairs={{1,2},{2,3},{5,6},{6,7},{9,10},{10,11},{13,14},{14,15},{17,18},{18... | collective-permute-start | bytes 1572872 | tf_op jit(solution)/shard_map/ppermute | solution.py:120
  664.1 60.8 %collective-permute-start.39 = (bf16[256,1024]{1,0:T(8,128)(2,1)}, bf16[256,1024]{1,0:T(8,128)(2,1)}, u32[]{:S(2)}, u32[]{:S(2)}) collective-permute-start(bf16[256,1024]{1,0:T(8,128)(2,1)} %collective-permute-done.37), channel_id=1, source_target_pairs={{1,0},{2,1},{5,4},{6,5},{9,8},{10,9},{13,12},{14,13},{17,16},{18,1... | collective-permute-start | bytes 1572872 | tf_op jit(solution)/shard_map/ppermute | solution.py:121
  724.9 15.7 %collective-permute-start.41 = (bf16[256,1024]{1,0:T(8,128)(2,1)}, bf16[256,1024]{1,0:T(8,128)(2,1)S(1)}, u32[]{:S(2)}, u32[]{:S(2)}) collective-permute-start(bf16[256,1024]{1,0:T(8,128)(2,1)} %collective-permute-done.39), channel_id=1, source_target_pairs={{1,0},{5,4},{9,8},{13,12},{17,16},{21,20},{25,24},{29,28}} | collective-permute-start | bytes 1572872 | tf_op jit(solution)/shard_map/ppermute | solution.py:121
  (148 other events, 1564.9 us)
Sparse Core Ops, SparseCore 0:
  9.6 48.6 all-gather.6
  59.9 56.3 all-gather.8
  162.6 61.1 all-gather.10
  351.7 81.5 all-reduce.9
  458.2 107.2 all-reduce.11
  623.1 84.6 all-reduce.7

commit v7 on v6

--- a/solution.py
+++ b/solution.py
@@ -110,22 +110,17 @@
     return lax.psum(partial_value.astype(jnp.bfloat16), "tensor").astype(jnp.float32)
 
 
-def relay_gather(block, axis):
+def relay_pieces(block, axis):
     count = lax.axis_size(axis)
     me = lax.axis_index(axis)
-    out = jnp.zeros((count + 1,) + block.shape, block.dtype)
-    out = lax.dynamic_update_index_in_dim(out, block, me, 0)
+    pieces = [(block, me)]
     from_left, from_right = block, block
     for k in range(1, count):
         from_left = lax.ppermute(from_left, axis, [(i, i + 1) for i in range(k - 1, count - 1)])
         from_right = lax.ppermute(from_right, axis, [(i, i - 1) for i in range(1, count - k + 1)])
-        out = lax.dynamic_update_index_in_dim(
-            out, from_left, jnp.where(me - k >= 0, me - k, count), 0
-        )
-        out = lax.dynamic_update_index_in_dim(
-            out, from_right, jnp.where(me + k < count, me + k, count), 0
-        )
-    return out[:count]
+        pieces.append((from_left, me - k))
+        pieces.append((from_right, me + k))
+    return pieces
 
 
 def relay_scatter(value, axis):
@@ -158,7 +153,14 @@
 def relay_total(partial_value):
     low_value = partial_value.astype(jnp.bfloat16)
     reduced = relay_scatter(low_value, "tensor")
-    return relay_gather(reduced, "tensor").reshape(low_value.shape).astype(jnp.float32)
+    pieces = relay_pieces(reduced, "tensor")
+    shards = []
+    for owner in range(len(pieces) // 2 + 1):
+        shard = jnp.zeros_like(reduced)
+        for piece, source in pieces:
+            shard = jnp.where(source == owner, piece, shard)
+        shards.append(shard)
+    return jnp.concatenate(shards).astype(jnp.float32)
 
 
 def stacked_psum(matrix, rows, axis):
@@ -174,9 +176,16 @@
     return lax.psum(term.astype(jnp.bfloat16), "dp").astype(jnp.float32)
 
 
-def gathered_sum(pieces, weights, spec):
-    partial_value = jnp.einsum(spec, pieces, weights, preferred_element_type=jnp.float32)
-    return jnp.sum(partial_value.astype(jnp.bfloat16).astype(jnp.float32), axis=0)
+def gathered_sum(block, weights, spec):
+    count = weights.shape[0]
+    total = None
+    for piece, source in relay_pieces(block, "tensor"):
+        weight = lax.dynamic_index_in_dim(weights, jnp.clip(source, 0, count - 1), 0, keepdims=False)
+        partial_value = jnp.einsum(spec, piece, weight, preferred_element_type=jnp.float32)
+        partial_value = partial_value.astype(jnp.bfloat16).astype(jnp.float32)
+        total = partial_value if total is None else total + partial_value
+        total = lax.optimization_barrier(total)
+    return total
 
 
 def local(
@@ -221,8 +230,7 @@
     self_out_all = lax.all_gather(self_out, "tensor")
     cross_out_all = lax.all_gather(cross_out, "tensor")
     cross_query_all = lax.all_gather(cross_query, "tensor")
-    self_pieces = relay_gather(self_flat, "tensor")
-    after_self = inputs + gathered_sum(self_pieces, self_out_all, "gsk,gkd->gsd")
+    after_self = inputs + gathered_sum(self_flat, self_out_all, "sk,kd->sd")
     normed_cross = layer_norm(after_self, cross_gain, cross_bias).astype(jnp.bfloat16)
     cross_queries = jnp.dot(normed_cross, cross_query, preferred_element_type=jnp.float32).astype(
         jnp.bfloat16
@@ -240,10 +248,8 @@
         cross_clip, (cross_queries, text_proj[0], text_proj[1], text_token_length)
     )
     cross_flat = cross_heads.reshape(row_total, local_width)
-    cross_pieces = relay_gather(cross_flat, "tensor")
-    after_cross = after_self + gathered_sum(cross_pieces, cross_out_all, "gsk,gkd->gsd")
+    after_cross = after_self + gathered_sum(cross_flat, cross_out_all, "sk,kd->sd")
     normed_feed = layer_norm(after_cross, feed_gain, feed_bias).astype(jnp.bfloat16)
-    cross_query_all, normed_feed = lax.optimization_barrier((cross_query_all, normed_feed))
     upward = jnp.dot(normed_feed, feed_up, preferred_element_type=jnp.float32)
     active = gelu_exact(upward).astype(jnp.bfloat16)
     feed_part = jnp.dot(active, feed_down, preferred_element_type=jnp.float32)
@@ -255,11 +261,11 @@
         "sk,sd->kd", active, out_grad, preferred_element_type=jnp.float32
     )
     up_grad = jnp.einsum("sd,sk->dk", normed_feed, upward_grad, preferred_element_type=jnp.float32)
-    feed_sums = [dp_sum(up_grad), dp_sum(downward_gradient)]
     feed_input_part = jnp.einsum(
         "sk,dk->sd", upward_grad, feed_up, preferred_element_type=jnp.float32
     )
     feed_back = norm_back(after_cross, feed_gain, feed_bias, relay_total(feed_input_part))
+    feed_sums = [dp_sum(up_grad), dp_sum(downward_gradient)]
     cross_grad_rows = out_grad.astype(jnp.float32) + feed_back[0]
     cross_grad_low = cross_grad_rows.astype(jnp.bfloat16)
     cout_grad = jnp.einsum(
@@ -302,8 +308,7 @@
     text_part = jnp.einsum(
         "gcte,gde->ctd", keyval_grad_low, cross_keyval, preferred_element_type=jnp.float32
     )
-    query_pieces = relay_gather(query_grad_low, "tensor")
-    cross_sum = gathered_sum(query_pieces, cross_query_all, "gse,gde->gsd")
+    cross_sum = gathered_sum(query_grad_low, cross_query_all, "se,de->sd")
     text_grad = lax.psum(text_part.astype(jnp.bfloat16), "tensor").astype(jnp.float32)
     cross_back = norm_back(after_self, cross_gain, cross_bias, cross_sum)
     self_grad_rows = cross_grad_rows + cross_back[0]

time: 787 us -> 691 us (0.88)
  local copies, waits for them, and re-layouts: 128 us -> 51.3 us
  waiting for transfers between devices: 321 us -> 291 us
  starting transfers between devices: 80.3 us -> 95.7 us
  other arithmetic: 107 us -> 99 us
    dynamic_update_slice x33 -> x0, local copies, waits for them, and re-layouts: 43.6 us -> none  [the longest x15 22.1 us: relay_gather(): lax.dynamic_update_index_in_dim(out, from_left, jnp.where(me - k >= 0, me...]
    psum x1, waiting for transfers between devices: 34.3 us -> 0.02 us  [dp_sum(): return lax.psum(term.astype(jnp.bfloat16), 'dp').astype(jnp.float32)]
    all_gather x1, waiting for transfers between devices: 0.01 us -> 26.2 us  [local(): cross_query_all = lax.all_gather(cross_query, 'tensor')]
    ppermute x30, waiting for transfers between devices: 196 us -> 173 us  [the longest x15 162 us: relay_pieces(): lax.ppermute(from_right, axis, [(i, i - 1) for i in range(1, count - k +...]
    ppermute x30, starting transfers between devices: 49.5 us -> 63.8 us  [the longest x15 44.4 us: relay_pieces(): lax.ppermute(from_left, axis, [(i, i + 1) for i in range(k - 1, count - 1)])]
    dot_general x3 -> x21, matrix products: 19.9 us -> 33.6 us  [gathered_sum(): jnp.einsum(spec, piece, weight, preferred_element_type=jnp.float32)]
    broadcast_in_dim x4 -> x0, local copies, waits for them, and re-layouts: 8.54 us -> none  [relay_gather(): out = lax.dynamic_update_index_in_dim(out, block, me, 0)]
    unnamed x221 -> x201, local copies, waits for them, and re-layouts: 27.2 us -> 20.7 us
  transfers between devices with their start and end apart: 48 -> 48, of which waited for: 25 -> 24; matrix products, arithmetic and copies ran while one was open for 36% -> 31% of each run, Pallas kernels for 0% -> 0%
where the time goes in v7:
time: 691 us; the launch traced here: 684 us
  waiting for transfers between devices  291 us (42%)
  matrix products  117 us (17%)
  other arithmetic  99 us (14%)
  starting transfers between devices  95.7 us (14%)
  local copies, waits for them, and re-layouts  51.3 us (7%)
  between operations  16.6 us (2%)
  blocking collectives  12.8 us (2%)
    ppermute x15, waiting for transfers between devices, relay_pieces(): lax.ppermute(from_right, axis, [(i, i - 1) for i in range(1, count - k +...  162 us
    ppermute x15, starting transfers between devices, relay_pieces(): lax.ppermute(from_left, axis, [(i, i + 1) for i in range(k - 1, count - 1)])  44.4 us
    psum x1, waiting for transfers between devices, stacked_psum(): lax.psum(jnp.concatenate([matrix, extra]).astype(jnp.bfloat16), axis)  39.6 us
    dot_general x21, matrix products, gathered_sum(): jnp.einsum(spec, piece, weight, preferred_element_type=jnp.float32)  33.6 us
    ppermute x6, waiting for transfers between devices, relay_scatter(): lax.ppermute(send_right.astype(value.dtype), axis, [(i, i + 1) for i in r...  32.7 us
    ppermute x6, starting transfers between devices, relay_scatter(): lax.ppermute(send_right.astype(value.dtype), axis, [(i, i + 1) for i in r...  26.2 us
    all_gather x1, waiting for transfers between devices, local(): cross_query_all = lax.all_gather(cross_query, 'tensor')  26.2 us
    reduce_sum x14, other arithmetic, layer_norm(): return centred * lax.rsqrt(spread + EPSILON) * norm_gain + norm_bias  24.9 us
  transfers between devices with their start and end apart: 48, of which 24 were waited for; matrix products, arithmetic and copies ran while one was open for 31% of the time, Pallas kernels for 0%

profile of v7, /device:TPU:0, one launch (start us, length us, event | category | flops | bytes accessed | tf_op | source)
XLA Modules:
  0.0 684.0 jit_solution(3925030254965795769)
XLA Ops:
  19.3 20.4 %while.94 = (s32[]{:T(128)}, bf16[2,512,4,64]{1,3,2,0:T(8,128)(2,1)}, f32[2,4,512]{2,1,0:T(4,128)S(1)}, s32[]{:T(128)}, s32[2]{0:T(128)S(1)}, /*index=5*/bf16[2,...) while((s32[]{:T(128)}, ...), condition=%wide.region_5.6_spmd, body=%wide.region_2.5_spmd.sunk | while | flops 563215872 | bytes 35199192 | solution.py:64
  43.1 6.4 collective-permute-start
  49.5 18.2 %collective-permute-done.1 = bf16[1024,256]{0,1:T(8,128)(2,1)} collective-permute-done((bf16[1024,256]{0,1:T(8,128)(2,1)S(1)}, bf16[1024,256]{0,1:T(8,128)(2,1)}, u32[]{:S(2)}, u32[]{:S(2)}) %collective-permute-start.1) | collective-permute-done | bytes 524320 | tf_op jit(solution)/shard_map/ppermute | solution.py:120
  72.4 11.3 %collective-permute-done.3 = bf16[1024,256]{0,1:T(8,128)(2,1)} collective-permute-done((bf16[1024,256]{0,1:T(8,128)(2,1)}, bf16[1024,256]{0,1:T(8,128)(2,1)}, u32[]{:S(2)}, u32[]{:S(2)}) %collective-permute-start.3) | collective-permute-done | bytes 524320 | tf_op jit(solution)/shard_map/ppermute | solution.py:120
  100.2 26.8 %collective-permute-done.5 = bf16[1024,256]{0,1:T(8,128)(2,1)} collective-permute-done((bf16[1024,256]{0,1:T(8,128)(2,1)}, bf16[1024,256]{0,1:T(8,128)(2,1)}, u32[]{:S(2)}, u32[]{:S(2)}) %collective-permute-start.5) | collective-permute-done | bytes 524320 | tf_op jit(solution)/shard_map/ppermute | solution.py:120
  163.4 8.5 %collective-permute-done.9 = bf16[1024,256]{0,1:T(8,128)(2,1)S(1)} collective-permute-done((bf16[1024,256]{0,1:T(8,128)(2,1)}, bf16[1024,256]{0,1:T(8,128)(2,1)S(1)}, u32[]{:S(2)}, u32[]{:S(2)}) %collective-permute-start.9) | collective-permute-done | bytes 524320 | tf_op jit(solution)/shard_map/ppermute | solution.py:120
  173.2 9.4 %collective-permute-start.10 = (bf16[1024,256]{0,1:T(8,128)(2,1)S(1)}, bf16[1024,256]{0,1:T(8,128)(2,1)S(1)}, u32[]{:S(2)}, u32[]{:S(2)}) collective-permute-start(bf16[1024,256]{0,1:T(8,128)(2,1)S(1)} %collective-permute-done.8), channel_id=1, source_target_pairs={{2,3},{6,7},{10,11},{14,15},{18,19},{22,23},{26,27},{30,31}} | collective-permute-start | bytes 1572872 | tf_op jit(solution)/shard_map/ppermute | solution.py:119
  190.3 11.0 %multiply_convert_fusion.2 = (bf16[1024,1024]{1,0:T(8,128)(2,1)S(1)}, f32[1024,1024]{1,0:T(8,128)S(1)}, f32[1024,1024]{1,0:T(8,128)S(1)}) fusion(bf16[1024,1024]{1,0:T(8,128)(2,1)S(1)} %copy-done, f32[1024,1024]{1,0:T(8,128)S(1)} %get-tuple-element.618, f32[1024]{0:T(1024)S(1)} %copy-done.100, f32[1024]{0:T(1024)S(1)} %copy-done.90, ...), kind=kOutput, calls=%fused_computation.140 | convolution fusion | flops 2220883968 | bytes 16793600 | tf_op jit(solution)/shard_map/dot_general | solution.py:253
  212.8 6.8 collective-permute-done.12
  248.8 8.8 %collective-permute-done.17 = bf16[256,1024]{1,0:T(8,128)(2,1)S(1)} collective-permute-done((bf16[256,1024]{1,0:T(8,128)(2,1)S(1)}, bf16[256,1024]{1,0:T(8,128)(2,1)S(1)}, u32[]{:S(2)}, u32[]{:S(2)}) %collective-permute-start.17) | collective-permute-done | bytes 524320 | tf_op jit(solution)/shard_map/ppermute | solution.py:144
  270.4 9.3 %collective-permute-done.18 = bf16[256,1024]{1,0:T(8,128)(2,1)S(1)} collective-permute-done((bf16[256,1024]{1,0:T(8,128)(2,1)S(1)}, bf16[256,1024]{1,0:T(8,128)(2,1)S(1)}, u32[]{:S(2)}, u32[]{:S(2)}) %collective-permute-start.18) | collective-permute-done | bytes 524320 | tf_op jit(solution)/shard_map/ppermute | solution.py:120
  281.9 13.7 %collective-permute-done.19 = bf16[256,1024]{1,0:T(8,128)(2,1)S(1)} collective-permute-done((bf16[256,1024]{1,0:T(8,128)(2,1)S(1)}, bf16[256,1024]{1,0:T(8,128)(2,1)S(1)}, u32[]{:S(2)}, u32[]{:S(2)}) %collective-permute-start.19) | collective-permute-done | bytes 524320 | tf_op jit(solution)/shard_map/ppermute | solution.py:120
  325.8 6.9 %while.96 = (s32[]{:T(128)}, f32[128,4,64]{0,2,1:T(8,128)S(1)}, f32[128,4,64]{0,2,1:T(8,128)S(1)}, bf16[2,512,4,64]{1,3,2,0:T(8,128)(2,1)}, bf16[2,512,4,64]{1,3...) while((s32[]{:T(128)}, f32[128,4,64]{0,2,1:T(8,128)S(1)}, ...), condition=%wide.region_18.19_spmd.clone, body=%wide.region_16.18_spmd.clone.sunk | while | flops 170424448 | bytes 14394204 | solution.py:103
  347.4 26.2 %all-gather.11.cloned.1.call-done = bf16[4096,256]{1,0:T(8,128)(2,1)} async-done(((bf16[1024,256]{1,0:T(8,128)(2,1)}), bf16[4096,256]{1,0:T(8,128)(2,1)}) %all-gather.11.cloned.1.call-update) | async-done | bytes 2097168 | tf_op jit(solution)/shard_map/all_gather | solution.py:232
  387.2 26.9 %collective-permute-done.27 = bf16[1024,256]{0,1:T(8,128)(2,1)S(1)} collective-permute-done((bf16[1024,256]{0,1:T(8,128)(2,1)}, bf16[1024,256]{0,1:T(8,128)(2,1)S(1)}, u32[]{:S(2)}, u32[]{:S(2)}) %collective-permute-start.27) | collective-permute-done | bytes 524320 | tf_op jit(solution)/shard_map/ppermute | solution.py:120
  419.5 26.1 %collective-permute-done.29 = bf16[1024,256]{0,1:T(8,128)(2,1)S(1)} collective-permute-done((bf16[1024,256]{0,1:T(8,128)(2,1)S(1)}, bf16[1024,256]{0,1:T(8,128)(2,1)S(1)}, u32[]{:S(2)}, u32[]{:S(2)}) %collective-permute-start.29) | collective-permute-done | bytes 524320 | tf_op jit(solution)/shard_map/ppermute | solution.py:120
  460.9 29.0 %while.97 = (s32[]{:T(128)}, f32[1024,4,64]{0,2,1:T(8,128)S(1)}, f32[1024,4,64]{0,2,1:T(8,128)}, bf16[2,512,4,64]{1,3,2,0:T(8,128)(2,1)}, bf16[2,512,4,64]{1,3,2...) while((s32[]{:T(128)}, f32[1024,4,64]{0,2,1:T(8,128)S(1)}, ...), condition=%wide.region_26.27_spmd.clone, body=%wide.region_24.26_spmd.clone.sunk | while | flops 1376124416 | bytes 84998440 | solution.py:103
  501.6 9.1 %collective-permute-done.30 = bf16[256,1024]{1,0:T(8,128)(2,1)S(1)} collective-permute-done((bf16[256,1024]{1,0:T(8,128)(2,1)S(1)}, bf16[256,1024]{1,0:T(8,128)(2,1)S(1)}, u32[]{:S(2)}, u32[]{:S(2)}) %collective-permute-start.30) | collective-permute-done | bytes 524320 | tf_op jit(solution)/shard_map/ppermute | solution.py:141
  518.5 6.7 collective-permute-done.31
  545.0 9.6 %collective-permute-done.35 = bf16[256,1024]{1,0:T(8,128)(2,1)} collective-permute-done((bf16[256,1024]{1,0:T(8,128)(2,1)}, bf16[256,1024]{1,0:T(8,128)(2,1)}, u32[]{:S(2)}, u32[]{:S(2)}) %collective-permute-start.35) | collective-permute-done | bytes 524320 | tf_op jit(solution)/shard_map/ppermute | solution.py:144
  575.8 7.9 %collective-permute-done.37 = bf16[256,1024]{1,0:T(8,128)(2,1)} collective-permute-done((bf16[256,1024]{1,0:T(8,128)(2,1)}, bf16[256,1024]{1,0:T(8,128)(2,1)}, u32[]{:S(2)}, u32[]{:S(2)}) %collective-permute-start.37) | collective-permute-done | bytes 524320 | tf_op jit(solution)/shard_map/ppermute | solution.py:120
  590.1 39.6 %all-reduce.8.cloned.1.call-done = (bf16[272,1024]{1,0:T(8,128)(2,1)}, bf16[3,1024,256]{1,2,0:T(8,128)(2,1)}, bf16[2,1024,256]{1,2,0:T(8,128)(2,1)}, bf16[256,1024]{1,0:T(8,128)(2,1)}, bf16[1024,256]{1,0:T(8,128)(2,1)}) async-done(((bf16[272,1024]{1,0:T(8,128)(2,1)}, bf16[3,1024,256]{1,2,0:T(8,128)(2,1)}, bf16[2,1024,256]{1,2,0:T(8,128)(2,1)}, bf16[256,1024]{1,0:T(8,128)(2,1)}, ...) | async-done | bytes 4227088 | tf_op jit(solution)/shard_map/psum | solution.py:169
  656.4 12.8 %all-reduce = (bf16[1024]{0:T(1024)(128)(2,1)S(1)}, bf16[1024]{0:T(1024)(128)(2,1)S(1)}) all-reduce(bf16[1024]{0:T(1024)(128)(2,1)S(1)} %get-tuple-element.509, bf16[1024]{0:T(1024)(128)(2,1)S(1)} %add_add_fusion.6), channel_id=1, replica_groups=mesh['dp'=8,'tensor'=4] {'dp'}, use_global_device_ids=true, to_apply=%region_31.32 | all-reduce | flops 2048 | bytes 8192 | tf_op jit(solution)/shard_map/psum | solution.py:176
  670.3 6.6 add_bitcast_fusion
  (529 shorter events, 367.9 us)
Async XLA Ops:
  7.2 79.6 %all-gather.7.cloned.1.call-start = ((), (), s32[]{:S(2)}) async-start(), calls=%async_computation | async-start | bytes 2621440 | tf_op jit(solution)/shard_map/all_gather | solution.py:230
  8.0 140.5 %all-gather.9.cloned.1.call-start = ((), (), s32[]{:S(2)}) async-start(), calls=%async_computation.1 | async-start | bytes 2621440 | tf_op jit(solution)/shard_map/all_gather | solution.py:231
  41.8 25.9 %collective-permute-start.1 = (bf16[1024,256]{0,1:T(8,128)(2,1)S(1)}, bf16[1024,256]{0,1:T(8,128)(2,1)}, u32[]{:S(2)}, u32[]{:S(2)}) collective-permute-start(bf16[1024,256]{0,1:T(8,128)(2,1)S(1)} %bitcast.441), channel_id=1, source_target_pairs={{1,0},{2,1},{3,2},{5,4},{6,5},{7,6},{9,8},{10,9},{11,10},{13,12},{... | collective-permute-start | bytes 1572872 | tf_op jit(solution)/shard_map/ppermute | solution.py:120
  43.1 25.9 %collective-permute-start = (bf16[1024,256]{0,1:T(8,128)(2,1)S(1)}, bf16[1024,256]{0,1:T(8,128)(2,1)}, u32[]{:S(2)}, u32[]{:S(2)}) collective-permute-start(bf16[1024,256]{0,1:T(8,128)(2,1)S(1)} %bitcast.442), channel_id=1, source_target_pairs={{0,1},{1,2},{2,3},{4,5},{5,6},{6,7},{8,9},{9,10},{10,11},{12,13},{... | collective-permute-start | bytes 1572872 | tf_op jit(solution)/shard_map/ppermute | solution.py:119
  67.8 15.9 %collective-permute-start.3 = (bf16[1024,256]{0,1:T(8,128)(2,1)}, bf16[1024,256]{0,1:T(8,128)(2,1)}, u32[]{:S(2)}, u32[]{:S(2)}) collective-permute-start(bf16[1024,256]{0,1:T(8,128)(2,1)} %collective-permute-done.1), channel_id=1, source_target_pairs={{1,0},{2,1},{5,4},{6,5},{9,8},{10,9},{13,12},{14,13},{17,16},{18,1... | collective-permute-start | bytes 1572872 | tf_op jit(solution)/shard_map/ppermute | solution.py:120
  69.1 15.9 %collective-permute-start.2 = (bf16[1024,256]{0,1:T(8,128)(2,1)}, bf16[1024,256]{0,1:T(8,128)(2,1)}, u32[]{:S(2)}, u32[]{:S(2)}) collective-permute-start(bf16[1024,256]{0,1:T(8,128)(2,1)} %collective-permute-done), channel_id=1, source_target_pairs={{1,2},{2,3},{5,6},{6,7},{9,10},{10,11},{13,14},{14,15},{17,18},{18... | collective-permute-start | bytes 1572872 | tf_op jit(solution)/shard_map/ppermute | solution.py:119
  70.6 269.8 %all-reduce.10.cloned.1.call-start = ((), (), s32[]{:S(2)}) async-start(), calls=%async_computation.4 | async-start | bytes 8388608 | tf_op jit(solution)/shard_map/psum | solution.py:176
  83.7 43.3 %collective-permute-start.5 = (bf16[1024,256]{0,1:T(8,128)(2,1)}, bf16[1024,256]{0,1:T(8,128)(2,1)}, u32[]{:S(2)}, u32[]{:S(2)}) collective-permute-start(bf16[1024,256]{0,1:T(8,128)(2,1)} %collective-permute-done.3), channel_id=1, source_target_pairs={{1,0},{5,4},{9,8},{13,12},{17,16},{21,20},{25,24},{29,28}} | collective-permute-start | bytes 1572872 | tf_op jit(solution)/shard_map/ppermute | solution.py:120
  212.1 16.7 %collective-permute-start.15 = (bf16[256,1024]{1,0:T(8,128)(2,1)S(1)}, bf16[256,1024]{1,0:T(8,128)(2,1)S(1)}, u32[]{:S(2)}, u32[]{:S(2)}) collective-permute-start(bf16[256,1024]{1,0:T(8,128)(2,1)S(1)} %get-tuple-element.636), channel_id=1, source_target_pairs={{3,2},{7,6},{11,10},{15,14},{19,18},{23,22},{27,26},{31,30}} | collective-permute-start | bytes 1572872 | tf_op jit(solution)/shard_map/ppermute | solution.py:144
  236.7 136.9 %all-gather.11.cloned.1.call-start = ((), (), s32[]{:S(2)}) async-start(), calls=%async_computation.2 | async-start | bytes 2621440 | tf_op jit(solution)/shard_map/all_gather | solution.py:232
  263.0 16.7 %collective-permute-start.18 = (bf16[256,1024]{1,0:T(8,128)(2,1)S(1)}, bf16[256,1024]{1,0:T(8,128)(2,1)S(1)}, u32[]{:S(2)}, u32[]{:S(2)}) collective-permute-start(bf16[256,1024]{1,0:T(8,128)(2,1)S(1)} %fusion.126), channel_id=1, source_target_pairs={{1,0},{2,1},{3,2},{5,4},{6,5},{7,6},{9,8},{10,9},{11,10},{13,12},{... | collective-permute-start | bytes 1572872 | tf_op jit(solution)/shard_map/ppermute | solution.py:120
  279.7 15.8 %collective-permute-start.19 = (bf16[256,1024]{1,0:T(8,128)(2,1)S(1)}, bf16[256,1024]{1,0:T(8,128)(2,1)S(1)}, u32[]{:S(2)}, u32[]{:S(2)}) collective-permute-start(bf16[256,1024]{1,0:T(8,128)(2,1)S(1)} %collective-permute-done.18), channel_id=1, source_target_pairs={{1,0},{2,1},{5,4},{6,5},{9,8},{10,9},{13,12},{14,13},{17,16},{18,1... | collective-permute-start | bytes 1572872 | tf_op jit(solution)/shard_map/ppermute | solution.py:120
  281.0 291.5 %all-reduce.12.cloned.1.call-start = ((), (), s32[]{:S(2)}) async-start(), calls=%async_computation.5 | async-start | bytes 4718592 | tf_op jit(solution)/shard_map/psum | solution.py:297
  281.2 21.5 %collective-permute-start.23 = (bf16[256,1024]{1,0:T(8,128)(2,1)S(1)}, bf16[256,1024]{1,0:T(8,128)(2,1)S(1)}, u32[]{:S(2)}, u32[]{:S(2)}) collective-permute-start(bf16[256,1024]{1,0:T(8,128)(2,1)S(1)} %collective-permute-done.22), channel_id=1, source_target_pairs={{2,3},{6,7},{10,11},{14,15},{18,19},{22,23},{26,27},{30,31}} | collective-permute-start | bytes 1572872 | tf_op jit(solution)/shard_map/ppermute | solution.py:119
  334.4 44.4 %collective-permute-start.25 = (bf16[1024,256]{0,1:T(8,128)(2,1)S(1)}, bf16[1024,256]{0,1:T(8,128)(2,1)}, u32[]{:S(2)}, u32[]{:S(2)}) collective-permute-start(bf16[1024,256]{0,1:T(8,128)(2,1)S(1)} %bitcast.476), channel_id=1, source_target_pairs={{1,0},{2,1},{3,2},{5,4},{6,5},{7,6},{9,8},{10,9},{11,10},{13,12},{... | collective-permute-start | bytes 1572872 | tf_op jit(solution)/shard_map/ppermute | solution.py:120
  335.7 44.5 %collective-permute-start.24 = (bf16[1024,256]{0,1:T(8,128)(2,1)S(1)}, bf16[1024,256]{0,1:T(8,128)(2,1)S(1)}, u32[]{:S(2)}, u32[]{:S(2)}) collective-permute-start(bf16[1024,256]{0,1:T(8,128)(2,1)S(1)} %bitcast.477), channel_id=1, source_target_pairs={{0,1},{1,2},{2,3},{4,5},{5,6},{6,7},{8,9},{9,10},{10,11},{12,13},{... | collective-permute-start | bytes 1572872 | tf_op jit(solution)/shard_map/ppermute | solution.py:119
  378.8 250.9 %all-reduce.8.cloned.1.call-start = ((), (), s32[]{:S(2)}) async-start(), calls=%async_computation.3 | async-start | bytes 8454144 | tf_op jit(solution)/shard_map/psum | solution.py:169
  378.8 35.3 %collective-permute-start.27 = (bf16[1024,256]{0,1:T(8,128)(2,1)}, bf16[1024,256]{0,1:T(8,128)(2,1)S(1)}, u32[]{:S(2)}, u32[]{:S(2)}) collective-permute-start(bf16[1024,256]{0,1:T(8,128)(2,1)} %collective-permute-done.25), channel_id=1, source_target_pairs={{1,0},{2,1},{5,4},{6,5},{9,8},{10,9},{13,12},{14,13},{17,16},{18,1... | collective-permute-start | bytes 1572872 | tf_op jit(solution)/shard_map/ppermute | solution.py:120
  380.3 35.1 %collective-permute-start.26 = (bf16[1024,256]{0,1:T(8,128)(2,1)S(1)}, bf16[1024,256]{0,1:T(8,128)(2,1)S(1)}, u32[]{:S(2)}, u32[]{:S(2)}) collective-permute-start(bf16[1024,256]{0,1:T(8,128)(2,1)S(1)} %collective-permute-done.24), channel_id=1, source_target_pairs={{1,2},{2,3},{5,6},{6,7},{9,10},{10,11},{13,14},{14,15},{17,18},{18... | collective-permute-start | bytes 1572872 | tf_op jit(solution)/shard_map/ppermute | solution.py:119
  414.1 31.5 %collective-permute-start.29 = (bf16[1024,256]{0,1:T(8,128)(2,1)S(1)}, bf16[1024,256]{0,1:T(8,128)(2,1)S(1)}, u32[]{:S(2)}, u32[]{:S(2)}) collective-permute-start(bf16[1024,256]{0,1:T(8,128)(2,1)S(1)} %collective-permute-done.27), channel_id=1, source_target_pairs={{1,0},{5,4},{9,8},{13,12},{17,16},{21,20},{25,24},{29,28}} | collective-permute-start | bytes 1572872 | tf_op jit(solution)/shard_map/ppermute | solution.py:120
  500.9 17.6 %collective-permute-start.33 = (bf16[256,1024]{1,0:T(8,128)(2,1)S(1)}, bf16[256,1024]{1,0:T(8,128)(2,1)S(1)}, u32[]{:S(2)}, u32[]{:S(2)}) collective-permute-start(bf16[256,1024]{1,0:T(8,128)(2,1)S(1)} %get-tuple-element.632), channel_id=1, source_target_pairs={{3,2},{7,6},{11,10},{15,14},{19,18},{23,22},{27,26},{31,30}} | collective-permute-start | bytes 1572872 | tf_op jit(solution)/shard_map/ppermute | solution.py:144
  536.7 17.8 %collective-permute-start.35 = (bf16[256,1024]{1,0:T(8,128)(2,1)}, bf16[256,1024]{1,0:T(8,128)(2,1)}, u32[]{:S(2)}, u32[]{:S(2)}) collective-permute-start(bf16[256,1024]{1,0:T(8,128)(2,1)} %fusion.116), channel_id=1, source_target_pairs={{1,0},{2,1},{3,2},{5,4},{6,5},{7,6},{9,8},{10,9},{11,10},{13,12},{... | collective-permute-start | bytes 1572872 | tf_op jit(solution)/shard_map/ppermute | solution.py:144
  574.3 69.0 %collective-permute-start.41 = (bf16[256,1024]{1,0:T(8,128)(2,1)}, bf16[256,1024]{1,0:T(8,128)(2,1)}, u32[]{:S(2)}, u32[]{:S(2)}) collective-permute-start(bf16[256,1024]{1,0:T(8,128)(2,1)} %collective-permute-done.40), channel_id=1, source_target_pairs={{2,3},{6,7},{10,11},{14,15},{18,19},{22,23},{26,27},{30,31}} | collective-permute-start | bytes 1572872 | tf_op jit(solution)/shard_map/ppermute | solution.py:119
  583.7 59.6 %collective-permute-start.38 = (bf16[256,1024]{1,0:T(8,128)(2,1)}, bf16[256,1024]{1,0:T(8,128)(2,1)}, u32[]{:S(2)}, u32[]{:S(2)}) collective-permute-start(bf16[256,1024]{1,0:T(8,128)(2,1)} %collective-permute-done.37), channel_id=1, source_target_pairs={{1,0},{5,4},{9,8},{13,12},{17,16},{21,20},{25,24},{29,28}} | collective-permute-start | bytes 1572872 | tf_op jit(solution)/shard_map/ppermute | solution.py:120
  (139 other events, 1434.6 us)
Sparse Core Ops, SparseCore 0:
  9.6 51.8 all-gather.6
  70.7 59.7 all-gather.8
  236.8 83.5 all-reduce.9
  321.8 51.6 all-gather.10
  378.9 107.1 all-reduce.11
  542.4 87.1 all-reduce.7

commit v8 on v7

--- a/solution.py
+++ b/solution.py
@@ -170,6 +170,41 @@
     summed = summed.astype(jnp.float32)
     count = matrix.shape[0]
     return [summed[:count]] + [summed[count + i] for i in range(len(rows))]
+
+
+def butterfly_sum(terms, axis):
+    count = lax.axis_size(axis)
+    me = lax.axis_index(axis)
+    pieces = [term.astype(jnp.bfloat16).reshape(-1, 128) for term in terms]
+    rows = sum(piece.shape[0] for piece in pieces)
+    pad = (-rows) % (16 * count)
+    if pad:
+        pieces.append(jnp.zeros((pad, 128), jnp.bfloat16))
+    current = jnp.concatenate(pieces)
+    steps = count.bit_length() - 1
+    for level in range(steps):
+        pairs = [(i, i ^ (1 << level)) for i in range(count)]
+        half = current.shape[0] // 2
+        bit = (me // (1 << level)) % 2
+        keep = lax.dynamic_slice_in_dim(current, bit * half, half)
+        sent = lax.dynamic_slice_in_dim(current, (1 - bit) * half, half)
+        arrived = lax.ppermute(sent, axis, pairs)
+        current = (keep.astype(jnp.float32) + arrived.astype(jnp.float32)).astype(jnp.bfloat16)
+    for level in reversed(range(steps)):
+        pairs = [(i, i ^ (1 << level)) for i in range(count)]
+        bit = (me // (1 << level)) % 2
+        arrived = lax.ppermute(current, axis, pairs)
+        current = jnp.where(
+            bit == 0,
+            jnp.concatenate([current, arrived]),
+            jnp.concatenate([arrived, current]),
+        )
+    out, start = [], 0
+    for term in terms:
+        size = term.size // 128
+        out.append(current[start : start + size].astype(jnp.float32).reshape(term.shape))
+        start += size
+    return out
 
 
 def dp_sum(term):
@@ -359,9 +394,19 @@
         feed_back[1],
         feed_back[2],
     )
-    late_sums = [dp_sum(term) for term in (qkv_grad, sout_grad, cquery_grad, ckeyval_grad)]
-    late_sums = late_sums + stacked_psum(
-        cout_grad, [cross_back[1], cross_back[2], feed_back[1], feed_back[2]], "dp"
+    late_sums = butterfly_sum(
+        (
+            qkv_grad,
+            sout_grad,
+            cquery_grad,
+            ckeyval_grad,
+            cout_grad,
+            cross_back[1],
+            cross_back[2],
+            feed_back[1],
+            feed_back[2],
+        ),
+        "dp",
     )
     summed = (
         self_norm_terms[0],

time: 691 us -> 764 us (1.11)
  other arithmetic: 99 us -> 121 us
  local copies, waits for them, and re-layouts: 51.3 us -> 73.1 us
  waiting for transfers between devices: 291 us -> 306 us
  starting transfers between devices: 95.7 us -> 106 us
    psum x1 -> x0, waiting for transfers between devices: 39.6 us -> none  [stacked_psum(): lax.psum(jnp.concatenate([matrix, extra]).astype(jnp.bfloat16), axis)]
    psum x1, waiting for transfers between devices: 0.02 us -> 33.8 us  [local(): lax.psum(feed_low, 'tensor').astype(jnp.float32)]
    all_gather x1, waiting for transfers between devices: 26.2 us -> 0.01 us  [local(): cross_query_all = lax.all_gather(cross_query, 'tensor')]
    ppermute x0 -> x6, waiting for transfers between devices: none -> 21.5 us  [the longest x3 21.5 us: butterfly_sum(): arrived = lax.ppermute(current, axis, pairs)]
    reshape x4 -> x10, local copies, waits for them, and re-layouts: 0.02 us -> 19.7 us  [the longest x5 12.5 us: butterfly_sum(): current[start:start + size].astype(jnp.float32).reshape(term.shape)]
    psum x1, waiting for transfers between devices: 0.02 us -> 17.4 us  [dp_sum(): return lax.psum(term.astype(jnp.bfloat16), 'dp').astype(jnp.float32)]
    select_n x0 -> x3, other arithmetic: none -> 16.7 us  [butterfly_sum(): jnp.where(bit == 0, jnp.concatenate([current, arrived]), jnp.concatenate(...]
    ppermute x15, waiting for transfers between devices: 162 us -> 148 us  [relay_pieces(): lax.ppermute(from_right, axis, [(i, i - 1) for i in range(1, count - k +...]
  transfers between devices with their start and end apart: 48 -> 53, of which waited for: 24 -> 25; matrix products, arithmetic and copies ran while one was open for 31% -> 23% of each run, Pallas kernels for 0% -> 0%
where the time goes in v8:
time: 764 us; the launch traced here: 754 us
  waiting for transfers between devices  306 us (40%)
  other arithmetic  121 us (16%)
  matrix products  116 us (15%)
  starting transfers between devices  106 us (14%)
  local copies, waits for them, and re-layouts  73.1 us (10%)
  between operations  16.6 us (2%)
  blocking collectives  14.8 us (2%)
    ppermute x15, waiting for transfers between devices, relay_pieces(): lax.ppermute(from_right, axis, [(i, i - 1) for i in range(1, count - k +...  148 us
    ppermute x15, starting transfers between devices, relay_pieces(): lax.ppermute(from_left, axis, [(i, i + 1) for i in range(k - 1, count - 1)])  47.7 us
    ppermute x6, waiting for transfers between devices, relay_scatter(): lax.ppermute(send_right.astype(value.dtype), axis, [(i, i + 1) for i in r...  41.6 us
    psum x1, waiting for transfers between devices, local(): lax.psum(feed_low, 'tensor').astype(jnp.float32)  33.8 us
    dot_general x21, matrix products, gathered_sum(): jnp.einsum(spec, piece, weight, preferred_element_type=jnp.float32)  30.4 us
    ppermute x6, starting transfers between devices, relay_scatter(): lax.ppermute(send_right.astype(value.dtype), axis, [(i, i + 1) for i in r...  27.1 us
    reduce_sum x13, other arithmetic, layer_norm(): return centred * lax.rsqrt(spread + EPSILON) * norm_gain + norm_bias  23.7 us
    ppermute x6, waiting for transfers between devices, relay_scatter(): lax.ppermute(send_left.astype(value.dtype), axis, [(i, i - 1) for i in ra...  23.2 us
  transfers between devices with their start and end apart: 53, of which 25 were waited for; matrix products, arithmetic and copies ran while one was open for 23% of the time, Pallas kernels for 0%

profile of v8, /device:TPU:0, one launch (start us, length us, event | category | flops | bytes accessed | tf_op | source)
XLA Modules:
  0.0 753.9 jit_solution(13696308364492704346)
XLA Ops:
  19.4 20.4 %while.94 = (s32[]{:T(128)}, bf16[2,512,4,64]{1,3,2,0:T(8,128)(2,1)}, f32[2,4,512]{2,1,0:T(4,128)S(1)}, s32[]{:T(128)}, s32[2]{0:T(128)S(1)}, /*index=5*/bf16[2,...) while((s32[]{:T(128)}, ...), condition=%wide.region_5.6_spmd, body=%wide.region_2.5_spmd.sunk | while | flops 563215872 | bytes 35199192 | solution.py:64
  49.6 18.2 %collective-permute-done.1 = bf16[1024,256]{0,1:T(8,128)(2,1)} collective-permute-done((bf16[1024,256]{0,1:T(8,128)(2,1)S(1)}, bf16[1024,256]{0,1:T(8,128)(2,1)}, u32[]{:S(2)}, u32[]{:S(2)}) %collective-permute-start.1) | collective-permute-done | bytes 524320 | tf_op jit(solution)/shard_map/ppermute | solution.py:120
  72.4 11.3 %collective-permute-done.3 = bf16[1024,256]{0,1:T(8,128)(2,1)} collective-permute-done((bf16[1024,256]{0,1:T(8,128)(2,1)}, bf16[1024,256]{0,1:T(8,128)(2,1)}, u32[]{:S(2)}, u32[]{:S(2)}) %collective-permute-start.3) | collective-permute-done | bytes 524320 | tf_op jit(solution)/shard_map/ppermute | solution.py:120
  100.2 26.8 %collective-permute-done.5 = bf16[1024,256]{0,1:T(8,128)(2,1)} collective-permute-done((bf16[1024,256]{0,1:T(8,128)(2,1)}, bf16[1024,256]{0,1:T(8,128)(2,1)}, u32[]{:S(2)}, u32[]{:S(2)}) %collective-permute-start.5) | collective-permute-done | bytes 524320 | tf_op jit(solution)/shard_map/ppermute | solution.py:120
  163.4 8.6 %collective-permute-done.9 = bf16[1024,256]{0,1:T(8,128)(2,1)S(1)} collective-permute-done((bf16[1024,256]{0,1:T(8,128)(2,1)}, bf16[1024,256]{0,1:T(8,128)(2,1)S(1)}, u32[]{:S(2)}, u32[]{:S(2)}) %collective-permute-start.9) | collective-permute-done | bytes 524320 | tf_op jit(solution)/shard_map/ppermute | solution.py:120
  173.3 9.4 %collective-permute-start.10 = (bf16[1024,256]{0,1:T(8,128)(2,1)S(1)}, bf16[1024,256]{0,1:T(8,128)(2,1)S(1)}, u32[]{:S(2)}, u32[]{:S(2)}) collective-permute-start(bf16[1024,256]{0,1:T(8,128)(2,1)S(1)} %collective-permute-done.8), channel_id=1, source_target_pairs={{2,3},{6,7},{10,11},{14,15},{18,19},{22,23},{26,27},{30,31}} | collective-permute-start | bytes 1572872 | tf_op jit(solution)/shard_map/ppermute | solution.py:119
  190.3 11.0 %multiply_convert_fusion.2 = (bf16[1024,1024]{1,0:T(8,128)(2,1)S(1)}, f32[1024,1024]{1,0:T(8,128)S(1)}, f32[1024,1024]{1,0:T(8,128)S(1)}) fusion(bf16[1024,1024]{1,0:T(8,128)(2,1)S(1)} %copy-done, f32[1024,1024]{1,0:T(8,128)S(1)} %get-tuple-element.581, f32[1024]{0:T(1024)S(1)} %copy-done.111, f32[1024]{0:T(1024)S(1)} %copy-done.100, ...), kind=kOutput, calls=%fused_computation.142 | convolution fusion | flops 2220883968 | bytes 16793600 | tf_op jit(solution)/shard_map/dot_general | solution.py:288
  248.9 8.8 %collective-permute-done.17 = bf16[256,1024]{1,0:T(8,128)(2,1)S(1)} collective-permute-done((bf16[256,1024]{1,0:T(8,128)(2,1)S(1)}, bf16[256,1024]{1,0:T(8,128)(2,1)S(1)}, u32[]{:S(2)}, u32[]{:S(2)}) %collective-permute-start.17) | collective-permute-done | bytes 524320 | tf_op jit(solution)/shard_map/ppermute | solution.py:144
  271.2 8.6 %collective-permute-done.18 = bf16[256,1024]{1,0:T(8,128)(2,1)S(1)} collective-permute-done((bf16[256,1024]{1,0:T(8,128)(2,1)S(1)}, bf16[256,1024]{1,0:T(8,128)(2,1)S(1)}, u32[]{:S(2)}, u32[]{:S(2)}) %collective-permute-start.18) | collective-permute-done | bytes 524320 | tf_op jit(solution)/shard_map/ppermute | solution.py:120
  282.7 13.1 %collective-permute-done.19 = bf16[256,1024]{1,0:T(8,128)(2,1)} collective-permute-done((bf16[256,1024]{1,0:T(8,128)(2,1)S(1)}, bf16[256,1024]{1,0:T(8,128)(2,1)}, u32[]{:S(2)}, u32[]{:S(2)}) %collective-permute-start.19) | collective-permute-done | bytes 524320 | tf_op jit(solution)/shard_map/ppermute | solution.py:120
  303.0 17.4 %all-reduce.6.cloned.1.call-done = (bf16[1024,1024]{1,0:T(8,128)(2,1)}, bf16[1024,1024]{1,0:T(8,128)(2,1)}) async-done(((bf16[1024,1024]{1,0:T(8,128)(2,1)}, bf16[1024,1024]{1,0:T(8,128)(2,1)}), (bf16[1024,1024]{1,0:T(8,128)(2,1)}, bf16[1024,1024]{1,0:T(8,128)(2,1)})) %all-reduce.6.cloned.1.call-update) | async-done | bytes 4194320 | tf_op jit(solution)/shard_map/psum | solution.py:211
  384.3 8.9 %collective-permute-done.27 = bf16[1024,256]{0,1:T(8,128)(2,1)S(1)} collective-permute-done((bf16[1024,256]{0,1:T(8,128)(2,1)}, bf16[1024,256]{0,1:T(8,128)(2,1)S(1)}, u32[]{:S(2)}, u32[]{:S(2)}) %collective-permute-start.27) | collective-permute-done | bytes 524320 | tf_op jit(solution)/shard_map/ppermute | solution.py:120
  398.7 9.4 %collective-permute-done.29 = bf16[1024,256]{0,1:T(8,128)(2,1)S(1)} collective-permute-done((bf16[1024,256]{0,1:T(8,128)(2,1)S(1)}, bf16[1024,256]{0,1:T(8,128)(2,1)S(1)}, u32[]{:S(2)}, u32[]{:S(2)}) %collective-permute-start.29) | collective-permute-done | bytes 524320 | tf_op jit(solution)/shard_map/ppermute | solution.py:120
  425.8 29.0 %while.97 = (s32[]{:T(128)}, f32[1024,4,64]{0,2,1:T(8,128)S(1)}, f32[1024,4,64]{0,2,1:T(8,128)}, bf16[2,512,4,64]{1,3,2,0:T(8,128)(2,1)}, bf16[2,512,4,64]{1,3,2...) while((s32[]{:T(128)}, f32[1024,4,64]{0,2,1:T(8,128)S(1)}, ...), condition=%wide.region_26.27_spmd.clone, body=%wide.region_24.26_spmd.clone.sunk | while | flops 1376124416 | bytes 84998440 | solution.py:103
  480.2 11.2 %collective-permute-done.30 = bf16[256,1024]{1,0:T(8,128)(2,1)S(1)} collective-permute-done((bf16[256,1024]{1,0:T(8,128)(2,1)S(1)}, bf16[256,1024]{1,0:T(8,128)(2,1)S(1)}, u32[]{:S(2)}, u32[]{:S(2)}) %collective-permute-start.30) | collective-permute-done | bytes 524320 | tf_op jit(solution)/shard_map/ppermute | solution.py:141
  496.8 10.3 %collective-permute-done.31 = bf16[256,1024]{1,0:T(8,128)(2,1)} collective-permute-done((bf16[256,1024]{1,0:T(8,128)(2,1)S(1)}, bf16[256,1024]{1,0:T(8,128)(2,1)}, u32[]{:S(2)}, u32[]{:S(2)}) %collective-permute-start.31) | collective-permute-done | bytes 524320 | tf_op jit(solution)/shard_map/ppermute | solution.py:141
  531.8 14.5 %collective-permute-done.35 = bf16[256,1024]{1,0:T(8,128)(2,1)} collective-permute-done((bf16[256,1024]{1,0:T(8,128)(2,1)}, bf16[256,1024]{1,0:T(8,128)(2,1)}, u32[]{:S(2)}, u32[]{:S(2)}) %collective-permute-start.35) | collective-permute-done | bytes 524320 | tf_op jit(solution)/shard_map/ppermute | solution.py:144
  558.9 14.4 %collective-permute-done.39 = bf16[256,1024]{1,0:T(8,128)(2,1)S(1)} collective-permute-done((bf16[256,1024]{1,0:T(8,128)(2,1)S(1)}, bf16[256,1024]{1,0:T(8,128)(2,1)S(1)}, u32[]{:S(2)}, u32[]{:S(2)}) %collective-permute-start.39) | collective-permute-done | bytes 524320 | tf_op jit(solution)/shard_map/ppermute | solution.py:119
  574.0 16.2 %collective-permute-done.36 = bf16[256,1024]{1,0:T(8,128)(2,1)S(1)} collective-permute-done((bf16[256,1024]{1,0:T(8,128)(2,1)S(1)}, bf16[256,1024]{1,0:T(8,128)(2,1)S(1)}, u32[]{:S(2)}, u32[]{:S(2)}) %collective-permute-start.36) | collective-permute-done | bytes 524320 | tf_op jit(solution)/shard_map/ppermute | solution.py:120
  592.2 19.5 %collective-permute-done.37 = bf16[256,1024]{1,0:T(8,128)(2,1)S(1)} collective-permute-done((bf16[256,1024]{1,0:T(8,128)(2,1)S(1)}, bf16[256,1024]{1,0:T(8,128)(2,1)S(1)}, u32[]{:S(2)}, u32[]{:S(2)}) %collective-permute-start.37) | collective-permute-done | bytes 524320 | tf_op jit(solution)/shard_map/ppermute | solution.py:120
  617.0 33.8 %all-reduce.8.cloned.1.call-done = (bf16[1024,1024]{1,0:T(8,128)(2,1)}, bf16[1,128,1024]{2,1,0:T(8,128)(2,1)}) async-done(((bf16[1024,1024]{1,0:T(8,128)(2,1)}, bf16[1,128,1024]{2,1,0:T(8,128)(2,1)}), (bf16[1024,1024]{1,0:T(8,128)(2,1)}, bf16[1,128,1024]{2,1,0:T(8,128)(2,1)})) %all-reduce.8.cloned.1.call-update) | async-done | bytes 2359312 | tf_op jit(solution)/shard_map/psum | solution.py:332
  664.9 21.4 %collective-permute-done.46 = bf16[4128,128]{1,0:T(8,128)(2,1)S(1)} collective-permute-done((bf16[4128,128]{1,0:T(8,128)(2,1)S(1)}, bf16[4128,128]{1,0:T(8,128)(2,1)S(1)}, u32[]{:S(2)}, u32[]{:S(2)}) %collective-permute-start.46) | collective-permute-done | bytes 1056800 | tf_op jit(solution)/shard_map/ppermute | solution.py:196
  686.3 8.3 %maximum_select_fusion.1 = bf16[8256,128]{1,0:T(8,128)(2,1)} fusion(bf16[4128,128]{1,0:T(8,128)(2,1)S(1)} %collective-permute-done.46, bf16[4128,128]{1,0:T(8,128)(2,1)S(1)} %maximum_select_fusion.2, pred[]{:T(512)S(6)} %eq.157), kind=kLoop, calls=%fused_computation.174 | loop fusion | flops 9510912 | bytes 4227073 | tf_op jit(solution)/shard_map/jit(_where)/select_n | solution.py:197
  701.6 14.8 %all-reduce = (bf16[1024]{0:T(1024)(128)(2,1)S(1)}, bf16[1024]{0:T(1024)(128)(2,1)S(1)}) all-reduce(bf16[1024]{0:T(1024)(128)(2,1)S(1)} %get-tuple-element.477, bf16[1024]{0:T(1024)(128)(2,1)S(1)} %add_add_fusion.5), channel_id=1, replica_groups=mesh['dp'=8,'tensor'=4] {'dp'}, use_global_device_ids=true, to_apply=%region_31.32 | all-reduce | flops 2048 | bytes 8192 | tf_op jit(solution)/shard_map/psum | solution.py:211
  (581 shorter events, 430.5 us)
Async XLA Ops:
  7.2 79.6 %all-gather.7.cloned.1.call-start = ((), (), s32[]{:S(2)}) async-start(), calls=%async_computation | async-start | bytes 2621440 | tf_op jit(solution)/shard_map/all_gather | solution.py:265
  8.0 140.5 %all-gather.9.cloned.1.call-start = ((), (), s32[]{:S(2)}) async-start(), calls=%async_computation.1 | async-start | bytes 2621440 | tf_op jit(solution)/shard_map/all_gather | solution.py:266
  41.8 25.9 %collective-permute-start.1 = (bf16[1024,256]{0,1:T(8,128)(2,1)S(1)}, bf16[1024,256]{0,1:T(8,128)(2,1)}, u32[]{:S(2)}, u32[]{:S(2)}) collective-permute-start(bf16[1024,256]{0,1:T(8,128)(2,1)S(1)} %bitcast.465), channel_id=1, source_target_pairs={{1,0},{2,1},{3,2},{5,4},{6,5},{7,6},{9,8},{10,9},{11,10},{13,12},{... | collective-permute-start | bytes 1572872 | tf_op jit(solution)/shard_map/ppermute | solution.py:120
  43.1 25.9 %collective-permute-start = (bf16[1024,256]{0,1:T(8,128)(2,1)S(1)}, bf16[1024,256]{0,1:T(8,128)(2,1)}, u32[]{:S(2)}, u32[]{:S(2)}) collective-permute-start(bf16[1024,256]{0,1:T(8,128)(2,1)S(1)} %bitcast.466), channel_id=1, source_target_pairs={{0,1},{1,2},{2,3},{4,5},{5,6},{6,7},{8,9},{9,10},{10,11},{12,13},{... | collective-permute-start | bytes 1572872 | tf_op jit(solution)/shard_map/ppermute | solution.py:119
  70.6 249.8 %all-reduce.6.cloned.1.call-start = ((), (), s32[]{:S(2)}) async-start(), calls=%async_computation.3 | async-start | bytes 8388608 | tf_op jit(solution)/shard_map/psum | solution.py:211
  83.7 43.3 %collective-permute-start.5 = (bf16[1024,256]{0,1:T(8,128)(2,1)}, bf16[1024,256]{0,1:T(8,128)(2,1)}, u32[]{:S(2)}, u32[]{:S(2)}) collective-permute-start(bf16[1024,256]{0,1:T(8,128)(2,1)} %collective-permute-done.3), channel_id=1, source_target_pairs={{1,0},{5,4},{9,8},{13,12},{17,16},{21,20},{25,24},{29,28}} | collective-permute-start | bytes 1572872 | tf_op jit(solution)/shard_map/ppermute | solution.py:120
  236.7 136.9 %all-gather.11.cloned.1.call-start = ((), (), s32[]{:S(2)}) async-start(), calls=%async_computation.2 | async-start | bytes 2621440 | tf_op jit(solution)/shard_map/all_gather | solution.py:267
  281.0 369.8 %all-reduce.8.cloned.1.call-start = ((), (), s32[]{:S(2)}) async-start(), calls=%async_computation.4 | async-start | bytes 4718592 | tf_op jit(solution)/shard_map/psum | solution.py:332
  281.2 45.9 %collective-permute-start.23 = (bf16[256,1024]{1,0:T(8,128)(2,1)}, bf16[256,1024]{1,0:T(8,128)(2,1)}, u32[]{:S(2)}, u32[]{:S(2)}) collective-permute-start(bf16[256,1024]{1,0:T(8,128)(2,1)} %collective-permute-done.22), channel_id=1, source_target_pairs={{2,3},{6,7},{10,11},{14,15},{18,19},{22,23},{26,27},{30,31}} | collective-permute-start | bytes 1572872 | tf_op jit(solution)/shard_map/ppermute | solution.py:119
  295.9 31.2 %collective-permute-start.20 = (bf16[256,1024]{1,0:T(8,128)(2,1)}, bf16[256,1024]{1,0:T(8,128)(2,1)}, u32[]{:S(2)}, u32[]{:S(2)}) collective-permute-start(bf16[256,1024]{1,0:T(8,128)(2,1)} %collective-permute-done.19), channel_id=1, source_target_pairs={{1,0},{5,4},{9,8},{13,12},{17,16},{21,20},{25,24},{29,28}} | collective-permute-start | bytes 1572872 | tf_op jit(solution)/shard_map/ppermute | solution.py:120
  357.0 20.3 %collective-permute-start.25 = (bf16[1024,256]{0,1:T(8,128)(2,1)}, bf16[1024,256]{0,1:T(8,128)(2,1)}, u32[]{:S(2)}, u32[]{:S(2)}) collective-permute-start(bf16[1024,256]{0,1:T(8,128)(2,1)} %bitcast.131), channel_id=1, source_target_pairs={{1,0},{2,1},{3,2},{5,4},{6,5},{7,6},{9,8},{10,9},{11,10},{13,12},{... | collective-permute-start | bytes 1572872 | tf_op jit(solution)/shard_map/ppermute | solution.py:120
  358.3 20.3 %collective-permute-start.24 = (bf16[1024,256]{0,1:T(8,128)(2,1)}, bf16[1024,256]{0,1:T(8,128)(2,1)}, u32[]{:S(2)}, u32[]{:S(2)}) collective-permute-start(bf16[1024,256]{0,1:T(8,128)(2,1)} %bitcast.131), channel_id=1, source_target_pairs={{0,1},{1,2},{2,3},{4,5},{5,6},{6,7},{8,9},{9,10},{10,11},{12,13},{... | collective-permute-start | bytes 1572872 | tf_op jit(solution)/shard_map/ppermute | solution.py:119
  475.3 34.8 %collective-permute-start.42 = (bf16[8256,128]{1,0:T(8,128)(2,1)}, bf16[8256,128]{1,0:T(8,128)(2,1)}, u32[]{:S(2)}, u32[]{:S(2)}) collective-permute-start(bf16[8256,128]{1,0:T(8,128)(2,1)} %constant_dynamic-slice_fusion.2), channel_id=1, source_target_pairs={{0,4},{4,0},{8,12},{12,8},{16,20},{20,16},{24,28},{28,24},{1,5},{5... | collective-permute-start | bytes 6340616 | tf_op jit(solution)/shard_map/ppermute | solution.py:191
  515.0 40.1 %collective-permute-start.43 = (bf16[4128,128]{1,0:T(8,128)(2,1)}, bf16[4128,128]{1,0:T(8,128)(2,1)}, u32[]{:S(2)}, u32[]{:S(2)}) collective-permute-start(bf16[4128,128]{1,0:T(8,128)(2,1)} %constant_dynamic-slice_fusion.1), channel_id=1, source_target_pairs={{0,8},{4,12},{8,0},{12,4},{16,24},{20,28},{24,16},{28,20},{1,9},{5... | collective-permute-start | bytes 3170312 | tf_op jit(solution)/shard_map/ppermute | solution.py:191
  523.3 22.9 %collective-permute-start.35 = (bf16[256,1024]{1,0:T(8,128)(2,1)}, bf16[256,1024]{1,0:T(8,128)(2,1)}, u32[]{:S(2)}, u32[]{:S(2)}) collective-permute-start(bf16[256,1024]{1,0:T(8,128)(2,1)} %fusion.116), channel_id=1, source_target_pairs={{1,0},{2,1},{3,2},{5,4},{6,5},{7,6},{9,8},{10,9},{11,10},{13,12},{... | collective-permute-start | bytes 1572872 | tf_op jit(solution)/shard_map/ppermute | solution.py:144
  547.7 25.6 %collective-permute-start.39 = (bf16[256,1024]{1,0:T(8,128)(2,1)S(1)}, bf16[256,1024]{1,0:T(8,128)(2,1)S(1)}, u32[]{:S(2)}, u32[]{:S(2)}) collective-permute-start(bf16[256,1024]{1,0:T(8,128)(2,1)S(1)} %fusion.120), channel_id=1, source_target_pairs={{0,1},{1,2},{2,3},{4,5},{5,6},{6,7},{8,9},{9,10},{10,11},{12,13},{... | collective-permute-start | bytes 1572872 | tf_op jit(solution)/shard_map/ppermute | solution.py:119
  553.8 36.4 %collective-permute-start.36 = (bf16[256,1024]{1,0:T(8,128)(2,1)S(1)}, bf16[256,1024]{1,0:T(8,128)(2,1)S(1)}, u32[]{:S(2)}, u32[]{:S(2)}) collective-permute-start(bf16[256,1024]{1,0:T(8,128)(2,1)S(1)} %fusion.120), channel_id=1, source_target_pairs={{1,0},{2,1},{3,2},{5,4},{6,5},{7,6},{9,8},{10,9},{11,10},{13,12},{... | collective-permute-start | bytes 1572872 | tf_op jit(solution)/shard_map/ppermute | solution.py:120
  557.9 55.3 %collective-permute-start.44 = (bf16[2064,128]{1,0:T(8,128)(2,1)}, bf16[2064,128]{1,0:T(8,128)(2,1)}, u32[]{:S(2)}, u32[]{:S(2)}) collective-permute-start(bf16[2064,128]{1,0:T(8,128)(2,1)} %constant_dynamic-slice_fusion), channel_id=1, source_target_pairs={{0,16},{4,20},{8,24},{12,28},{16,0},{20,4},{24,8},{28,12},{1,17},{... | collective-permute-start | bytes 1585160 | tf_op jit(solution)/shard_map/ppermute | solution.py:191
  590.2 21.5 %collective-permute-start.37 = (bf16[256,1024]{1,0:T(8,128)(2,1)S(1)}, bf16[256,1024]{1,0:T(8,128)(2,1)S(1)}, u32[]{:S(2)}, u32[]{:S(2)}) collective-permute-start(bf16[256,1024]{1,0:T(8,128)(2,1)S(1)} %collective-permute-done.36), channel_id=1, source_target_pairs={{1,0},{2,1},{5,4},{6,5},{9,8},{10,9},{13,12},{14,13},{17,16},{18,1... | collective-permute-start | bytes 1572872 | tf_op jit(solution)/shard_map/ppermute | solution.py:120
  591.5 65.1 %collective-permute-start.41 = (bf16[256,1024]{1,0:T(8,128)(2,1)S(1)}, bf16[256,1024]{1,0:T(8,128)(2,1)S(1)}, u32[]{:S(2)}, u32[]{:S(2)}) collective-permute-start(bf16[256,1024]{1,0:T(8,128)(2,1)S(1)} %collective-permute-done.40), channel_id=1, source_target_pairs={{2,3},{6,7},{10,11},{14,15},{18,19},{22,23},{26,27},{30,31}} | collective-permute-start | bytes 1572872 | tf_op jit(solution)/shard_map/ppermute | solution.py:119
  611.7 45.7 %collective-permute-start.38 = (bf16[256,1024]{1,0:T(8,128)(2,1)S(1)}, bf16[256,1024]{1,0:T(8,128)(2,1)}, u32[]{:S(2)}, u32[]{:S(2)}) collective-permute-start(bf16[256,1024]{1,0:T(8,128)(2,1)S(1)} %collective-permute-done.37), channel_id=1, source_target_pairs={{1,0},{5,4},{9,8},{13,12},{17,16},{21,20},{25,24},{29,28}} | collective-permute-start | bytes 1572872 | tf_op jit(solution)/shard_map/ppermute | solution.py:120
  615.4 43.8 %collective-permute-start.45 = (bf16[2064,128]{1,0:T(8,128)(2,1)}, bf16[2064,128]{1,0:T(8,128)(2,1)}, u32[]{:S(2)}, u32[]{:S(2)}) collective-permute-start(bf16[2064,128]{1,0:T(8,128)(2,1)} %add_convert_fusion.6), channel_id=1, source_target_pairs={{0,16},{4,20},{8,24},{12,28},{16,0},{20,4},{24,8},{28,12},{1,17},{... | collective-permute-start | bytes 1585160 | tf_op jit(solution)/shard_map/ppermute | solution.py:196
  661.0 25.3 %collective-permute-start.46 = (bf16[4128,128]{1,0:T(8,128)(2,1)S(1)}, bf16[4128,128]{1,0:T(8,128)(2,1)S(1)}, u32[]{:S(2)}, u32[]{:S(2)}) collective-permute-start(bf16[4128,128]{1,0:T(8,128)(2,1)S(1)} %maximum_select_fusion.2), channel_id=1, source_target_pairs={{0,8},{4,12},{8,0},{12,4},{16,24},{20,28},{24,16},{28,20},{1,9},{5... | collective-permute-start | bytes 3170312 | tf_op jit(solution)/shard_map/ppermute | solution.py:196
  694.6 29.1 %collective-permute-start.47 = (bf16[8256,128]{1,0:T(8,128)(2,1)}, bf16[8256,128]{1,0:T(8,128)(2,1)}, u32[]{:S(2)}, u32[]{:S(2)}) collective-permute-start(bf16[8256,128]{1,0:T(8,128)(2,1)} %maximum_select_fusion.1), channel_id=1, source_target_pairs={{0,4},{4,0},{8,12},{12,8},{16,20},{20,16},{24,28},{28,24},{1,5},{5... | collective-permute-start | bytes 6340616 | tf_op jit(solution)/shard_map/ppermute | solution.py:196
  (155 other events, 1890.4 us)
Sparse Core Ops, SparseCore 0:
  9.6 51.8 all-gather.6
  70.7 59.7 all-gather.8
  236.8 83.5 all-reduce.5
  321.8 48.6 all-gather.10
  526.0 124.7 all-reduce.7

commit v9 on v7

--- a/solution.py
+++ b/solution.py
@@ -61,8 +61,25 @@
         result = jnp.einsum("hbk,khe->bhe", probs_low, values, preferred_element_type=jnp.float32)
         return (result.astype(jnp.bfloat16), row_max[..., 0] + jnp.log(row_sum[..., 0]))
 
-    result, log_total = lax.map(one_block, (portions, offsets))
-    return (result.reshape(row_count, head_count, head_size), log_total)
+    if not causal:
+        result, log_total = lax.map(one_block, (portions, offsets))
+        return (result.reshape(row_count, head_count, head_size), log_total)
+    results, totals = [], []
+    for index in range(row_count // block_len):
+        key_end = (index + 1) * block_len
+        scores = masked_scores(
+            portions[index], index * block_len, key_rows[:key_end], key_limit, causal, score_scale
+        )
+        row_max = jnp.max(scores, axis=-1, keepdims=True)
+        unnormed = jnp.exp(scores - row_max)
+        row_sum = jnp.sum(unnormed, axis=-1, keepdims=True)
+        probs_low = (unnormed / row_sum).astype(jnp.bfloat16)
+        result = jnp.einsum(
+            "hbk,khe->bhe", probs_low, values[:key_end], preferred_element_type=jnp.float32
+        )
+        results.append(result.astype(jnp.bfloat16))
+        totals.append(row_max[..., 0] + jnp.log(row_sum[..., 0]))
+    return (jnp.concatenate(results).reshape(row_count, head_count, head_size), jnp.stack(totals))
 
 
 def attend_back(queries, key_rows, values, log_total, out_grad, key_limit, causal, score_scale):
@@ -100,9 +117,35 @@
         return ((key_grad, value_grad), query_grad)
 
     empty = jnp.zeros(key_rows.shape, jnp.float32)
-    (key_grad, value_grad), query_grad = lax.scan(
-        one_block, (empty, empty), (portions, grad_parts, log_total, offsets)
-    )
+    if not causal:
+        (key_grad, value_grad), query_grad = lax.scan(
+            one_block, (empty, empty), (portions, grad_parts, log_total, offsets)
+        )
+        return (query_grad.reshape(row_count, head_count, head_size), key_grad, value_grad)
+    key_grad, value_grad, query_grads = empty, empty, []
+    for index in range(row_count // block_len):
+        key_end = (index + 1) * block_len
+        portion, grad_part = portions[index], grad_parts[index]
+        keys, vals = key_rows[:key_end], values[:key_end]
+        scores = masked_scores(portion, index * block_len, keys, key_limit, causal, score_scale)
+        probs = jnp.exp(scores - log_total[index][..., None])
+        probs_grad = jnp.einsum("bhe,khe->hbk", grad_part, vals, preferred_element_type=jnp.float32)
+        row_dot = jnp.sum(probs * probs_grad, axis=-1, keepdims=True)
+        scores_grad = (probs * (probs_grad - row_dot)).astype(jnp.bfloat16)
+        value_part = jnp.einsum(
+            "hbk,bhe->khe", probs.astype(jnp.bfloat16), grad_part, preferred_element_type=jnp.float32
+        )
+        key_part = (
+            jnp.einsum("hbk,bhe->khe", scores_grad, portion, preferred_element_type=jnp.float32)
+            * score_scale
+        )
+        value_grad = value_grad.at[:key_end].add(value_part)
+        key_grad = key_grad.at[:key_end].add(key_part)
+        query_grads.append(
+            jnp.einsum("hbk,khe->bhe", scores_grad, keys, preferred_element_type=jnp.float32)
+            * score_scale
+        )
+    query_grad = jnp.concatenate(query_grads)
     return (query_grad.reshape(row_count, head_count, head_size), key_grad, value_grad)
 
 

time: 691 us -> 684 us (0.990)
  waiting for transfers between devices: 291 us -> 307 us
  local copies, waits for them, and re-layouts: 51.3 us -> 40.1 us
  matrix products: 117 us -> 106 us
    dot_general x0 -> x10, matrix products: none -> 14.3 us  [the longest x2 5.31 us: attend_back(): jnp.einsum('bhe,khe->hbk', grad_part, vals, preferred_element_type=jnp.fl...]
    ppermute x15, waiting for transfers between devices: 162 us -> 170 us  [relay_pieces(): lax.ppermute(from_right, axis, [(i, i - 1) for i in range(1, count - k +...]
    convert_element_type x0 -> x2, other arithmetic: none -> 8.39 us  [attend_back(): scores_grad = (probs * (probs_grad - row_dot)).astype(jnp.bfloat16)]
    unnamed x201 -> x221, local copies, waits for them, and re-layouts: 20.7 us -> 23.1 us
  transfers between devices with their start and end apart: 48 -> 48, of which waited for: 24 -> 24; matrix products, arithmetic and copies ran while one was open for 31% -> 27% of each run, Pallas kernels for 0% -> 0%
where the time goes in v9:
time: 684 us; the launch traced here: 675 us
  waiting for transfers between devices  307 us (45%)
  matrix products  106 us (15%)
  other arithmetic  97.3 us (14%)
  starting transfers between devices  93.7 us (14%)
  local copies, waits for them, and re-layouts  40.1 us (6%)
  between operations  17.4 us (3%)
  blocking collectives  12.8 us (2%)
    ppermute x15, waiting for transfers between devices, relay_pieces(): lax.ppermute(from_right, axis, [(i, i - 1) for i in range(1, count - k +...  170 us
    ppermute x15, starting transfers between devices, relay_pieces(): lax.ppermute(from_left, axis, [(i, i + 1) for i in range(k - 1, count - 1)])  42.2 us
    psum x1, waiting for transfers between devices, stacked_psum(): lax.psum(jnp.concatenate([matrix, extra]).astype(jnp.bfloat16), axis)  40.4 us
    ppermute x6, waiting for transfers between devices, relay_scatter(): lax.ppermute(send_right.astype(value.dtype), axis, [(i, i + 1) for i in r...  36.5 us
    dot_general x21, matrix products, gathered_sum(): jnp.einsum(spec, piece, weight, preferred_element_type=jnp.float32)  32.4 us
    all_gather x1, waiting for transfers between devices, local(): cross_query_all = lax.all_gather(cross_query, 'tensor')  30.8 us
    ppermute x6, starting transfers between devices, relay_scatter(): lax.ppermute(send_right.astype(value.dtype), axis, [(i, i + 1) for i in r...  26 us
    reduce_sum x14, other arithmetic, layer_norm(): return centred * lax.rsqrt(spread + EPSILON) * norm_gain + norm_bias  25.5 us
  transfers between devices with their start and end apart: 48, of which 24 were waited for; matrix products, arithmetic and copies ran while one was open for 27% of the time, Pallas kernels for 0%

profile of v9, /device:TPU:0, one launch (start us, length us, event | category | flops | bytes accessed | tf_op | source)
XLA Modules:
  0.0 674.7 jit_solution(9569079021168705691)
XLA Ops:
  27.4 6.4 collective-permute-start
  33.9 32.8 %collective-permute-done.1 = bf16[1024,256]{0,1:T(8,128)(2,1)} collective-permute-done((bf16[1024,256]{0,1:T(8,128)(2,1)S(1)}, bf16[1024,256]{0,1:T(8,128)(2,1)}, u32[]{:S(2)}, u32[]{:S(2)}) %collective-permute-start.1) | collective-permute-done | bytes 524320 | tf_op jit(solution)/shard_map/ppermute | solution.py:163
  71.3 11.5 %collective-permute-done.3 = bf16[1024,256]{0,1:T(8,128)(2,1)} collective-permute-done((bf16[1024,256]{0,1:T(8,128)(2,1)}, bf16[1024,256]{0,1:T(8,128)(2,1)}, u32[]{:S(2)}, u32[]{:S(2)}) %collective-permute-start.3) | collective-permute-done | bytes 524320 | tf_op jit(solution)/shard_map/ppermute | solution.py:163
  97.2 28.4 %collective-permute-done.5 = bf16[1024,256]{0,1:T(8,128)(2,1)} collective-permute-done((bf16[1024,256]{0,1:T(8,128)(2,1)}, bf16[1024,256]{0,1:T(8,128)(2,1)}, u32[]{:S(2)}, u32[]{:S(2)}) %collective-permute-start.5) | collective-permute-done | bytes 524320 | tf_op jit(solution)/shard_map/ppermute | solution.py:163
  152.5 6.9 %collective-permute-done.7 = bf16[1024,256]{0,1:T(8,128)(2,1)} collective-permute-done((bf16[1024,256]{0,1:T(8,128)(2,1)S(1)}, bf16[1024,256]{0,1:T(8,128)(2,1)}, u32[]{:S(2)}, u32[]{:S(2)}) %collective-permute-start.7) | collective-permute-done | bytes 524320 | tf_op jit(solution)/shard_map/ppermute | solution.py:163
  166.2 8.0 %collective-permute-done.9 = bf16[1024,256]{0,1:T(8,128)(2,1)S(1)} collective-permute-done((bf16[1024,256]{0,1:T(8,128)(2,1)}, bf16[1024,256]{0,1:T(8,128)(2,1)S(1)}, u32[]{:S(2)}, u32[]{:S(2)}) %collective-permute-start.9) | collective-permute-done | bytes 524320 | tf_op jit(solution)/shard_map/ppermute | solution.py:163
  175.6 9.4 %collective-permute-start.10 = (bf16[1024,256]{0,1:T(8,128)(2,1)S(1)}, bf16[1024,256]{0,1:T(8,128)(2,1)S(1)}, u32[]{:S(2)}, u32[]{:S(2)}) collective-permute-start(bf16[1024,256]{0,1:T(8,128)(2,1)S(1)} %collective-permute-done.8), channel_id=1, source_target_pairs={{2,3},{6,7},{10,11},{14,15},{18,19},{22,23},{26,27},{30,31}} | collective-permute-start | bytes 1572872 | tf_op jit(solution)/shard_map/ppermute | solution.py:162
  192.6 11.0 %multiply_convert_fusion.3 = (bf16[1024,1024]{1,0:T(8,128)(2,1)S(1)}, f32[1024,1024]{1,0:T(8,128)S(1)}, f32[1024,1024]{1,0:T(8,128)S(1)}) fusion(bf16[1024,1024]{1,0:T(8,128)(2,1)S(1)} %copy-done, f32[1024,1024]{1,0:T(8,128)S(1)} %get-tuple-element.483, f32[1024]{0:T(1024)S(1)} %copy-done.104, f32[1024]{0:T(1024)S(1)} %copy-done.92, f32[1024]{0:T(1024)S(1)} %fusion.199, ...), kind=kOutput, calls=%fused_computation.98 | convolution fusion | flops 2220883968 | bytes 16793600 | tf_op jit(solution)/shard_map/dot_general | solution.py:296
  215.1 8.3 %collective-permute-done.12 = bf16[256,1024]{1,0:T(8,128)(2,1)S(1)} collective-permute-done((bf16[256,1024]{1,0:T(8,128)(2,1)S(1)}, bf16[256,1024]{1,0:T(8,128)(2,1)S(1)}, u32[]{:S(2)}, u32[]{:S(2)}) %collective-permute-start.12) | collective-permute-done | bytes 524320 | tf_op jit(solution)/shard_map/ppermute | solution.py:184
  254.9 6.5 collective-permute-done.17
  273.0 6.3 collective-permute-done.18
  282.2 11.5 %collective-permute-done.19 = bf16[256,1024]{1,0:T(8,128)(2,1)S(1)} collective-permute-done((bf16[256,1024]{1,0:T(8,128)(2,1)S(1)}, bf16[256,1024]{1,0:T(8,128)(2,1)S(1)}, u32[]{:S(2)}, u32[]{:S(2)}) %collective-permute-start.19) | collective-permute-done | bytes 524320 | tf_op jit(solution)/shard_map/ppermute | solution.py:163
  323.1 8.3 %while.67 = (s32[]{:T(128)}, f32[128,4,64]{0,2,1:T(8,128)S(1)}, f32[128,4,64]{0,2,1:T(8,128)S(1)}, bf16[2,512,4,64]{1,3,2,0:T(8,128)(2,1)}, bf16[2,512,4,64]{1,3...) while((s32[]{:T(128)}, f32[128,4,64]{0,2,1:T(8,128)S(1)}, ...), condition=%wide.region_18.19_spmd.clone, body=%wide.region_16.18_spmd.clone.sunk | while | flops 170424448 | bytes 14394204 | solution.py:121
  346.7 30.8 %all-gather.11.cloned.1.call-done = bf16[4096,256]{1,0:T(8,128)(2,1)} async-done(((bf16[1024,256]{1,0:T(8,128)(2,1)}), bf16[4096,256]{1,0:T(8,128)(2,1)}) %all-gather.11.cloned.1.call-update) | async-done | bytes 2097168 | tf_op jit(solution)/shard_map/all_gather | solution.py:275
  390.9 23.2 %collective-permute-done.27 = bf16[1024,256]{0,1:T(8,128)(2,1)S(1)} collective-permute-done((bf16[1024,256]{0,1:T(8,128)(2,1)}, bf16[1024,256]{0,1:T(8,128)(2,1)S(1)}, u32[]{:S(2)}, u32[]{:S(2)}) %collective-permute-start.27) | collective-permute-done | bytes 524320 | tf_op jit(solution)/shard_map/ppermute | solution.py:163
  419.9 27.6 %collective-permute-done.29 = bf16[1024,256]{0,1:T(8,128)(2,1)S(1)} collective-permute-done((bf16[1024,256]{0,1:T(8,128)(2,1)S(1)}, bf16[1024,256]{0,1:T(8,128)(2,1)S(1)}, u32[]{:S(2)}, u32[]{:S(2)}) %collective-permute-start.29) | collective-permute-done | bytes 524320 | tf_op jit(solution)/shard_map/ppermute | solution.py:163
  472.9 7.2 %multiply_convert_fusion.1 = bf16[4,512,1024]{2,1,0:T(8,128)(2,1)S(1)} fusion(f32[4,512,1024]{2,1,0:T(8,128)} %get-tuple-element.518, f32[4,512,1024]{2,1,0:T(8,128)} %copy-done.2, f32[4,512]{1,0:T(4,128)S(1)} %get-tuple-element.517, f32[4,512]{1,0:T(4,128)S(1)} %log_add_fusion), kind=kLoop, calls=%fused_computation.43 | loop fusion | flops 8388608 | bytes 20987904 | tf_op jit(solution)/shard_map/while/body/eval_jaxpr/convert_element_type | solution.py:134
  491.3 8.6 %collective-permute-done.30 = bf16[256,1024]{1,0:T(8,128)(2,1)S(1)} collective-permute-done((bf16[256,1024]{1,0:T(8,128)(2,1)S(1)}, bf16[256,1024]{1,0:T(8,128)(2,1)S(1)}, u32[]{:S(2)}, u32[]{:S(2)}) %collective-permute-start.30) | collective-permute-done | bytes 524320 | tf_op jit(solution)/shard_map/ppermute | solution.py:184
  507.6 7.0 %collective-permute-done.31 = bf16[256,1024]{1,0:T(8,128)(2,1)S(1)} collective-permute-done((bf16[256,1024]{1,0:T(8,128)(2,1)S(1)}, bf16[256,1024]{1,0:T(8,128)(2,1)S(1)}, u32[]{:S(2)}, u32[]{:S(2)}) %collective-permute-start.31) | collective-permute-done | bytes 524320 | tf_op jit(solution)/shard_map/ppermute | solution.py:184
  534.9 9.7 %collective-permute-done.35 = bf16[256,1024]{1,0:T(8,128)(2,1)} collective-permute-done((bf16[256,1024]{1,0:T(8,128)(2,1)}, bf16[256,1024]{1,0:T(8,128)(2,1)}, u32[]{:S(2)}, u32[]{:S(2)}) %collective-permute-start.35) | collective-permute-done | bytes 524320 | tf_op jit(solution)/shard_map/ppermute | solution.py:187
  566.1 7.5 %collective-permute-done.37 = bf16[256,1024]{1,0:T(8,128)(2,1)} collective-permute-done((bf16[256,1024]{1,0:T(8,128)(2,1)}, bf16[256,1024]{1,0:T(8,128)(2,1)}, u32[]{:S(2)}, u32[]{:S(2)}) %collective-permute-start.37) | collective-permute-done | bytes 524320 | tf_op jit(solution)/shard_map/ppermute | solution.py:163
  579.9 40.4 %all-reduce.10.cloned.1.call-done = (bf16[272,1024]{1,0:T(8,128)(2,1)}, bf16[3,1024,256]{1,2,0:T(8,128)(2,1)}, bf16[2,1024,256]{1,2,0:T(8,128)(2,1)}, bf16[256,1024]{1,0:T(8,128)(2,1)}, bf16[1024,256]{1,0:T(8,128)(2,1)}) async-done(((bf16[272,1024]{1,0:T(8,128)(2,1)}, bf16[3,1024,256]{1,2,0:T(8,128)(2,1)}, bf16[2,1024,256]{1,2,0:T(8,128)(2,1)}, bf16[256,1024]{1,0:T(8,128)(2,1)}, ...) | async-done | bytes 4227088 | tf_op jit(solution)/shard_map/psum | solution.py:212
  647.1 12.8 %all-reduce.2 = (bf16[1024]{0:T(1024)(128)(2,1)S(1)}, bf16[1024]{0:T(1024)(128)(2,1)S(1)}) all-reduce(bf16[1024]{0:T(1024)(128)(2,1)S(1)} %get-tuple-element.412, bf16[1024]{0:T(1024)(128)(2,1)S(1)} %add_add_fusion.6), channel_id=1, replica_groups=mesh['dp'=8,'tensor'=4] {'dp'}, use_global_device_ids=true, to_apply=%region_30.31 | all-reduce | flops 2048 | bytes 8192 | tf_op jit(solution)/shard_map/psum | solution.py:219
  661.0 6.6 add_bitcast_fusion
  (496 shorter events, 334.2 us)
Async XLA Ops:
  7.2 77.8 %all-gather.7.cloned.1.call-start = ((), (), s32[]{:S(2)}) async-start(), calls=%async_computation | async-start | bytes 2621440 | tf_op jit(solution)/shard_map/all_gather | solution.py:273
  8.0 142.6 %all-gather.9.cloned.1.call-start = ((), (), s32[]{:S(2)}) async-start(), calls=%async_computation.1 | async-start | bytes 2621440 | tf_op jit(solution)/shard_map/all_gather | solution.py:274
  26.1 40.5 %collective-permute-start.1 = (bf16[1024,256]{0,1:T(8,128)(2,1)S(1)}, bf16[1024,256]{0,1:T(8,128)(2,1)}, u32[]{:S(2)}, u32[]{:S(2)}) collective-permute-start(bf16[1024,256]{0,1:T(8,128)(2,1)S(1)} %bitcast.398), channel_id=1, source_target_pairs={{1,0},{2,1},{3,2},{5,4},{6,5},{7,6},{9,8},{10,9},{11,10},{13,12},{... | collective-permute-start | bytes 1572872 | tf_op jit(solution)/shard_map/ppermute | solution.py:163
  27.4 40.5 %collective-permute-start = (bf16[1024,256]{0,1:T(8,128)(2,1)S(1)}, bf16[1024,256]{0,1:T(8,128)(2,1)}, u32[]{:S(2)}, u32[]{:S(2)}) collective-permute-start(bf16[1024,256]{0,1:T(8,128)(2,1)S(1)} %bitcast.399), channel_id=1, source_target_pairs={{0,1},{1,2},{2,3},{4,5},{5,6},{6,7},{8,9},{9,10},{10,11},{12,13},{... | collective-permute-start | bytes 1572872 | tf_op jit(solution)/shard_map/ppermute | solution.py:162
  66.7 16.1 %collective-permute-start.3 = (bf16[1024,256]{0,1:T(8,128)(2,1)}, bf16[1024,256]{0,1:T(8,128)(2,1)}, u32[]{:S(2)}, u32[]{:S(2)}) collective-permute-start(bf16[1024,256]{0,1:T(8,128)(2,1)} %collective-permute-done.1), channel_id=1, source_target_pairs={{1,0},{2,1},{5,4},{6,5},{9,8},{10,9},{13,12},{14,13},{17,16},{18,1... | collective-permute-start | bytes 1572872 | tf_op jit(solution)/shard_map/ppermute | solution.py:163
  68.0 16.1 %collective-permute-start.2 = (bf16[1024,256]{0,1:T(8,128)(2,1)}, bf16[1024,256]{0,1:T(8,128)(2,1)}, u32[]{:S(2)}, u32[]{:S(2)}) collective-permute-start(bf16[1024,256]{0,1:T(8,128)(2,1)} %collective-permute-done), channel_id=1, source_target_pairs={{1,2},{2,3},{5,6},{6,7},{9,10},{10,11},{13,14},{14,15},{17,18},{18... | collective-permute-start | bytes 1572872 | tf_op jit(solution)/shard_map/ppermute | solution.py:162
  69.5 270.2 %all-reduce.12.cloned.1.call-start = ((), (), s32[]{:S(2)}) async-start(), calls=%async_computation.4 | async-start | bytes 8388608 | tf_op jit(solution)/shard_map/psum | solution.py:219
  82.8 42.9 %collective-permute-start.5 = (bf16[1024,256]{0,1:T(8,128)(2,1)}, bf16[1024,256]{0,1:T(8,128)(2,1)}, u32[]{:S(2)}, u32[]{:S(2)}) collective-permute-start(bf16[1024,256]{0,1:T(8,128)(2,1)} %collective-permute-done.3), channel_id=1, source_target_pairs={{1,0},{5,4},{9,8},{13,12},{17,16},{21,20},{25,24},{29,28}} | collective-permute-start | bytes 1572872 | tf_op jit(solution)/shard_map/ppermute | solution.py:163
  143.9 15.5 %collective-permute-start.7 = (bf16[1024,256]{0,1:T(8,128)(2,1)S(1)}, bf16[1024,256]{0,1:T(8,128)(2,1)}, u32[]{:S(2)}, u32[]{:S(2)}) collective-permute-start(bf16[1024,256]{0,1:T(8,128)(2,1)S(1)} %bitcast.439), channel_id=1, source_target_pairs={{1,0},{2,1},{3,2},{5,4},{6,5},{7,6},{9,8},{10,9},{11,10},{13,12},{... | collective-permute-start | bytes 1572872 | tf_op jit(solution)/shard_map/ppermute | solution.py:163
  145.2 15.5 %collective-permute-start.6 = (bf16[1024,256]{0,1:T(8,128)(2,1)S(1)}, bf16[1024,256]{0,1:T(8,128)(2,1)}, u32[]{:S(2)}, u32[]{:S(2)}) collective-permute-start(bf16[1024,256]{0,1:T(8,128)(2,1)S(1)} %bitcast.440), channel_id=1, source_target_pairs={{0,1},{1,2},{2,3},{4,5},{5,6},{6,7},{8,9},{9,10},{10,11},{12,13},{... | collective-permute-start | bytes 1572872 | tf_op jit(solution)/shard_map/ppermute | solution.py:162
  214.4 18.3 %collective-permute-start.15 = (bf16[256,1024]{1,0:T(8,128)(2,1)S(1)}, bf16[256,1024]{1,0:T(8,128)(2,1)S(1)}, u32[]{:S(2)}, u32[]{:S(2)}) collective-permute-start(bf16[256,1024]{1,0:T(8,128)(2,1)S(1)} %get-tuple-element.497), channel_id=1, source_target_pairs={{3,2},{7,6},{11,10},{15,14},{19,18},{23,22},{27,26},{31,30}} | collective-permute-start | bytes 1572872 | tf_op jit(solution)/shard_map/ppermute | solution.py:187
  242.1 135.4 %all-gather.11.cloned.1.call-start = ((), (), s32[]{:S(2)}) async-start(), calls=%async_computation.2 | async-start | bytes 2621440 | tf_op jit(solution)/shard_map/all_gather | solution.py:275
  280.6 282.2 %all-reduce.14.cloned.1.call-start = ((), (), s32[]{:S(2)}) async-start(), calls=%async_computation.5 | async-start | bytes 4718592 | tf_op jit(solution)/shard_map/psum | solution.py:340
  281.5 19.3 %collective-permute-start.23 = (bf16[256,1024]{1,0:T(8,128)(2,1)S(1)}, bf16[256,1024]{1,0:T(8,128)(2,1)S(1)}, u32[]{:S(2)}, u32[]{:S(2)}) collective-permute-start(bf16[256,1024]{1,0:T(8,128)(2,1)S(1)} %collective-permute-done.22), channel_id=1, source_target_pairs={{2,3},{6,7},{10,11},{14,15},{18,19},{22,23},{26,27},{30,31}} | collective-permute-start | bytes 1572872 | tf_op jit(solution)/shard_map/ppermute | solution.py:162
  333.1 49.6 %collective-permute-start.25 = (bf16[1024,256]{0,1:T(8,128)(2,1)S(1)}, bf16[1024,256]{0,1:T(8,128)(2,1)}, u32[]{:S(2)}, u32[]{:S(2)}) collective-permute-start(bf16[1024,256]{0,1:T(8,128)(2,1)S(1)} %bitcast.435), channel_id=1, source_target_pairs={{1,0},{2,1},{3,2},{5,4},{6,5},{7,6},{9,8},{10,9},{11,10},{13,12},{... | collective-permute-start | bytes 1572872 | tf_op jit(solution)/shard_map/ppermute | solution.py:163
  334.4 49.8 %collective-permute-start.24 = (bf16[1024,256]{0,1:T(8,128)(2,1)S(1)}, bf16[1024,256]{0,1:T(8,128)(2,1)S(1)}, u32[]{:S(2)}, u32[]{:S(2)}) collective-permute-start(bf16[1024,256]{0,1:T(8,128)(2,1)S(1)} %bitcast.436), channel_id=1, source_target_pairs={{0,1},{1,2},{2,3},{4,5},{5,6},{6,7},{8,9},{9,10},{10,11},{12,13},{... | collective-permute-start | bytes 1572872 | tf_op jit(solution)/shard_map/ppermute | solution.py:162
  382.6 237.7 %all-reduce.10.cloned.1.call-start = ((), (), s32[]{:S(2)}) async-start(), calls=%async_computation.3 | async-start | bytes 8454144 | tf_op jit(solution)/shard_map/psum | solution.py:212
  382.7 31.4 %collective-permute-start.27 = (bf16[1024,256]{0,1:T(8,128)(2,1)}, bf16[1024,256]{0,1:T(8,128)(2,1)S(1)}, u32[]{:S(2)}, u32[]{:S(2)}) collective-permute-start(bf16[1024,256]{0,1:T(8,128)(2,1)} %collective-permute-done.25), channel_id=1, source_target_pairs={{1,0},{2,1},{5,4},{6,5},{9,8},{10,9},{13,12},{14,13},{17,16},{18,1... | collective-permute-start | bytes 1572872 | tf_op jit(solution)/shard_map/ppermute | solution.py:163
  384.1 31.6 %collective-permute-start.26 = (bf16[1024,256]{0,1:T(8,128)(2,1)S(1)}, bf16[1024,256]{0,1:T(8,128)(2,1)S(1)}, u32[]{:S(2)}, u32[]{:S(2)}) collective-permute-start(bf16[1024,256]{0,1:T(8,128)(2,1)S(1)} %collective-permute-done.24), channel_id=1, source_target_pairs={{1,2},{2,3},{5,6},{6,7},{9,10},{10,11},{13,14},{14,15},{17,18},{18... | collective-permute-start | bytes 1572872 | tf_op jit(solution)/shard_map/ppermute | solution.py:162
  414.1 33.4 %collective-permute-start.29 = (bf16[1024,256]{0,1:T(8,128)(2,1)S(1)}, bf16[1024,256]{0,1:T(8,128)(2,1)S(1)}, u32[]{:S(2)}, u32[]{:S(2)}) collective-permute-start(bf16[1024,256]{0,1:T(8,128)(2,1)S(1)} %collective-permute-done.27), channel_id=1, source_target_pairs={{1,0},{5,4},{9,8},{13,12},{17,16},{21,20},{25,24},{29,28}} | collective-permute-start | bytes 1572872 | tf_op jit(solution)/shard_map/ppermute | solution.py:163
  490.6 17.0 %collective-permute-start.33 = (bf16[256,1024]{1,0:T(8,128)(2,1)S(1)}, bf16[256,1024]{1,0:T(8,128)(2,1)S(1)}, u32[]{:S(2)}, u32[]{:S(2)}) collective-permute-start(bf16[256,1024]{1,0:T(8,128)(2,1)S(1)} %get-tuple-element.493), channel_id=1, source_target_pairs={{3,2},{7,6},{11,10},{15,14},{19,18},{23,22},{27,26},{31,30}} | collective-permute-start | bytes 1572872 | tf_op jit(solution)/shard_map/ppermute | solution.py:187
  526.4 18.2 %collective-permute-start.35 = (bf16[256,1024]{1,0:T(8,128)(2,1)}, bf16[256,1024]{1,0:T(8,128)(2,1)}, u32[]{:S(2)}, u32[]{:S(2)}) collective-permute-start(bf16[256,1024]{1,0:T(8,128)(2,1)} %fusion.109), channel_id=1, source_target_pairs={{1,0},{2,1},{3,2},{5,4},{6,5},{7,6},{9,8},{10,9},{11,10},{13,12},{... | collective-permute-start | bytes 1572872 | tf_op jit(solution)/shard_map/ppermute | solution.py:187
  564.6 69.4 %collective-permute-start.41 = (bf16[256,1024]{1,0:T(8,128)(2,1)}, bf16[256,1024]{1,0:T(8,128)(2,1)}, u32[]{:S(2)}, u32[]{:S(2)}) collective-permute-start(bf16[256,1024]{1,0:T(8,128)(2,1)} %collective-permute-done.40), channel_id=1, source_target_pairs={{2,3},{6,7},{10,11},{14,15},{18,19},{22,23},{26,27},{30,31}} | collective-permute-start | bytes 1572872 | tf_op jit(solution)/shard_map/ppermute | solution.py:162
  573.6 60.4 %collective-permute-start.38 = (bf16[256,1024]{1,0:T(8,128)(2,1)}, bf16[256,1024]{1,0:T(8,128)(2,1)}, u32[]{:S(2)}, u32[]{:S(2)}) collective-permute-start(bf16[256,1024]{1,0:T(8,128)(2,1)} %collective-permute-done.37), channel_id=1, source_target_pairs={{1,0},{5,4},{9,8},{13,12},{17,16},{21,20},{25,24},{29,28}} | collective-permute-start | bytes 1572872 | tf_op jit(solution)/shard_map/ppermute | solution.py:163
  (136 other events, 1303.4 us)
Sparse Core Ops, SparseCore 0:
  9.6 59.6 all-gather.6
  70.8 57.8 all-gather.8
  242.2 83.6 all-reduce.11
  327.3 50.1 all-gather.10
  382.7 107.4 all-reduce.13
  532.1 88.2 all-reduce.9
